TPU v7x, 512 devices: a whole 4x8x8 slice. The times are simulated.
512 devices in a mesh: dp: 64 (over x, y, core), mp: 8 (over z).
Axes of the slice: x: 4, y: 8, z: 8, core: 2. Of those that a mesh axis runs over, the one named last changes fastest.
Arguments:
- corpus: bfloat16 [8192, 16, 320], P('dp'), may hold values from -6 to 6
- picks: int32 [64, 64], P('dp'), may hold values from 0 to 127
- lengths: int32 [8192], P('dp'), may hold values from 1 to 16, 98304 in all
- langs: int32 [8192], P('dp'), may hold values from 0 to 127
- w_in: bfloat16 [320, 1536], P(None, 'mp'), may hold values from -0.3125 to 0.3125
- lang_table: bfloat16 [128, 1536], P(None, 'mp'), may hold values from -3 to 3
- ln_gain: float32 [1536], P('mp'), may hold values from 0.1 to 1.9
- w_pw1: bfloat16 [1536, 2, 1536], P('dp', None, 'mp'), may hold values from -0.15625 to 0.15625
- kernel: float32 [31, 1536], P(None, 'mp'), may hold values from -1.5 to 1.5
- bn_gain: float32 [1536], P('mp'), may hold values from 0.1 to 1.9
- bn_bias: float32 [1536], P('mp'), may hold values from -3 to 3
- w_pw2: bfloat16 [1536, 1536], P('dp', 'mp'), may hold values from -0.15625 to 0.15625
- cotangent: bfloat16 [65536, 1536], P('dp', 'mp'), may hold values from -6 to 6
Outputs:
- encoded: bfloat16 [65536, 1536], P('dp', 'mp')
- grad_pw1: float32 [1536, 2, 1536], P('dp', None, 'mp')
- grad_pw2: float32 [1536, 1536], P('dp', 'mp')
- grad_kernel: float32 [31, 1536], P(None, 'mp')
- grad_bn_gain: float32 [1536], P('mp')
- grad_bn_bias: float32 [1536], P('mp')
Inputs may be any that keep to these rules, and one draw needn't show every extreme that they name: `picks`: each trainer takes one block of every shard; a shard may give the same block to several trainers.
All inputs are finite; a program needn't handle non-finite values. No bound on the sum of `lengths` on one device may be relied on, other than what follows from the above.
Results may differ from a plain program's by a relative error of at most 0.0057.
Values may be sent and summed in bfloat16 or wider, within the bound.
No kernel may reach another device: no remote copies, remote signals or barrier semaphores. Data moves between devices by JAX's collectives and lax.ppermute only.
A program may use at most 64 MiB of HBM per device.

v0:
```python
import jax
import jax.numpy as jnp
from jax import lax
from jax.sharding import PartitionSpec as P

EPS = 1e-05


def depth_conv(values, taps, frames):
    chans = values.shape[1]
    shaped = values.reshape(-1, frames, chans)
    margin = taps.shape[0] // 2
    padded = jnp.pad(shaped, ((0, 0), (margin, margin), (0, 0)))
    total = jnp.zeros(shaped.shape, jnp.float32)
    for step in range(taps.shape[0]):
        total = total + taps[step] * padded[:, step : step + frames]
    return total.reshape(values.shape)


def depth_back(grads, taps, frames):
    chans = grads.shape[1]
    shaped = grads.reshape(-1, frames, chans)
    margin = taps.shape[0] // 2
    padded = jnp.pad(shaped, ((0, 0), (margin, margin), (0, 0)))
    total = jnp.zeros(shaped.shape, jnp.float32)
    for step in range(taps.shape[0]):
        begin = 2 * margin - step
        total = total + taps[step] * padded[:, begin : begin + frames]
    return total.reshape(grads.shape)


def kernel_terms(grads, values, width, frames):
    chans = values.shape[1]
    shaped = values.reshape(-1, frames, chans)
    grad_shaped = grads.reshape(-1, frames, chans)
    margin = width // 2
    padded = jnp.pad(shaped, ((0, 0), (margin, margin), (0, 0)))
    rows_out = []
    for step in range(width):
        rows_out.append(jnp.sum(grad_shaped * padded[:, step : step + frames], axis=(0, 1)))
    return jnp.stack(rows_out, 0)


def contract_rows(left, right):
    return lax.dot_general(
        left, right, (((0,), (0,)), ((), ())), preferred_element_type=jnp.float32
    )


def on_device(
    corpus,
    picks,
    lengths,
    langs,
    w_in,
    lang_table,
    ln_gain,
    w_pw1,
    kernel,
    bn_gain,
    bn_bias,
    w_pw2,
    cotangent,
):
    model_width = w_pw2.shape[0] * lax.axis_size("dp")
    chosen = picks[0]
    blocks = jnp.take(corpus, chosen, axis=0)
    lens_send = jnp.take(lengths, chosen)
    lang_send = jnp.take(langs, chosen)
    received, lens, lang = (
        lax.all_to_all(blocks, "dp", split_axis=0, concat_axis=0, tiled=True),
        lax.all_to_all(lens_send, "dp", split_axis=0, concat_axis=0, tiled=True),
        lax.all_to_all(lang_send, "dp", split_axis=0, concat_axis=0, tiled=True),
    )
    frames = received.shape[1]
    valid = (
        (jnp.arange(frames, dtype=jnp.int32)[None, :] < lens[:, None])
        .astype(jnp.float32)
        .reshape(-1)
    )
    valid_col = valid[:, None]
    mel = received.reshape(-1, received.shape[2]) * valid_col.astype(jnp.bfloat16)
    onehot = (lang[:, None] == jnp.arange(lang_table.shape[0], dtype=jnp.int32)[None, :]).astype(
        jnp.bfloat16
    )
    lang_rows = jnp.dot(onehot, lang_table, preferred_element_type=jnp.float32)
    inputs = jnp.dot(mel, w_in, preferred_element_type=jnp.float32) + jnp.repeat(
        lang_rows, frames, axis=0
    )
    row_sum, row_sq = lax.psum((jnp.sum(inputs, 1), jnp.sum(inputs * inputs, 1)), "mp")
    mean = row_sum / model_width
    var = row_sq / model_width - mean * mean
    normed_in = ((inputs - mean[:, None]) * lax.rsqrt(var + EPS)[:, None] * ln_gain).astype(
        jnp.bfloat16
    )
    weights_one = lax.all_gather(w_pw1, "dp", axis=0, tiled=True).reshape(model_width, -1)
    half = weights_one.shape[1] // 2
    normed_full = lax.all_gather(normed_in, "mp", axis=1, tiled=True)
    pre = jnp.dot(normed_full, weights_one, preferred_element_type=jnp.float32)
    linear_part = pre[:, :half]
    gate_part = pre[:, half:]
    gate_sig = jax.nn.sigmoid(gate_part)
    glu_out = linear_part * gate_sig * valid_col
    conv_out = depth_conv(glu_out, kernel, frames)
    sum_conv, sum_sq, count = lax.psum(
        (
            jnp.sum(valid_col * conv_out, 0),
            jnp.sum(valid_col * conv_out * conv_out, 0),
            jnp.sum(valid),
        ),
        "dp",
    )
    mu_conv = sum_conv / count
    var_conv = sum_sq / count - mu_conv * mu_conv
    inv_std = lax.rsqrt(var_conv + EPS)
    normed_conv = (conv_out - mu_conv) * inv_std
    act = normed_conv * bn_gain + bn_bias
    act_sig = jax.nn.sigmoid(act)
    hidden = (valid_col * act * act_sig).astype(jnp.bfloat16)
    weights_two = lax.all_gather(w_pw2, "dp", axis=0, tiled=True)
    hidden_full = lax.all_gather(hidden, "mp", axis=1, tiled=True)
    encoded = (
        inputs + jnp.dot(hidden_full, weights_two, preferred_element_type=jnp.float32)
    ).astype(jnp.bfloat16)
    grad_pw2 = lax.psum_scatter(
        contract_rows(hidden_full, cotangent), "dp", scatter_dimension=0, tiled=True
    )
    cot_full = lax.all_gather(cotangent, "mp", axis=1, tiled=True)
    weights_rows = lax.all_to_all(weights_two, "mp", split_axis=0, concat_axis=1, tiled=True)
    dhidden = lax.dot_general(
        cot_full, weights_rows, (((1,), (1,)), ((), ())), preferred_element_type=jnp.float32
    )
    dact = dhidden * valid_col * act_sig * (1.0 + act * (1.0 - act_sig))
    grad_bias, grad_gain = lax.psum((jnp.sum(dact, 0), jnp.sum(dact * normed_conv, 0)), "dp")
    dconv = (
        valid_col * inv_std * bn_gain * (dact - grad_bias / count - normed_conv * grad_gain / count)
    )
    grad_kernel = lax.psum(kernel_terms(dconv, glu_out, kernel.shape[0], frames), "dp")
    dglu = depth_back(dconv, kernel, frames)
    dlin = dglu * valid_col * gate_sig
    dgate = dglu * valid_col * linear_part * gate_sig * (1.0 - gate_sig)
    dpre = jnp.concatenate([dlin, dgate], 1).astype(jnp.bfloat16)
    grad_pw1 = lax.psum_scatter(
        contract_rows(normed_full, dpre), "dp", scatter_dimension=0, tiled=True
    )
    grad_pw1 = grad_pw1.reshape(grad_pw1.shape[0], 2, half)
    return (encoded, grad_pw1, grad_pw2, grad_kernel, grad_gain, grad_bias)


def solution(mesh):
    return jax.shard_map(
        on_device,
        mesh=mesh,
        in_specs=(
            P("dp", None, None),
            P("dp", None),
            P("dp"),
            P("dp"),
            P(None, "mp"),
            P(None, "mp"),
            P("mp"),
            P("dp", None, "mp"),
            P(None, "mp"),
            P("mp"),
            P("mp"),
            P("dp", "mp"),
            P("dp", "mp"),
        ),
        out_specs=(
            P("dp", "mp"),
            P("dp", None, "mp"),
            P("dp", "mp"),
            P(None, "mp"),
            P("mp"),
            P("mp"),
        ),
        check_vma=False,
    )
```

profile of v0, /device:TPU:1, one launch (start us, length us, event | category | flops | bytes accessed | tf_op | source)
XLA Modules:
  0.0 824.4 jit_solution(1097332180774315246)
XLA Ops:
  7.2 0.7 compare_select_fusion.1
  7.9 1.4 gather_fusion.1
  10.0 0.7 copy.39
  10.7 11.6 %all-to-all-start.1 = ((s32[64,1,1]{2,1,0:T(1,128)}), s32[64,1,1]{2,1,0:T(1,128)S(1)}, u32[]{:S(2)}, u32[]{:S(2)}) async-start(s32[64,1,1]{2,1,0:T(1,128)} %copy.39), calls=%async_computation.1 | async-start | bytes 65536 | tf_op jit(solution)/shard_map/all_to_all | solution.py:72
  23.0 1.4 gather_fusion.2
  24.4 2.1 copy.38
  26.6 0.7 copy.40
  27.3 0.7 gather_fusion
  28.0 3.5 all-to-all-done.1
  31.5 6.8 all-to-all-start.2
  38.4 1.0 broadcast_select_fusion
  39.4 8.2 all-to-all-done.2
  47.6 4.7 all-to-all-start
  52.4 0.7 all-gather.7.cloned.1.call-update
  53.1 1.2 reduce.4
  54.5 1.2 reduce.5
  56.4 19.0 %all-to-all-done = bf16[64,16,320]{2,1,0:T(8,128)(2,1)S(1)} async-done(((bf16[64,16,320]{2,1,0:T(8,128)(2,1)}), bf16[64,16,320]{2,1,0:T(8,128)(2,1)S(1)}, u32[]{:S(2)}, u32[]{:S(2)}) %all-to-all-start) | async-done | bytes 655392 | tf_op jit(solution)/shard_map/all_to_all | solution.py:71
  76.1 20.0 %all-reduce.5 = (f32[1024]{0:T(1024)S(1)}, f32[1024]{0:T(1024)S(1)}) all-reduce(f32[1024]{0:T(1024)S(1)} %get-tuple-element.42, f32[1024]{0:T(1024)S(1)} %get-tuple-element.41), channel_id=1, replica_groups=mesh['dp'=64,'mp'=8] {'mp'}, use_global_device_ids=true, to_apply=%region_3.5 | all-reduce | flops 2048 | bytes 16384 | tf_op jit(solution)/shard_map/psum | solution.py:90
  96.1 0.9 multiply_convert_fusion.3
  97.8 57.1 %all_gather.18 = bf16[1536,192]{1,0:T(8,128)(2,1)} all-gather(bf16[24,192]{1,0:T(8,128)(2,1)S(1)} %copy-done.11), channel_id=1, replica_groups=mesh['dp'=64,'mp'=8] {'dp'}, dimensions={0}, use_global_device_ids=true | all-gather | bytes 599040 | tf_op jit(solution)/shard_map/all_gather | solution.py:120
  154.9 3.5 all-to-all-start.3
  160.0 0.7 fusion.74
  160.7 29.1 %all-to-all-done.3 = bf16[8,192,192]{2,1,0:T(8,128)(2,1)S(1)} async-done(((bf16[8,192,192]{2,1,0:T(8,128)(2,1)}), bf16[8,192,192]{2,1,0:T(8,128)(2,1)S(1)}, u32[]{:S(2)}, u32[]{:S(2)}) %all-to-all-start.3) | async-done | bytes 589856 | tf_op jit(solution)/shard_map/all_to_all | solution.py:129
  190.2 1.5 all_to_all.37
  191.7 4.9 copy.42
  196.6 12.2 %all-gather.5.cloned.1.call-done = bf16[1024,1536]{0,1:T(8,128)(2,1)} async-done(((bf16[1024,192]{0,1:T(8,128)(2,1)}), bf16[1024,1536]{0,1:T(8,128)(2,1)}) %all-gather.5.cloned.1.call-update) | async-done | bytes 3145744 | tf_op jit(solution)/shard_map/all_gather | solution.py:98
  208.8 3.6 fusion.82
  213.1 6.3 fusion.3
  219.3 1.5 copy.44
  220.9 125.0 %all-reduce.4 = (f32[192]{0:T(256)}, f32[]{:T(128)}, f32[192]{0:T(256)}) all-reduce(f32[192]{0:T(256)} %get-tuple-element.38, f32[]{:T(128)} %fusion.74, f32[192]{0:T(256)} %get-tuple-element.37), channel_id=1, replica_groups=mesh['dp'=64,'mp'=8] {'dp'}, use_global_device_ids=true, to_apply=%region_5.7 | all-reduce | flops 385 | bytes 3080 | tf_op jit(solution)/shard_map/psum | solution.py:105
  345.9 1.9 add_rsqrt_fusion.1
  347.8 4.5 fusion.77
  352.3 127.1 %all-reduce.3 = (f32[192]{0:T(256)}, f32[192]{0:T(256)}) all-reduce(f32[192]{0:T(256)} %get-tuple-element.40, f32[192]{0:T(256)} %get-tuple-element.39), channel_id=1, replica_groups=mesh['dp'=64,'mp'=8] {'dp'}, use_global_device_ids=true, to_apply=%region_13.15 | all-reduce | flops 384 | bytes 3072 | tf_op jit(solution)/shard_map/psum | solution.py:134
  479.4 1.3 broadcast_divide_fusion
  480.7 4.1 multiply_reduce_fusion.31
  484.9 1.5 copy.46
  486.4 4.3 fusion.55
  490.7 1.3 copy.47
  492.0 2.1 multiply_convert_fusion.1
  494.6 3.2 fusion.67
  498.1 26.7 %all-gather.9.cloned.1.call-done = bf16[1024,1536]{0,1:T(8,128)(2,1)} async-done(((bf16[1024,192]{0,1:T(8,128)(2,1)}), bf16[1024,1536]{0,1:T(8,128)(2,1)}) %all-gather.9.cloned.1.call-update) | async-done | bytes 3145744 | tf_op jit(solution)/shard_map/all_gather | solution.py:121
  524.9 4.0 fusion.81
  528.9 1.7 multiply_reduce_fusion.2
  530.6 3.0 multiply_reduce_fusion.1
  533.7 245.8 %psum.63 = f32[31,192]{1,0:T(8,128)} all-reduce(f32[31,192]{1,0:T(8,128)S(1)} %stack.127), channel_id=1, replica_groups=mesh['dp'=64,'mp'=8] {'dp'}, use_global_device_ids=true, to_apply=%region_47.49 | all-reduce | flops 5952 | bytes 47616 | tf_op jit(solution)/shard_map/psum | solution.py:138
  779.5 1.5 reshape.176
  781.0 3.6 fusion.2
  784.7 32.9 %reduce-scatter.5.cloned.1.call-done = f32[24,192]{1,0:T(8,128)} async-done(((f32[1536,192]{1,0:T(8,128)}), f32[24,192]{1,0:T(8,128)}) %reduce-scatter.5.cloned.1.call-update) | async-done | bytes 18448 | tf_op jit(solution)/shard_map/reduce_scatter | solution.py:125
  (64 shorter events, 7.1 us)
Async XLA Ops:
  7.2 68.4 %copy-start = (bf16[320,192]{0,1:T(8,128)(2,1)S(1)}, bf16[320,192]{0,1:T(8,128)(2,1)}, u32[]{:S(2)}) copy-start(bf16[320,192]{0,1:T(8,128)(2,1)} %param.19) | copy-start | bytes 368644
  10.7 20.9 %all-to-all-start.1 = ((s32[64,1,1]{2,1,0:T(1,128)}), s32[64,1,1]{2,1,0:T(1,128)S(1)}, u32[]{:S(2)}, u32[]{:S(2)}) async-start(s32[64,1,1]{2,1,0:T(1,128)} %copy.39), calls=%async_computation.1 | async-start | bytes 65536 | tf_op jit(solution)/shard_map/all_to_all | solution.py:72
  26.6 29.2 %copy-start.9 = (bf16[128,192]{0,1:T(8,128)(2,1)S(1)}, bf16[128,192]{0,1:T(8,128)(2,1)}, u32[]{:S(2)}) copy-start(bf16[128,192]{0,1:T(8,128)(2,1)} %param.20) | copy-start | bytes 147460
  31.5 16.0 %all-to-all-start.2 = ((s32[64,1,1]{2,1,0:T(1,128)}), s32[64,1,1]{2,1,0:T(1,128)S(1)}, u32[]{:S(2)}, u32[]{:S(2)}) async-start(s32[64,1,1]{2,1,0:T(1,128)} %copy.40), calls=%async_computation.2 | async-start | bytes 65536 | tf_op jit(solution)/shard_map/all_to_all | solution.py:73
  47.6 27.8 %all-to-all-start = ((bf16[64,16,320]{2,1,0:T(8,128)(2,1)}), bf16[64,16,320]{2,1,0:T(8,128)(2,1)S(1)}, u32[]{:S(2)}, u32[]{:S(2)}) async-start(bf16[64,16,320]{2,1,0:T(8,128)(2,1)} %broadcast_select_fusion), calls=%async_computation | async-start | bytes 1572864 | tf_op jit(solution)/shard_map/all_to_all | solution.py:71
  52.3 139.4 %all-gather.7.cloned.1.call-start = ((), (), s32[]{:S(2)}) async-start(), calls=%async_computation.7 | async-start | bytes 1597440 | tf_op jit(solution)/shard_map/all_gather | solution.py:96
  53.1 155.7 %all-gather.5.cloned.1.call-start = ((), (), s32[]{:S(2)}) async-start(), calls=%async_computation.6 | async-start | bytes 3538944 | tf_op jit(solution)/shard_map/all_gather | solution.py:98
  54.4 1.3 copy-start.5
  54.5 1.2 copy-start.6
  56.1 40.1 %copy-start.13 = (f32[192]{0:T(256)S(1)}, f32[192]{0:T(256)}, u32[]{:S(2)}) copy-start(f32[192]{0:T(256)} %param.21) | copy-start | bytes 2308
  56.4 41.4 %copy-start.11 = (bf16[24,192]{1,0:T(8,128)(2,1)S(1)}, bf16[24,192]{1,0:T(8,128)(2,1)}, u32[]{:S(2)}) copy-start(bf16[24,192]{1,0:T(8,128)(2,1)} %param.26) | copy-start | bytes 27652
  75.6 83.1 %copy-start.10 = (f32[31,192]{1,0:T(8,128)S(1)}, f32[31,192]{1,0:T(8,128)}, u32[]{:S(2)}) copy-start(f32[31,192]{1,0:T(8,128)} %param.23) | copy-start | bytes 71428
  76.1 115.7 %copy-start.2 = (f32[1024,192]{0,1:T(8,128)}, f32[1024,192]{0,1:T(8,128)S(1)}, u32[]{:S(2)}) copy-start(f32[1024,192]{0,1:T(8,128)S(1)} %get-tuple-element.93) | copy-start | bytes 2359300
  97.0 250.7 %all-gather.11.cloned.1.call-start = ((), (), s32[]{:S(2)}) async-start(), calls=%async_computation.9 | async-start | bytes 3538944 | tf_op jit(solution)/shard_map/all_gather | solution.py:128
  154.9 34.9 %all-to-all-start.3 = ((bf16[8,192,192]{2,1,0:T(8,128)(2,1)}), bf16[8,192,192]{2,1,0:T(8,128)(2,1)S(1)}, u32[]{:S(2)}, u32[]{:S(2)}) async-start(bf16[8,192,192]{2,1,0:T(8,128)(2,1)} %bitcast.41), calls=%async_computation.3 | async-start | bytes 1572864 | tf_op jit(solution)/shard_map/all_to_all | solution.py:129
  158.5 366.4 %all-gather.9.cloned.1.call-start = ((), (), s32[]{:S(2)}) async-start(), calls=%async_computation.8 | async-start | bytes 3538944 | tf_op jit(solution)/shard_map/all_gather | solution.py:121
  208.8 3.7 copy-start.7
  212.5 272.3 %copy-start.1 = (f32[1024,384]{0,1:T(8,128)}, f32[1024,384]{0,1:T(8,128)S(1)}, u32[]{:S(2)}) copy-start(f32[1024,384]{0,1:T(8,128)S(1)} %fusion.82) | copy-start | bytes 4718596
  484.8 7.2 copy-start.8
  484.9 294.7 %reduce-scatter.7.cloned.1.call-start = ((), (), s32[]{:S(2)}) async-start(), calls=%async_computation.11 | async-start | bytes 2396160
  492.0 2.6 copy-start.14
  494.6 30.3 %copy-start.4 = (bf16[1024,192]{0,1:T(8,128)(2,1)S(1)}, bf16[1024,192]{0,1:T(8,128)(2,1)}, u32[]{:S(2)}) copy-start(bf16[1024,192]{0,1:T(8,128)(2,1)} %param.27) | copy-start | bytes 1179652
  497.9 319.7 %reduce-scatter.5.cloned.1.call-start = ((), (), s32[]{:S(2)}) async-start(), calls=%async_computation.10 | async-start | bytes 1597440 | tf_op jit(solution)/shard_map/reduce_scatter | solution.py:125
  528.9 4.7 copy-start.12
  528.9 252.1 %copy-start.3 = (f32[1024,192]{0,1:T(8,128)S(1)}, f32[1024,192]{0,1:T(8,128)}, u32[]{:S(2)}) copy-start(f32[1024,192]{0,1:T(8,128)} %copy-done.2) | copy-start | bytes 2359300
Sparse Core Ops, SparseCore 0:
  56.5 86.9 all-gather.6
  146.1 62.6 all-gather.4
  210.9 44.0 all-gather.10
  485.0 39.8 all-gather.8
  529.4 135.4 reduce-scatter.6
  669.9 147.5 reduce-scatter.4
where the time goes:
time: 830 us; the launch traced here: 824 us
  blocking collectives  575 us (69%)
  waiting for transfers between devices  133 us (16%)
  other arithmetic  32.4 us (4%)
  starting transfers between devices  27.3 us (3%)
  local copies, waits for them, and re-layouts  22.4 us (3%)
  matrix products  19.7 us (2%)
  between operations  14.4 us (2%)
    psum x1, blocking collectives, on_device(): lax.psum(kernel_terms(dconv, glu_out, kernel.shape[0], frames), 'dp')  246 us
    psum x1, blocking collectives, on_device(): lax.psum((jnp.sum(dact, 0), jnp.sum(dact * normed_conv, 0)), 'dp')  127 us
    psum x1, blocking collectives, on_device(): lax.psum((jnp.sum(valid_col * conv_out, 0), jnp.sum(valid_col * conv_out...  125 us
    all_gather x1, blocking collectives, on_device(): weights_two = lax.all_gather(w_pw2, 'dp', axis=0, tiled=True)  57.1 us
    reduce_scatter x1, waiting for transfers between devices, on_device(): lax.psum_scatter(contract_rows(hidden_full, cotangent), 'dp', scatter_dim...  32.9 us
    all_to_all x1, waiting for transfers between devices, on_device(): lax.all_to_all(weights_two, 'mp', split_axis=0, concat_axis=1, tiled=True)  29.1 us
    all_gather x1, waiting for transfers between devices, on_device(): hidden_full = lax.all_gather(hidden, 'mp', axis=1, tiled=True)  26.7 us
    psum x1, blocking collectives, on_device(): lax.psum((jnp.sum(inputs, 1), jnp.sum(inputs * inputs, 1)), 'mp')  20 us
  transfers between devices with their start and end apart: 10, of which 7 were waited for; matrix products, arithmetic and copies ran while one was open for 7% of the time, Pallas kernels for 0%

commit v1 on v0

--- a/solution.py
+++ b/solution.py
@@ -1,7 +1,7 @@
 import jax
 import jax.numpy as jnp
 from jax import lax
-from jax.sharding import PartitionSpec as P
+from jax.sharding import Mesh, PartitionSpec as P
 
 EPS = 1e-05
 
@@ -39,6 +39,15 @@
     for step in range(width):
         rows_out.append(jnp.sum(grad_shaped * padded[:, step : step + frames], axis=(0, 1)))
     return jnp.stack(rows_out, 0)
+
+
+DP_AXES = ("x", "y", "c")
+
+
+def dp_sum(value):
+    for name in reversed(DP_AXES):
+        value = lax.psum(value, name)
+    return value
 
 
 def contract_rows(left, right):
@@ -62,15 +71,15 @@
     w_pw2,
     cotangent,
 ):
-    model_width = w_pw2.shape[0] * lax.axis_size("dp")
+    model_width = w_pw2.shape[0] * lax.axis_size(DP_AXES)
     chosen = picks[0]
     blocks = jnp.take(corpus, chosen, axis=0)
     lens_send = jnp.take(lengths, chosen)
     lang_send = jnp.take(langs, chosen)
     received, lens, lang = (
-        lax.all_to_all(blocks, "dp", split_axis=0, concat_axis=0, tiled=True),
-        lax.all_to_all(lens_send, "dp", split_axis=0, concat_axis=0, tiled=True),
-        lax.all_to_all(lang_send, "dp", split_axis=0, concat_axis=0, tiled=True),
+        lax.all_to_all(blocks, DP_AXES, split_axis=0, concat_axis=0, tiled=True),
+        lax.all_to_all(lens_send, DP_AXES, split_axis=0, concat_axis=0, tiled=True),
+        lax.all_to_all(lang_send, DP_AXES, split_axis=0, concat_axis=0, tiled=True),
     )
     frames = received.shape[1]
     valid = (
@@ -93,7 +102,7 @@
     normed_in = ((inputs - mean[:, None]) * lax.rsqrt(var + EPS)[:, None] * ln_gain).astype(
         jnp.bfloat16
     )
-    weights_one = lax.all_gather(w_pw1, "dp", axis=0, tiled=True).reshape(model_width, -1)
+    weights_one = lax.all_gather(w_pw1, DP_AXES, axis=0, tiled=True).reshape(model_width, -1)
     half = weights_one.shape[1] // 2
     normed_full = lax.all_gather(normed_in, "mp", axis=1, tiled=True)
     pre = jnp.dot(normed_full, weights_one, preferred_element_type=jnp.float32)
@@ -102,13 +111,12 @@
     gate_sig = jax.nn.sigmoid(gate_part)
     glu_out = linear_part * gate_sig * valid_col
     conv_out = depth_conv(glu_out, kernel, frames)
-    sum_conv, sum_sq, count = lax.psum(
+    sum_conv, sum_sq, count = dp_sum(
         (
             jnp.sum(valid_col * conv_out, 0),
             jnp.sum(valid_col * conv_out * conv_out, 0),
             jnp.sum(valid),
-        ),
-        "dp",
+        )
     )
     mu_conv = sum_conv / count
     var_conv = sum_sq / count - mu_conv * mu_conv
@@ -117,13 +125,13 @@
     act = normed_conv * bn_gain + bn_bias
     act_sig = jax.nn.sigmoid(act)
     hidden = (valid_col * act * act_sig).astype(jnp.bfloat16)
-    weights_two = lax.all_gather(w_pw2, "dp", axis=0, tiled=True)
+    weights_two = lax.all_gather(w_pw2, DP_AXES, axis=0, tiled=True)
     hidden_full = lax.all_gather(hidden, "mp", axis=1, tiled=True)
     encoded = (
         inputs + jnp.dot(hidden_full, weights_two, preferred_element_type=jnp.float32)
     ).astype(jnp.bfloat16)
     grad_pw2 = lax.psum_scatter(
-        contract_rows(hidden_full, cotangent), "dp", scatter_dimension=0, tiled=True
+        contract_rows(hidden_full, cotangent), DP_AXES, scatter_dimension=0, tiled=True
     )
     cot_full = lax.all_gather(cotangent, "mp", axis=1, tiled=True)
     weights_rows = lax.all_to_all(weights_two, "mp", split_axis=0, concat_axis=1, tiled=True)
@@ -131,45 +139,61 @@
         cot_full, weights_rows, (((1,), (1,)), ((), ())), preferred_element_type=jnp.float32
     )
     dact = dhidden * valid_col * act_sig * (1.0 + act * (1.0 - act_sig))
-    grad_bias, grad_gain = lax.psum((jnp.sum(dact, 0), jnp.sum(dact * normed_conv, 0)), "dp")
+    grad_bias, grad_gain = dp_sum((jnp.sum(dact, 0), jnp.sum(dact * normed_conv, 0)))
     dconv = (
         valid_col * inv_std * bn_gain * (dact - grad_bias / count - normed_conv * grad_gain / count)
     )
-    grad_kernel = lax.psum(kernel_terms(dconv, glu_out, kernel.shape[0], frames), "dp")
+    grad_kernel = dp_sum(kernel_terms(dconv, glu_out, kernel.shape[0], frames))
     dglu = depth_back(dconv, kernel, frames)
     dlin = dglu * valid_col * gate_sig
     dgate = dglu * valid_col * linear_part * gate_sig * (1.0 - gate_sig)
     dpre = jnp.concatenate([dlin, dgate], 1).astype(jnp.bfloat16)
     grad_pw1 = lax.psum_scatter(
-        contract_rows(normed_full, dpre), "dp", scatter_dimension=0, tiled=True
+        contract_rows(normed_full, dpre), DP_AXES, scatter_dimension=0, tiled=True
     )
     grad_pw1 = grad_pw1.reshape(grad_pw1.shape[0], 2, half)
     return (encoded, grad_pw1, grad_pw2, grad_kernel, grad_gain, grad_bias)
 
 
+def dp_shape(mesh):
+    along = mesh.devices[:, 0]
+    try:
+        xs = len({d.coords[0] for d in along})
+        ys = len({d.coords[1] for d in along})
+    except AttributeError:
+        xs, ys = 1, 1
+    cores = mesh.shape["dp"] // (xs * ys)
+    return xs, ys, cores
+
+
 def solution(mesh):
+    xs, ys, cores = dp_shape(mesh)
+    fine = Mesh(
+        mesh.devices.reshape(xs, ys, cores, mesh.shape["mp"]), DP_AXES + ("mp",)
+    )
+    D = DP_AXES
     return jax.shard_map(
         on_device,
-        mesh=mesh,
+        mesh=fine,
         in_specs=(
-            P("dp", None, None),
-            P("dp", None),
-            P("dp"),
-            P("dp"),
-            P(None, "mp"),
-            P(None, "mp"),
-            P("mp"),
-            P("dp", None, "mp"),
-            P(None, "mp"),
-            P("mp"),
-            P("mp"),
-            P("dp", "mp"),
-            P("dp", "mp"),
+            P(D, None, None),
+            P(D, None),
+            P(D),
+            P(D),
+            P(None, "mp"),
+            P(None, "mp"),
+            P("mp"),
+            P(D, None, "mp"),
+            P(None, "mp"),
+            P("mp"),
+            P("mp"),
+            P(D, "mp"),
+            P(D, "mp"),
         ),
         out_specs=(
-            P("dp", "mp"),
-            P("dp", None, "mp"),
-            P("dp", "mp"),
+            P(D, "mp"),
+            P(D, None, "mp"),
+            P(D, "mp"),
             P(None, "mp"),
             P("mp"),
             P("mp"),

time: 830 us -> 644 us (0.78)
  blocking collectives: 575 us -> 172 us
  waiting for transfers between devices: 133 us -> 350 us
    psum x3 -> x9, blocking collectives: 498 us -> 95 us  [dp_sum(): value = lax.psum(value, name)]
    reduce_scatter x1, waiting for transfers between devices: 32.9 us -> 148 us  [on_device(): lax.psum_scatter(contract_rows(hidden_full, cotangent), DP_AXES, scatter_...]
    unnamed x7, waiting for transfers between devices: 1.43 us -> 91.5 us
  transfers between devices with their start and end apart: 10 -> 10, of which waited for: 7 -> 9; matrix products, arithmetic and copies ran while one was open for 7% -> 9% of each run, Pallas kernels for 0% -> 0%
where the time goes in v1:
time: 644 us; the launch traced here: 639 us
  waiting for transfers between devices  350 us (54%)
  blocking collectives  172 us (27%)
  other arithmetic  32.3 us (5%)
  starting transfers between devices  27.3 us (4%)
  local copies, waits for them, and re-layouts  22.4 us (3%)
  matrix products  19.7 us (3%)
  between operations  14.4 us (2%)
    reduce_scatter x1, waiting for transfers between devices, on_device(): lax.psum_scatter(contract_rows(hidden_full, cotangent), DP_AXES, scatter_...  148 us
    psum x9, blocking collectives, dp_sum(): value = lax.psum(value, name)  95 us
    unnamed x7, waiting for transfers between devices  91.5 us
    all_gather x1, blocking collectives, on_device(): weights_two = lax.all_gather(w_pw2, DP_AXES, axis=0, tiled=True)  57.1 us
    all_gather x1, waiting for transfers between devices, on_device(): hidden_full = lax.all_gather(hidden, 'mp', axis=1, tiled=True)  33.9 us
    all_to_all x1, waiting for transfers between devices, on_device(): lax.all_to_all(weights_two, 'mp', split_axis=0, concat_axis=1, tiled=True)  29.1 us
    psum x1, blocking collectives, on_device(): lax.psum((jnp.sum(inputs, 1), jnp.sum(inputs * inputs, 1)), 'mp')  20 us
    all_to_all x1, waiting for transfers between devices, on_device(): lax.all_to_all(blocks, DP_AXES, split_axis=0, concat_axis=0, tiled=True)  19 us
  transfers between devices with their start and end apart: 10, of which 9 were waited for; matrix products, arithmetic and copies ran while one was open for 9% of the time, Pallas kernels for 0%

profile of v1, /device:TPU:1, one launch (start us, length us, event | category | flops | bytes accessed | tf_op | source)
XLA Modules:
  0.0 638.5 jit_solution(16453349370406005419)
XLA Ops:
  7.9 1.4 gather_fusion.1
  10.7 11.6 %all-to-all-start.1 = ((s32[64,1,1]{2,1,0:T(1,128)}), s32[64,1,1]{2,1,0:T(1,128)S(1)}, u32[]{:S(2)}, u32[]{:S(2)}) async-start(s32[64,1,1]{2,1,0:T(1,128)} %copy.39), calls=%async_computation.1 | async-start | bytes 65536 | tf_op jit(solution)/shard_map/all_to_all | solution.py:81
  23.0 1.4 gather_fusion.2
  24.4 2.1 copy.38
  28.0 3.5 all-to-all-done.1
  31.5 6.8 %all-to-all-start.2 = ((s32[64,1,1]{2,1,0:T(1,128)}), s32[64,1,1]{2,1,0:T(1,128)S(1)}, u32[]{:S(2)}, u32[]{:S(2)}) async-start(s32[64,1,1]{2,1,0:T(1,128)} %copy.40), calls=%async_computation.2 | async-start | bytes 65536 | tf_op jit(solution)/shard_map/all_to_all | solution.py:82
  39.4 8.2 %all-to-all-done.2 = s32[64,1,1]{2,1,0:T(1,128)S(1)} async-done(((s32[64,1,1]{2,1,0:T(1,128)}), s32[64,1,1]{2,1,0:T(1,128)S(1)}, u32[]{:S(2)}, u32[]{:S(2)}) %all-to-all-start.2) | async-done | bytes 288 | tf_op jit(solution)/shard_map/all_to_all | solution.py:82
  47.6 4.7 all-to-all-start
  53.1 1.2 reduce.4
  54.5 1.2 reduce.5
  56.4 19.0 %all-to-all-done = bf16[64,16,320]{2,1,0:T(8,128)(2,1)S(1)} async-done(((bf16[64,16,320]{2,1,0:T(8,128)(2,1)}), bf16[64,16,320]{2,1,0:T(8,128)(2,1)S(1)}, u32[]{:S(2)}, u32[]{:S(2)}) %all-to-all-start) | async-done | bytes 655392 | tf_op jit(solution)/shard_map/all_to_all | solution.py:80
  76.1 20.0 %all-reduce.3 = (f32[1024]{0:T(1024)S(1)}, f32[1024]{0:T(1024)S(1)}) all-reduce(f32[1024]{0:T(1024)S(1)} %get-tuple-element.42, f32[1024]{0:T(1024)S(1)} %get-tuple-element.41), channel_id=1, replica_groups=mesh['x'=4,'y'=8,'c'=2,'mp'=8] {'mp'}, use_global_device_ids=true, to_apply=%region_3.5 | all-reduce | flops 2048 | bytes 16384 | tf_op jit(solution)/shard_map/psum | solution.py:99
  97.8 57.1 %all_gather.18 = bf16[1536,192]{1,0:T(8,128)(2,1)} all-gather(bf16[24,192]{1,0:T(8,128)(2,1)S(1)} %copy-done.11), channel_id=1, replica_groups=mesh['x'=4,'y'=8,'c'=2,'mp'=8] {'x','y','c'}, dimensions={0}, use_global_device_ids=true | all-gather | bytes 599040 | tf_op jit(solution)/shard_map/all_gather | solution.py:128
  154.9 3.5 all-to-all-start.3
  160.7 29.1 %all-to-all-done.3 = bf16[8,192,192]{2,1,0:T(8,128)(2,1)S(1)} async-done(((bf16[8,192,192]{2,1,0:T(8,128)(2,1)}), bf16[8,192,192]{2,1,0:T(8,128)(2,1)S(1)}, u32[]{:S(2)}, u32[]{:S(2)}) %all-to-all-start.3) | async-done | bytes 589856 | tf_op jit(solution)/shard_map/all_to_all | solution.py:137
  190.2 1.5 all_to_all.37
  191.8 4.9 copy.42
  196.6 12.3 %all-gather.5.cloned.1.call-done = bf16[1024,1536]{0,1:T(8,128)(2,1)} async-done(((bf16[1024,192]{0,1:T(8,128)(2,1)}), bf16[1024,1536]{0,1:T(8,128)(2,1)}) %all-gather.5.cloned.1.call-update) | async-done | bytes 3145744 | tf_op jit(solution)/shard_map/all_gather | solution.py:107
  208.9 3.6 fusion.82
  213.1 6.3 fusion.3
  219.4 1.5 copy.44
  220.9 3.7 all-reduce.9
  224.6 14.4 %all-reduce.5 = (f32[192]{0:T(256)}, f32[]{:T(128)}, f32[192]{0:T(256)}) all-reduce(f32[192]{0:T(256)} %get-tuple-element.57, f32[]{:T(128)} %get-tuple-element.58, f32[192]{0:T(256)} %get-tuple-element.59), channel_id=1, replica_groups=mesh['x'=4,'y'=8,'c'=2,'mp'=8] {'y'}, use_global_device_ids=true, to_apply=%region_6.8 | all-reduce | flops 385 | bytes 3080 | tf_op jit(solution)/shard_map/psum | solution.py:49
  239.0 9.3 %all-reduce.7 = (f32[192]{0:T(256)}, f32[]{:T(128)}, f32[192]{0:T(256)}) all-reduce(f32[192]{0:T(256)} %get-tuple-element.47, f32[]{:T(128)} %get-tuple-element.48, f32[192]{0:T(256)} %get-tuple-element.49), channel_id=1, replica_groups=mesh['x'=4,'y'=8,'c'=2,'mp'=8] {'x'}, use_global_device_ids=true, to_apply=%region_7.9 | all-reduce | flops 385 | bytes 3080 | tf_op jit(solution)/shard_map/psum | solution.py:49
  248.3 1.9 add_rsqrt_fusion.1
  250.2 4.8 all-gather.11.cloned.1.call-done
  255.0 4.5 fusion.77
  259.5 3.6 all-reduce.8
  263.1 14.2 %all-reduce.4 = (f32[192]{0:T(256)}, f32[192]{0:T(256)}) all-reduce(f32[192]{0:T(256)} %get-tuple-element.55, f32[192]{0:T(256)} %get-tuple-element.56), channel_id=1, replica_groups=mesh['x'=4,'y'=8,'c'=2,'mp'=8] {'y'}, use_global_device_ids=true, to_apply=%region_22.24 | all-reduce | flops 384 | bytes 3072 | tf_op jit(solution)/shard_map/psum | solution.py:49
  277.3 9.1 %all-reduce.6 = (f32[192]{0:T(256)}, f32[192]{0:T(256)}) all-reduce(f32[192]{0:T(256)} %get-tuple-element.45, f32[192]{0:T(256)} %get-tuple-element.46), channel_id=1, replica_groups=mesh['x'=4,'y'=8,'c'=2,'mp'=8] {'x'}, use_global_device_ids=true, to_apply=%region_23.25 | all-reduce | flops 384 | bytes 3072 | tf_op jit(solution)/shard_map/psum | solution.py:49
  286.4 1.3 broadcast_divide_fusion
  287.7 4.1 multiply_reduce_fusion.31
  291.9 1.5 copy.46
  293.3 4.3 fusion.55
  297.7 1.3 copy.47
  299.0 2.1 multiply_convert_fusion.1
  301.6 3.2 fusion.67
  305.1 33.9 %all-gather.9.cloned.1.call-done = bf16[1024,1536]{0,1:T(8,128)(2,1)} async-done(((bf16[1024,192]{0,1:T(8,128)(2,1)}), bf16[1024,1536]{0,1:T(8,128)(2,1)}) %all-gather.9.cloned.1.call-update) | async-done | bytes 3145744 | tf_op jit(solution)/shard_map/all_gather | solution.py:129
  339.0 4.0 fusion.81
  343.1 1.7 multiply_reduce_fusion.2
  344.7 3.0 multiply_reduce_fusion.1
  347.9 4.1 psum.157
  351.9 22.7 %psum.158 = f32[31,192]{1,0:T(8,128)S(1)} all-reduce(f32[31,192]{1,0:T(8,128)S(1)} %psum.157), channel_id=1, replica_groups=mesh['x'=4,'y'=8,'c'=2,'mp'=8] {'y'}, use_global_device_ids=true, to_apply=%region_58.60 | all-reduce | flops 5952 | bytes 47616 | tf_op jit(solution)/shard_map/psum | solution.py:49
  374.6 14.0 %psum.159 = f32[31,192]{1,0:T(8,128)} all-reduce(f32[31,192]{1,0:T(8,128)S(1)} %psum.158), channel_id=1, replica_groups=mesh['x'=4,'y'=8,'c'=2,'mp'=8] {'x'}, use_global_device_ids=true, to_apply=%region_59.61 | all-reduce | flops 5952 | bytes 47616 | tf_op jit(solution)/shard_map/psum | solution.py:49
  388.6 90.1 %reduce-scatter.7.cloned.1.call-done = f32[24,384]{1,0:T(8,128)} async-done(((f32[1536,384]{1,0:T(8,128)}), f32[24,384]{1,0:T(8,128)}) %reduce-scatter.7.cloned.1.call-update) | async-done | bytes 36880
  478.7 1.5 reshape.176
  480.2 3.7 fusion.2
  483.8 147.9 %reduce-scatter.5.cloned.1.call-done = f32[24,192]{1,0:T(8,128)} async-done(((f32[1536,192]{1,0:T(8,128)}), f32[24,192]{1,0:T(8,128)}) %reduce-scatter.5.cloned.1.call-update) | async-done | bytes 18448 | tf_op jit(solution)/shard_map/reduce_scatter | solution.py:133
  (70 shorter events, 13.2 us)
Async XLA Ops:
  7.2 68.4 %copy-start = (bf16[320,192]{0,1:T(8,128)(2,1)S(1)}, bf16[320,192]{0,1:T(8,128)(2,1)}, u32[]{:S(2)}) copy-start(bf16[320,192]{0,1:T(8,128)(2,1)} %param.19) | copy-start | bytes 368644
  10.7 20.9 %all-to-all-start.1 = ((s32[64,1,1]{2,1,0:T(1,128)}), s32[64,1,1]{2,1,0:T(1,128)S(1)}, u32[]{:S(2)}, u32[]{:S(2)}) async-start(s32[64,1,1]{2,1,0:T(1,128)} %copy.39), calls=%async_computation.1 | async-start | bytes 65536 | tf_op jit(solution)/shard_map/all_to_all | solution.py:81
  26.6 29.2 %copy-start.9 = (bf16[128,192]{0,1:T(8,128)(2,1)S(1)}, bf16[128,192]{0,1:T(8,128)(2,1)}, u32[]{:S(2)}) copy-start(bf16[128,192]{0,1:T(8,128)(2,1)} %param.20) | copy-start | bytes 147460
  31.5 16.0 %all-to-all-start.2 = ((s32[64,1,1]{2,1,0:T(1,128)}), s32[64,1,1]{2,1,0:T(1,128)S(1)}, u32[]{:S(2)}, u32[]{:S(2)}) async-start(s32[64,1,1]{2,1,0:T(1,128)} %copy.40), calls=%async_computation.2 | async-start | bytes 65536 | tf_op jit(solution)/shard_map/all_to_all | solution.py:82
  47.6 27.8 %all-to-all-start = ((bf16[64,16,320]{2,1,0:T(8,128)(2,1)}), bf16[64,16,320]{2,1,0:T(8,128)(2,1)S(1)}, u32[]{:S(2)}, u32[]{:S(2)}) async-start(bf16[64,16,320]{2,1,0:T(8,128)(2,1)} %broadcast_select_fusion), calls=%async_computation | async-start | bytes 1572864 | tf_op jit(solution)/shard_map/all_to_all | solution.py:80
  52.3 139.4 %all-gather.7.cloned.1.call-start = ((), (), s32[]{:S(2)}) async-start(), calls=%async_computation.7 | async-start | bytes 1597440 | tf_op jit(solution)/shard_map/all_gather | solution.py:105
  53.1 155.8 %all-gather.5.cloned.1.call-start = ((), (), s32[]{:S(2)}) async-start(), calls=%async_computation.6 | async-start | bytes 3538944 | tf_op jit(solution)/shard_map/all_gather | solution.py:107
  54.4 1.3 copy-start.5
  54.5 1.2 copy-start.6
  56.1 40.1 %copy-start.13 = (f32[192]{0:T(256)S(1)}, f32[192]{0:T(256)}, u32[]{:S(2)}) copy-start(f32[192]{0:T(256)} %param.21) | copy-start | bytes 2308
  56.4 41.4 %copy-start.11 = (bf16[24,192]{1,0:T(8,128)(2,1)S(1)}, bf16[24,192]{1,0:T(8,128)(2,1)}, u32[]{:S(2)}) copy-start(bf16[24,192]{1,0:T(8,128)(2,1)} %param.26) | copy-start | bytes 27652
  75.6 83.1 %copy-start.10 = (f32[31,192]{1,0:T(8,128)S(1)}, f32[31,192]{1,0:T(8,128)}, u32[]{:S(2)}) copy-start(f32[31,192]{1,0:T(8,128)} %param.23) | copy-start | bytes 71428
  76.1 115.7 %copy-start.2 = (f32[1024,192]{0,1:T(8,128)}, f32[1024,192]{0,1:T(8,128)S(1)}, u32[]{:S(2)}) copy-start(f32[1024,192]{0,1:T(8,128)S(1)} %get-tuple-element.103) | copy-start | bytes 2359300
  97.0 157.9 %all-gather.11.cloned.1.call-start = ((), (), s32[]{:S(2)}) async-start(), calls=%async_computation.9 | async-start | bytes 3538944 | tf_op jit(solution)/shard_map/all_gather | solution.py:136
  154.9 34.9 %all-to-all-start.3 = ((bf16[8,192,192]{2,1,0:T(8,128)(2,1)}), bf16[8,192,192]{2,1,0:T(8,128)(2,1)S(1)}, u32[]{:S(2)}, u32[]{:S(2)}) async-start(bf16[8,192,192]{2,1,0:T(8,128)(2,1)} %bitcast.41), calls=%async_computation.3 | async-start | bytes 1572864 | tf_op jit(solution)/shard_map/all_to_all | solution.py:137
  158.4 180.6 %all-gather.9.cloned.1.call-start = ((), (), s32[]{:S(2)}) async-start(), calls=%async_computation.8 | async-start | bytes 3538944 | tf_op jit(solution)/shard_map/all_gather | solution.py:129
  208.9 3.7 copy-start.7
  212.5 79.3 %copy-start.1 = (f32[1024,384]{0,1:T(8,128)}, f32[1024,384]{0,1:T(8,128)S(1)}, u32[]{:S(2)}) copy-start(f32[1024,384]{0,1:T(8,128)S(1)} %fusion.82) | copy-start | bytes 4718596
  291.8 7.2 %copy-start.8 = (f32[1024]{0:T(1024)S(1)}, f32[1024]{0:T(1024)}, u32[]{:S(2)}) copy-start(f32[1024]{0:T(1024)} %copy-done.6) | copy-start | bytes 12292
  291.8 186.8 %reduce-scatter.7.cloned.1.call-start = ((), (), s32[]{:S(2)}) async-start(), calls=%async_computation.11 | async-start | bytes 2396160
  299.0 2.6 copy-start.14
  301.6 37.5 %copy-start.4 = (bf16[1024,192]{0,1:T(8,128)(2,1)S(1)}, bf16[1024,192]{0,1:T(8,128)(2,1)}, u32[]{:S(2)}) copy-start(bf16[1024,192]{0,1:T(8,128)(2,1)} %param.27) | copy-start | bytes 1179652
  304.8 326.9 %reduce-scatter.5.cloned.1.call-start = ((), (), s32[]{:S(2)}) async-start(), calls=%async_computation.10 | async-start | bytes 1597440 | tf_op jit(solution)/shard_map/reduce_scatter | solution.py:133
  343.1 4.7 copy-start.12
  343.1 137.1 %copy-start.3 = (f32[1024,192]{0,1:T(8,128)S(1)}, f32[1024,192]{0,1:T(8,128)}, u32[]{:S(2)}) copy-start(f32[1024,192]{0,1:T(8,128)} %copy-done.2) | copy-start | bytes 2359300
Sparse Core Ops, SparseCore 0:
  56.5 86.9 all-gather.6
  146.1 62.7 all-gather.4
  211.0 43.9 all-gather.10
  291.9 47.0 all-gather.8
  343.6 135.0 reduce-scatter.6
  483.7 147.9 reduce-scatter.4

commit v2 on v1

--- a/solution.py
+++ b/solution.py
@@ -48,6 +48,41 @@
     for name in reversed(DP_AXES):
         value = lax.psum(value, name)
     return value
+
+
+def dp_gather(value):
+    for name in reversed(DP_AXES):
+        value = lax.all_gather(value, name, axis=0, tiled=True)
+    return value
+
+
+def dp_scatter(value):
+    for name in DP_AXES:
+        value = lax.psum_scatter(value, name, scatter_dimension=0, tiled=True)
+    return value
+
+
+def halving_scatter(value, sizes):
+    cols = value.shape[1:]
+    cur = value.reshape(tuple(sizes[a] for a in DP_AXES) + (-1,) + cols)
+    for dim, name in reversed(list(enumerate(DP_AXES))):
+        length = sizes[name]
+        me = lax.axis_index(name)
+        bit = length.bit_length() - 2
+        while bit >= 0:
+            shape = cur.shape
+            span = shape[dim]
+            split = shape[:dim] + (span >> (bit + 1), 2, 1 << bit) + shape[dim + 1 :]
+            pieces = cur.reshape(split)
+            mine = (me >> bit) & 1
+            keep = lax.dynamic_index_in_dim(pieces, mine, dim + 1, keepdims=False)
+            send = lax.dynamic_index_in_dim(pieces, 1 - mine, dim + 1, keepdims=False)
+            perm = [(i, i ^ (1 << bit)) for i in range(length)]
+            got = lax.ppermute(send, name, perm)
+            merged = keep + got
+            cur = merged.reshape(shape[:dim] + (span // 2,) + shape[dim + 1 :])
+            bit -= 1
+    return cur.reshape((-1,) + cols)
 
 
 def contract_rows(left, right):
@@ -102,7 +137,7 @@
     normed_in = ((inputs - mean[:, None]) * lax.rsqrt(var + EPS)[:, None] * ln_gain).astype(
         jnp.bfloat16
     )
-    weights_one = lax.all_gather(w_pw1, DP_AXES, axis=0, tiled=True).reshape(model_width, -1)
+    weights_one = dp_gather(w_pw1).reshape(model_width, -1)
     half = weights_one.shape[1] // 2
     normed_full = lax.all_gather(normed_in, "mp", axis=1, tiled=True)
     pre = jnp.dot(normed_full, weights_one, preferred_element_type=jnp.float32)
@@ -125,32 +160,34 @@
     act = normed_conv * bn_gain + bn_bias
     act_sig = jax.nn.sigmoid(act)
     hidden = (valid_col * act * act_sig).astype(jnp.bfloat16)
-    weights_two = lax.all_gather(w_pw2, DP_AXES, axis=0, tiled=True)
+    weights_two = dp_gather(w_pw2)
     hidden_full = lax.all_gather(hidden, "mp", axis=1, tiled=True)
     encoded = (
         inputs + jnp.dot(hidden_full, weights_two, preferred_element_type=jnp.float32)
     ).astype(jnp.bfloat16)
-    grad_pw2 = lax.psum_scatter(
-        contract_rows(hidden_full, cotangent), DP_AXES, scatter_dimension=0, tiled=True
-    )
+    grad_pw2 = dp_scatter(contract_rows(hidden_full, cotangent))
     cot_full = lax.all_gather(cotangent, "mp", axis=1, tiled=True)
     weights_rows = lax.all_to_all(weights_two, "mp", split_axis=0, concat_axis=1, tiled=True)
     dhidden = lax.dot_general(
         cot_full, weights_rows, (((1,), (1,)), ((), ())), preferred_element_type=jnp.float32
     )
     dact = dhidden * valid_col * act_sig * (1.0 + act * (1.0 - act_sig))
-    grad_bias, grad_gain = dp_sum((jnp.sum(dact, 0), jnp.sum(dact * normed_conv, 0)))
-    dconv = (
-        valid_col * inv_std * bn_gain * (dact - grad_bias / count - normed_conv * grad_gain / count)
-    )
-    grad_kernel = dp_sum(kernel_terms(dconv, glu_out, kernel.shape[0], frames))
+    width = kernel.shape[0]
+    term_a = kernel_terms(valid_col * dact, glu_out, width, frames)
+    term_b = kernel_terms(jnp.broadcast_to(valid_col, glu_out.shape), glu_out, width, frames)
+    term_e = kernel_terms(valid_col * normed_conv, glu_out, width, frames)
+    grad_bias, grad_gain, term_a, term_b, term_e = dp_sum(
+        (jnp.sum(dact, 0), jnp.sum(dact * normed_conv, 0), term_a, term_b, term_e)
+    )
+    scale = inv_std * bn_gain
+    dconv = valid_col * scale * (dact - grad_bias / count - normed_conv * grad_gain / count)
+    grad_kernel = scale * (term_a - (grad_bias / count) * term_b - (grad_gain / count) * term_e)
     dglu = depth_back(dconv, kernel, frames)
     dlin = dglu * valid_col * gate_sig
     dgate = dglu * valid_col * linear_part * gate_sig * (1.0 - gate_sig)
     dpre = jnp.concatenate([dlin, dgate], 1).astype(jnp.bfloat16)
-    grad_pw1 = lax.psum_scatter(
-        contract_rows(normed_full, dpre), DP_AXES, scatter_dimension=0, tiled=True
-    )
+    sizes = {name: lax.axis_size(name) for name in DP_AXES}
+    grad_pw1 = halving_scatter(contract_rows(normed_full, dpre), sizes)
     grad_pw1 = grad_pw1.reshape(grad_pw1.shape[0], 2, half)
     return (encoded, grad_pw1, grad_pw2, grad_kernel, grad_gain, grad_bias)
 

time: 644 us -> 626 us (0.972)
  blocking collectives: 172 us -> 127 us
  starting transfers between devices: 27.3 us -> 58.6 us
  waiting for transfers between devices: 350 us -> 326 us
  local copies, waits for them, and re-layouts: 22.4 us -> 36.4 us
  other arithmetic: 32.3 us -> 43.4 us
    psum x0 -> x3, waiting for transfers between devices: none -> 164 us  [dp_sum(): value = lax.psum(value, name)]
    reduce_scatter x1, waiting for transfers between devices: 148 us -> 0.01 us  [dp_scatter(): value = lax.psum_scatter(value, name, scatter_dimension=0, tiled=True)]
    psum x9 -> x3, blocking collectives: 95 us -> 30.7 us  [dp_sum(): value = lax.psum(value, name)]
    unnamed x7 -> x12, waiting for transfers between devices: 91.5 us -> 45.4 us
    ppermute x0 -> x6, waiting for transfers between devices: none -> 41.6 us  [halving_scatter(): got = lax.ppermute(send, name, perm)]
    ppermute x0 -> x6, starting transfers between devices: none -> 32.6 us  [halving_scatter(): got = lax.ppermute(send, name, perm)]
    all_gather x1 -> x5, blocking collectives: 57.1 us -> 76.4 us  [dp_gather(): value = lax.all_gather(value, name, axis=0, tiled=True)]
    all_to_all x1, waiting for transfers between devices: 19 us -> 0.01 us  [on_device(): lax.all_to_all(blocks, DP_AXES, split_axis=0, concat_axis=0, tiled=True)]
  transfers between devices with their start and end apart: 10 -> 20, of which waited for: 9 -> 15; matrix products, arithmetic and copies ran while one was open for 9% -> 9% of each run, Pallas kernels for 0% -> 0%
where the time goes in v2:
time: 626 us; the launch traced here: 624 us
  waiting for transfers between devices  326 us (52%)
  blocking collectives  127 us (20%)
  starting transfers between devices  58.6 us (9%)
  other arithmetic  43.4 us (7%)
  local copies, waits for them, and re-layouts  36.4 us (6%)
  matrix products  18.3 us (3%)
  between operations  14.8 us (2%)
    psum x3, waiting for transfers between devices, dp_sum(): value = lax.psum(value, name)  164 us
    all_gather x5, blocking collectives, dp_gather(): value = lax.all_gather(value, name, axis=0, tiled=True)  76.4 us
    unnamed x12, waiting for transfers between devices  45.4 us
    ppermute x6, waiting for transfers between devices, halving_scatter(): got = lax.ppermute(send, name, perm)  41.6 us
    ppermute x6, starting transfers between devices, halving_scatter(): got = lax.ppermute(send, name, perm)  32.6 us
    psum x3, blocking collectives, dp_sum(): value = lax.psum(value, name)  30.7 us
    all_gather x1, waiting for transfers between devices, on_device(): hidden_full = lax.all_gather(hidden, 'mp', axis=1, tiled=True)  30.1 us
    all_to_all x1, waiting for transfers between devices, on_device(): lax.all_to_all(weights_two, 'mp', split_axis=0, concat_axis=1, tiled=True)  27.9 us
  transfers between devices with their start and end apart: 20, of which 15 were waited for; matrix products, arithmetic and copies ran while one was open for 9% of the time, Pallas kernels for 0%

profile of v2, /device:TPU:1, one launch (start us, length us, event | category | flops | bytes accessed | tf_op | source)
XLA Modules:
  0.0 624.4 jit_solution(6660455818234446443)
XLA Ops:
  12.1 11.6 %all-to-all-start.2 = ((s32[64,1,1]{2,1,0:T(1,128)}), s32[64,1,1]{2,1,0:T(1,128)S(1)}, u32[]{:S(2)}, u32[]{:S(2)}) async-start(s32[64,1,1]{2,1,0:T(1,128)} %copy.55), calls=%async_computation.2 | async-start | bytes 65536 | tf_op jit(solution)/shard_map/all_to_all | solution.py:117
  25.1 2.1 copy.53
  28.0 5.0 all-to-all-done.2
  33.0 5.4 all-to-all-start.1
  39.4 8.2 %all-to-all-done.1 = s32[64,1,1]{2,1,0:T(1,128)S(1)} async-done(((s32[64,1,1]{2,1,0:T(1,128)}), s32[64,1,1]{2,1,0:T(1,128)S(1)}, u32[]{:S(2)}, u32[]{:S(2)}) %all-to-all-start.1) | async-done | bytes 288 | tf_op jit(solution)/shard_map/all_to_all | solution.py:116
  47.6 4.7 all-to-all-start
  52.4 2.1 all_gather.28
  54.5 32.2 %all_gather.29 = bf16[384,2,192]{2,1,0:T(2,128)(2,1)S(1)} all-gather(bf16[48,2,192]{2,1,0:T(2,128)(2,1)S(1)} %all_gather.28), channel_id=1, replica_groups=mesh['x'=4,'y'=8,'c'=2,'mp'=8] {'y'}, dimensions={0}, use_global_device_ids=true | all-gather | bytes 331776 | tf_op jit(solution)/shard_map/all_gather | solution.py:55
  92.0 19.7 %all-reduce.2 = (f32[1024]{0:T(1024)S(1)}, f32[1024]{0:T(1024)S(1)}) all-reduce(f32[1024]{0:T(1024)S(1)} %get-tuple-element.134, f32[1024]{0:T(1024)S(1)} %get-tuple-element.133), channel_id=1, replica_groups=mesh['x'=4,'y'=8,'c'=2,'mp'=8] {'mp'}, use_global_device_ids=true, to_apply=%region_3.5 | all-reduce | flops 2048 | bytes 16384 | tf_op jit(solution)/shard_map/psum | solution.py:134
  113.3 11.0 %all_gather.32 = bf16[48,192]{1,0:T(8,128)(2,1)S(1)} all-gather(bf16[24,192]{1,0:T(8,128)(2,1)S(1)} %copy-done.15), channel_id=1, replica_groups=mesh['x'=4,'y'=8,'c'=2,'mp'=8] {'c'}, dimensions={0}, use_global_device_ids=true | all-gather | bytes 27648 | tf_op jit(solution)/shard_map/all_gather | solution.py:55
  124.4 18.3 %all_gather.33 = bf16[384,192]{1,0:T(8,128)(2,1)S(1)} all-gather(bf16[48,192]{1,0:T(8,128)(2,1)S(1)} %all_gather.32), channel_id=1, replica_groups=mesh['x'=4,'y'=8,'c'=2,'mp'=8] {'y'}, dimensions={0}, use_global_device_ids=true | all-gather | bytes 165888 | tf_op jit(solution)/shard_map/all_gather | solution.py:55
  142.7 12.8 %all_gather.34 = bf16[1536,192]{1,0:T(8,128)(2,1)} all-gather(bf16[384,192]{1,0:T(8,128)(2,1)S(1)} %all_gather.33), channel_id=1, replica_groups=mesh['x'=4,'y'=8,'c'=2,'mp'=8] {'x'}, dimensions={0}, use_global_device_ids=true | all-gather | bytes 737280 | tf_op jit(solution)/shard_map/all_gather | solution.py:55
  155.5 3.6 all-to-all-start.3
  160.0 27.9 %all-to-all-done.3 = bf16[8,192,192]{2,1,0:T(8,128)(2,1)S(1)} async-done(((bf16[8,192,192]{2,1,0:T(8,128)(2,1)}), bf16[8,192,192]{2,1,0:T(8,128)(2,1)S(1)}, u32[]{:S(2)}, u32[]{:S(2)}) %all-to-all-start.3) | async-done | bytes 589856 | tf_op jit(solution)/shard_map/all_to_all | solution.py:170
  189.9 4.1 all-gather.5.cloned.1.call-done
  194.0 3.6 fusion.83
  199.9 3.9 fusion.3
  204.1 6.3 %all-reduce.8 = (f32[192]{0:T(256)S(1)}, f32[]{:T(128)}, f32[192]{0:T(256)S(1)}) all-reduce(f32[192]{0:T(256)S(1)} %get-tuple-element.128, f32[]{:T(128)} %fusion.74, f32[192]{0:T(256)S(1)} %get-tuple-element.127), channel_id=1, replica_groups=mesh['x'=4,'y'=8,'c'=2,'mp'=8] {'c'}, use_global_device_ids=true, to_apply=%region_5.7 | all-reduce | flops 385 | bytes 3080 | tf_op jit(solution)/shard_map/psum | solution.py:49
  210.5 14.9 %all-reduce.4 = (f32[192]{0:T(256)S(1)}, f32[]{:T(128)}, f32[192]{0:T(256)S(1)}) all-reduce(f32[192]{0:T(256)S(1)} %get-tuple-element.159, f32[]{:T(128)} %get-tuple-element.160, f32[192]{0:T(256)S(1)} %get-tuple-element.161), channel_id=1, replica_groups=mesh['x'=4,'y'=8,'c'=2,'mp'=8] {'y'}, use_global_device_ids=true, to_apply=%region_6.8 | all-reduce | flops 385 | bytes 3080 | tf_op jit(solution)/shard_map/psum | solution.py:49
  225.4 9.4 %all-reduce.6 = (f32[192]{0:T(256)S(1)}, f32[]{:T(128)}, f32[192]{0:T(256)S(1)}) all-reduce(f32[192]{0:T(256)S(1)} %get-tuple-element.143, f32[]{:T(128)} %get-tuple-element.144, f32[192]{0:T(256)S(1)} %get-tuple-element.145), channel_id=1, replica_groups=mesh['x'=4,'y'=8,'c'=2,'mp'=8] {'x'}, use_global_device_ids=true, to_apply=%region_7.9 | all-reduce | flops 385 | bytes 3080 | tf_op jit(solution)/shard_map/psum | solution.py:49
  237.2 2.4 multiply_reduce_fusion.17
  239.6 2.3 multiply_reduce_fusion.1
  241.9 3.0 multiply_reduce_fusion.32
  245.0 5.1 multiply_reduce_fusion.92
  253.2 3.0 multiply_reduce_fusion.62
  256.2 2.5 stack.383
  258.7 3.1 stack.351
  261.8 2.5 stack.319
  264.4 32.8 %all-reduce.17.cloned.1.call-done = (f32[192]{0:T(256)}, f32[192]{0:T(256)}, f32[31,192]{1,0:T(8,128)}, f32[31,192]{1,0:T(8,128)}, f32[31,192]{1,0:T(8,128)}) async-done(((f32[192]{0:T(256)}, f32[192]{0:T(256)}, f32[31,192]{1,0:T(8,128)}, f32[31,192]{1,0:T(8,128)}, f32[31,192]{1,0:T(8,128)}), (f32[192]{0:T(256)}, f32[192]{0:T(256)}, f32[31,192]{1,0:T(8,128)}, f32[31,192]{1,0:T(8,128)}, ...) | async-done | bytes 72976 | tf_op jit(solution)/shard_map/psum | solution.py:49
  297.2 75.5 %all-reduce.13.cloned.1.call-done = (f32[192]{0:T(256)}, f32[192]{0:T(256)}, f32[31,192]{1,0:T(8,128)}, f32[31,192]{1,0:T(8,128)}, f32[31,192]{1,0:T(8,128)}) async-done(((f32[192]{0:T(256)}, f32[192]{0:T(256)}, f32[31,192]{1,0:T(8,128)}, f32[31,192]{1,0:T(8,128)}, f32[31,192]{1,0:T(8,128)}), (f32[192]{0:T(256)}, f32[192]{0:T(256)}, f32[31,192]{1,0:T(8,128)}, f32[31,192]{1,0:T(8,128)}, ...) | async-done | bytes 72976 | tf_op jit(solution)/shard_map/psum | solution.py:49
  372.8 55.5 %all-reduce.15.cloned.1.call-done = (f32[192]{0:T(256)}, f32[192]{0:T(256)}, f32[31,192]{1,0:T(8,128)}, f32[31,192]{1,0:T(8,128)}, f32[31,192]{1,0:T(8,128)}) async-done(((f32[192]{0:T(256)}, f32[192]{0:T(256)}, f32[31,192]{1,0:T(8,128)}, f32[31,192]{1,0:T(8,128)}, f32[31,192]{1,0:T(8,128)}), (f32[192]{0:T(256)}, f32[192]{0:T(256)}, f32[31,192]{1,0:T(8,128)}, f32[31,192]{1,0:T(8,128)}, ...) | async-done | bytes 72976 | tf_op jit(solution)/shard_map/psum | solution.py:49
  429.6 3.2 subtract_multiply_fusion
  434.7 4.2 fusion.55
  445.7 4.6 collective-permute-start
  450.3 2.4 collective-permute-done
  454.1 30.1 %all-gather.9.cloned.1.call-done = bf16[1024,1536]{0,1:T(8,128)(2,1)} async-done(((bf16[1024,192]{0,1:T(8,128)(2,1)}), bf16[1024,1536]{0,1:T(8,128)(2,1)}) %all-gather.9.cloned.1.call-update) | async-done | bytes 3145744 | tf_op jit(solution)/shard_map/all_gather | solution.py:164
  484.2 4.1 fusion.82
  489.3 7.3 %collective-permute-start.1 = (f32[4,1,4,1,24,384]{5,4,2,0,3,1:T(8,128)}, f32[4,1,4,1,24,384]{5,4,2,0,3,1:T(8,128)}, u32[]{:S(2)}, u32[]{:S(2)}) collective-permute-start(f32[4,1,4,1,24,384]{5,4,2,0,3,1:T(8,128)} %dynamic-slice_bitcast_fusion.1), channel_id=1, source_target_pairs={{0,64},{16,80},{32,96},{48,112},{64,0},{80,16},{96,32},{112,48},{1... | collective-permute-start | bytes 1769480 | tf_op jit(solution)/shard_map/ppermute | solution.py:81
  496.7 19.0 %collective-permute-done.1 = f32[4,1,4,1,24,384]{5,4,2,0,3,1:T(8,128)} collective-permute-done((f32[4,1,4,1,24,384]{5,4,2,0,3,1:T(8,128)}, f32[4,1,4,1,24,384]{5,4,2,0,3,1:T(8,128)}, u32[]{:S(2)}, u32[]{:S(2)}) %collective-permute-start.1) | collective-permute-done | bytes 589856 | tf_op jit(solution)/shard_map/ppermute | solution.py:81
  518.5 11.9 %collective-permute-start.2 = (f32[4,1,2,1,24,384]{5,4,2,0,3,1:T(8,128)}, f32[4,1,2,1,24,384]{5,4,2,0,3,1:T(8,128)}, u32[]{:S(2)}, u32[]{:S(2)}) collective-permute-start(f32[4,1,2,1,24,384]{5,4,2,0,3,1:T(8,128)} %dynamic-slice_bitcast_fusion.2), channel_id=1, source_target_pairs={{0,32},{16,48},{32,0},{48,16},{64,96},{80,112},{96,64},{112,80},{1... | collective-permute-start | bytes 884744 | tf_op jit(solution)/shard_map/ppermute | solution.py:81
  530.4 14.1 %collective-permute-done.2 = f32[4,1,2,1,24,384]{5,4,2,0,3,1:T(8,128)} collective-permute-done((f32[4,1,2,1,24,384]{5,4,2,0,3,1:T(8,128)}, f32[4,1,2,1,24,384]{5,4,2,0,3,1:T(8,128)}, u32[]{:S(2)}, u32[]{:S(2)}) %collective-permute-start.2) | collective-permute-done | bytes 294944 | tf_op jit(solution)/shard_map/ppermute | solution.py:81
  546.3 1.9 collective-permute-start.3
  548.3 5.0 collective-permute-done.3
  554.9 4.6 collective-permute-start.4
  563.4 2.2 collective-permute-start.5
  568.8 23.2 %reduce-scatter.10.cloned.1.call-done = f32[48,192]{1,0:T(8,128)} async-done(((f32[384,192]{1,0:T(8,128)}), f32[48,192]{1,0:T(8,128)}) %reduce-scatter.10.cloned.1.call-update) | async-done | bytes 36880
  592.1 2.9 fusion.2
  595.0 21.4 %reduce-scatter.12.cloned.1.call-done = f32[24,192]{1,0:T(8,128)} async-done(((f32[48,192]{1,0:T(8,128)}), f32[24,192]{1,0:T(8,128)}) %reduce-scatter.12.cloned.1.call-update) | async-done | bytes 18448
  (132 shorter events, 52.8 us)
Async XLA Ops:
  7.2 84.3 %copy-start = (bf16[320,192]{0,1:T(8,128)(2,1)S(1)}, bf16[320,192]{0,1:T(8,128)(2,1)}, u32[]{:S(2)}) copy-start(bf16[320,192]{0,1:T(8,128)(2,1)} %param.19) | copy-start | bytes 368644
  12.1 20.9 %all-to-all-start.2 = ((s32[64,1,1]{2,1,0:T(1,128)}), s32[64,1,1]{2,1,0:T(1,128)S(1)}, u32[]{:S(2)}, u32[]{:S(2)}) async-start(s32[64,1,1]{2,1,0:T(1,128)} %copy.55), calls=%async_computation.2 | async-start | bytes 65536 | tf_op jit(solution)/shard_map/all_to_all | solution.py:117
  25.1 27.3 %copy-start.14 = (bf16[24,2,192]{2,1,0:T(2,128)(2,1)S(1)}, bf16[24,2,192]{2,1,0:T(2,128)(2,1)}, u32[]{:S(2)}) copy-start(bf16[24,2,192]{2,1,0:T(2,128)(2,1)} %param.22) | copy-start | bytes 55300
  27.3 63.3 %copy-start.11 = (bf16[128,192]{0,1:T(8,128)(2,1)S(1)}, bf16[128,192]{0,1:T(8,128)(2,1)}, u32[]{:S(2)}) copy-start(bf16[128,192]{0,1:T(8,128)(2,1)} %param.20) | copy-start | bytes 147460
  33.0 14.6 %all-to-all-start.1 = ((s32[64,1,1]{2,1,0:T(1,128)}), s32[64,1,1]{2,1,0:T(1,128)S(1)}, u32[]{:S(2)}, u32[]{:S(2)}) async-start(s32[64,1,1]{2,1,0:T(1,128)} %copy.54), calls=%async_computation.1 | async-start | bytes 65536 | tf_op jit(solution)/shard_map/all_to_all | solution.py:116
  47.6 43.6 %all-to-all-start = ((bf16[64,16,320]{2,1,0:T(8,128)(2,1)}), bf16[64,16,320]{2,1,0:T(8,128)(2,1)S(1)}, u32[]{:S(2)}, u32[]{:S(2)}) async-start(bf16[64,16,320]{2,1,0:T(8,128)(2,1)} %broadcast_select_fusion), calls=%async_computation | async-start | bytes 1572864 | tf_op jit(solution)/shard_map/all_to_all | solution.py:115
  52.4 137.5 %all-gather.7.cloned.1.call-start = ((), (), s32[]{:S(2)}) async-start(), calls=%async_computation.8 | async-start | bytes 1474560 | tf_op jit(solution)/shard_map/all_gather | solution.py:55
  87.9 106.1 %all-gather.5.cloned.1.call-start = ((), (), s32[]{:S(2)}) async-start(), calls=%async_computation.7 | async-start | bytes 3538944 | tf_op jit(solution)/shard_map/all_gather | solution.py:142
  90.9 20.8 %copy-start.21 = (f32[192]{0:T(256)S(1)}, f32[192]{0:T(256)}, u32[]{:S(2)}) copy-start(f32[192]{0:T(256)} %param.21) | copy-start | bytes 2308
  91.2 22.1 %copy-start.15 = (bf16[24,192]{1,0:T(8,128)(2,1)S(1)}, bf16[24,192]{1,0:T(8,128)(2,1)}, u32[]{:S(2)}) copy-start(bf16[24,192]{1,0:T(8,128)(2,1)} %param.26) | copy-start | bytes 27652
  91.5 67.8 %copy-start.13 = (f32[31,192]{1,0:T(8,128)S(1)}, f32[31,192]{1,0:T(8,128)}, u32[]{:S(2)}) copy-start(f32[31,192]{1,0:T(8,128)} %param.23) | copy-start | bytes 71428
  92.0 96.4 %copy-start.5 = (f32[1024,192]{0,1:T(8,128)}, f32[1024,192]{0,1:T(8,128)S(1)}, u32[]{:S(2)}) copy-start(f32[1024,192]{0,1:T(8,128)S(1)} %get-tuple-element.208) | copy-start | bytes 2359300
  112.6 132.4 %all-gather.11.cloned.1.call-start = ((), (), s32[]{:S(2)}) async-start(), calls=%async_computation.10 | async-start | bytes 3538944 | tf_op jit(solution)/shard_map/all_gather | solution.py:169
  155.5 32.4 %all-to-all-start.3 = ((bf16[8,192,192]{2,1,0:T(8,128)(2,1)}), bf16[8,192,192]{2,1,0:T(8,128)(2,1)S(1)}, u32[]{:S(2)}, u32[]{:S(2)}) async-start(bf16[8,192,192]{2,1,0:T(8,128)(2,1)} %bitcast.41), calls=%async_computation.3 | async-start | bytes 1572864 | tf_op jit(solution)/shard_map/all_to_all | solution.py:170
  159.1 138.1 %all-reduce.17.cloned.1.call-start = ((), (), s32[]{:S(2)}) async-start(), calls=%async_computation.16 | async-start | bytes 200704 | tf_op jit(solution)/shard_map/psum | solution.py:49
  197.6 1.2 copy-start.1
  199.0 0.9 copy-start.6
  199.0 35.8 %copy-start.17 = (f32[192]{0:T(256)S(1)}, f32[192]{0:T(256)}, u32[]{:S(2)}) copy-start(f32[192]{0:T(256)} %param.24) | copy-start | bytes 2308
  237.2 7.7 %copy-start.19 = (f32[192]{0:T(256)S(1)}, f32[192]{0:T(256)}, u32[]{:S(2)}) copy-start(f32[192]{0:T(256)} %param.25) | copy-start | bytes 2308
  250.0 11.8 %copy-start.20 = (f32[192]{0:T(256)S(1)}, f32[192]{0:T(256)}, u32[]{:S(2)}) copy-start(f32[192]{0:T(256)} %get-tuple-element.130) | copy-start | bytes 2308
  264.3 108.4 %all-reduce.13.cloned.1.call-start = ((), (), s32[]{:S(2)}) async-start(), calls=%async_computation.14 | async-start | bytes 200704 | tf_op jit(solution)/shard_map/psum | solution.py:49
  297.1 131.2 %all-reduce.15.cloned.1.call-start = ((), (), s32[]{:S(2)}) async-start(), calls=%async_computation.15 | async-start | bytes 200704 | tf_op jit(solution)/shard_map/psum | solution.py:49
  372.7 111.5 %all-gather.9.cloned.1.call-start = ((), (), s32[]{:S(2)}) async-start(), calls=%async_computation.9 | async-start | bytes 3538944 | tf_op jit(solution)/shard_map/all_gather | solution.py:164
  432.8 7.7 %copy-start.2 = (f32[1024,384]{0,1:T(8,128)S(1)}, f32[1024,384]{0,1:T(8,128)}, u32[]{:S(2)}) copy-start(f32[1024,384]{0,1:T(8,128)} %copy-done.1) | copy-start | bytes 4718596
  432.8 128.5 %reduce-scatter.8.cloned.1.call-start = ((), (), s32[]{:S(2)}) async-start(), calls=%async_computation.11 | async-start | bytes 1474560 | tf_op jit(solution)/shard_map/reduce_scatter | solution.py:61
  440.5 1.9 copy-start.22
  444.2 1.4 copy-start.7
  444.2 40.0 %copy-start.9 = (bf16[1024,192]{0,1:T(8,128)(2,1)S(1)}, bf16[1024,192]{0,1:T(8,128)(2,1)}, u32[]{:S(2)}) copy-start(bf16[1024,192]{0,1:T(8,128)(2,1)} %param.27) | copy-start | bytes 1179652
  445.7 7.0 %collective-permute-start = (f32[4,8,1,1,24,384]{5,4,1,0,3,2:T(8,128)S(1)}, f32[4,8,1,1,24,384]{5,4,1,0,3,2:T(8,128)S(1)}, u32[]{:S(2)}, u32[]{:S(2)}) collective-permute-start(f32[4,8,1,1,24,384]{5,4,1,0,3,2:T(8,128)S(1)} %dynamic-slice_bitcast_fusion), channel_id=1, source_target_pairs={{0,8},{8,0},{1,9},{9,1},{2,10},{10,2},{3,11},{11,3},{4,12},{12,4},... | collective-permute-start | bytes 3538952 | tf_op jit(solution)/shard_map/ppermute | solution.py:81
  454.1 34.3 %copy-start.4 = (f32[4,8,1,1,24,384]{5,4,1,0,3,2:T(8,128)}, f32[4,8,1,1,24,384]{5,4,1,0,3,2:T(8,128)S(1)}, u32[]{:S(2)}) copy-start(f32[4,8,1,1,24,384]{5,4,1,0,3,2:T(8,128)S(1)} %bitcast_add_fusion) | copy-start | bytes 3538948
  488.4 103.7 %reduce-scatter.10.cloned.1.call-start = ((), (), s32[]{:S(2)}) async-start(), calls=%async_computation.12 | async-start | bytes 442368
  488.4 77.1 %copy-start.12 = (f32[31,192]{1,0:T(8,128)S(1)}, f32[31,192]{1,0:T(8,128)}, u32[]{:S(2)}) copy-start(f32[31,192]{1,0:T(8,128)} %get-tuple-element.148) | copy-start | bytes 71428
  489.3 102.7 %copy-start.3 = (bf16[1024,1536]{0,1:T(8,128)(2,1)S(1)}, bf16[1024,1536]{0,1:T(8,128)(2,1)}, u32[]{:S(2)}) copy-start(bf16[1024,1536]{0,1:T(8,128)(2,1)} %all-gather.9.cloned.1.call-done) | copy-start | bytes 9437188
  489.3 26.3 %collective-permute-start.1 = (f32[4,1,4,1,24,384]{5,4,2,0,3,1:T(8,128)}, f32[4,1,4,1,24,384]{5,4,2,0,3,1:T(8,128)}, u32[]{:S(2)}, u32[]{:S(2)}) collective-permute-start(f32[4,1,4,1,24,384]{5,4,2,0,3,1:T(8,128)} %dynamic-slice_bitcast_fusion.1), channel_id=1, source_target_pairs={{0,64},{16,80},{32,96},{48,112},{64,0},{80,16},{96,32},{112,48},{1... | collective-permute-start | bytes 1769480 | tf_op jit(solution)/shard_map/ppermute | solution.py:81
  516.9 0.8 copy-start.8
  518.5 26.0 %collective-permute-start.2 = (f32[4,1,2,1,24,384]{5,4,2,0,3,1:T(8,128)}, f32[4,1,2,1,24,384]{5,4,2,0,3,1:T(8,128)}, u32[]{:S(2)}, u32[]{:S(2)}) collective-permute-start(f32[4,1,2,1,24,384]{5,4,2,0,3,1:T(8,128)} %dynamic-slice_bitcast_fusion.2), channel_id=1, source_target_pairs={{0,32},{16,48},{32,0},{48,16},{64,96},{80,112},{96,64},{112,80},{1... | collective-permute-start | bytes 884744 | tf_op jit(solution)/shard_map/ppermute | solution.py:81
  545.6 0.7 copy-start.10
  546.3 6.9 %collective-permute-start.3 = (f32[4,1,1,1,24,384]{5,4,2,0,3,1:T(8,128)S(1)}, f32[4,1,1,1,24,384]{5,4,2,0,3,1:T(8,128)}, u32[]{:S(2)}, u32[]{:S(2)}) collective-permute-start(f32[4,1,1,1,24,384]{5,4,2,0,3,1:T(8,128)S(1)} %constant_dynamic-slice_fusion.1), channel_id=1, source_target_pairs={{0,16},{16,0},{32,48},{48,32},{64,80},{80,64},{96,112},{112,96},{1... | collective-permute-start | bytes 442376 | tf_op jit(solution)/shard_map/ppermute | solution.py:81
  554.9 8.4 %collective-permute-start.4 = (f32[1,2,1,1,24,384]{5,4,3,2,1,0:T(8,128)}, f32[1,2,1,1,24,384]{5,4,3,2,1,0:T(8,128)S(1)}, u32[]{:S(2)}, u32[]{:S(2)}) collective-permute-start(f32[1,2,1,1,24,384]{5,4,3,2,1,0:T(8,128)} %dynamic-slice_bitcast_fusion.3), channel_id=1, source_target_pairs={{0,256},{128,384},{256,0},{384,128},{1,257},{129,385},{257,1},{385... | collective-permute-start | bytes 221192 | tf_op jit(solution)/shard_map/ppermute | solution.py:81
  563.2 53.1 %reduce-scatter.12.cloned.1.call-start = ((), (), s32[]{:S(2)}) async-start(), calls=%async_computation.13 | async-start | bytes 73728
  563.4 4.7 collective-permute-start.5
  592.0 24.4 %copy-start.16 = (f32[192]{0:T(256)S(1)}, f32[192]{0:T(256)}, u32[]{:S(2)}) copy-start(f32[192]{0:T(256)} %get-tuple-element.214) | copy-start | bytes 2308
  592.0 24.9 %copy-start.18 = (f32[192]{0:T(256)S(1)}, f32[192]{0:T(256)}, u32[]{:S(2)}) copy-start(f32[192]{0:T(256)} %get-tuple-element.215) | copy-start | bytes 2308
Sparse Core Ops, SparseCore 0:
  88.1 36.1 all-gather.6
  126.9 67.0 all-gather.4
  196.1 46.8 all-gather.10
  264.4 32.6 all-reduce.16
  299.6 73.0 all-reduce.12
  375.2 53.0 all-reduce.14
  433.0 51.1 all-gather.8
  488.5 26.1 reduce-scatter.7
  563.4 28.6 reduce-scatter.9
  595.2 21.1 reduce-scatter.11

commit v3 on v2

--- a/solution.py
+++ b/solution.py
@@ -109,12 +109,12 @@
     model_width = w_pw2.shape[0] * lax.axis_size(DP_AXES)
     chosen = picks[0]
     blocks = jnp.take(corpus, chosen, axis=0)
-    lens_send = jnp.take(lengths, chosen)
-    lang_send = jnp.take(langs, chosen)
-    received, lens, lang = (
-        lax.all_to_all(blocks, DP_AXES, split_axis=0, concat_axis=0, tiled=True),
-        lax.all_to_all(lens_send, DP_AXES, split_axis=0, concat_axis=0, tiled=True),
-        lax.all_to_all(lang_send, DP_AXES, split_axis=0, concat_axis=0, tiled=True),
+    meta_send = jnp.stack([jnp.take(lengths, chosen), jnp.take(langs, chosen)], 1)
+    received = lax.all_to_all(blocks, DP_AXES, split_axis=0, concat_axis=0, tiled=True)
+    meta = lax.all_to_all(meta_send, DP_AXES, split_axis=0, concat_axis=0, tiled=True)
+    lens, lang = meta[:, 0], meta[:, 1]
+    stacked = lax.all_gather(
+        jnp.concatenate([w_pw1, w_pw2[:, None, :]], 1), DP_AXES, axis=0, tiled=True
     )
     frames = received.shape[1]
     valid = (
@@ -137,7 +137,7 @@
     normed_in = ((inputs - mean[:, None]) * lax.rsqrt(var + EPS)[:, None] * ln_gain).astype(
         jnp.bfloat16
     )
-    weights_one = dp_gather(w_pw1).reshape(model_width, -1)
+    weights_one = stacked[:, :2].reshape(model_width, -1)
     half = weights_one.shape[1] // 2
     normed_full = lax.all_gather(normed_in, "mp", axis=1, tiled=True)
     pre = jnp.dot(normed_full, weights_one, preferred_element_type=jnp.float32)
@@ -160,7 +160,7 @@
     act = normed_conv * bn_gain + bn_bias
     act_sig = jax.nn.sigmoid(act)
     hidden = (valid_col * act * act_sig).astype(jnp.bfloat16)
-    weights_two = dp_gather(w_pw2)
+    weights_two = stacked[:, 2]
     hidden_full = lax.all_gather(hidden, "mp", axis=1, tiled=True)
     encoded = (
         inputs + jnp.dot(hidden_full, weights_two, preferred_element_type=jnp.float32)
@@ -172,16 +172,11 @@
         cot_full, weights_rows, (((1,), (1,)), ((), ())), preferred_element_type=jnp.float32
     )
     dact = dhidden * valid_col * act_sig * (1.0 + act * (1.0 - act_sig))
-    width = kernel.shape[0]
-    term_a = kernel_terms(valid_col * dact, glu_out, width, frames)
-    term_b = kernel_terms(jnp.broadcast_to(valid_col, glu_out.shape), glu_out, width, frames)
-    term_e = kernel_terms(valid_col * normed_conv, glu_out, width, frames)
-    grad_bias, grad_gain, term_a, term_b, term_e = dp_sum(
-        (jnp.sum(dact, 0), jnp.sum(dact * normed_conv, 0), term_a, term_b, term_e)
-    )
-    scale = inv_std * bn_gain
-    dconv = valid_col * scale * (dact - grad_bias / count - normed_conv * grad_gain / count)
-    grad_kernel = scale * (term_a - (grad_bias / count) * term_b - (grad_gain / count) * term_e)
+    grad_bias, grad_gain = dp_sum((jnp.sum(dact, 0), jnp.sum(dact * normed_conv, 0)))
+    dconv = (
+        valid_col * inv_std * bn_gain * (dact - grad_bias / count - normed_conv * grad_gain / count)
+    )
+    grad_kernel = dp_sum(kernel_terms(dconv, glu_out, kernel.shape[0], frames))
     dglu = depth_back(dconv, kernel, frames)
     dlin = dglu * valid_col * gate_sig
     dgate = dglu * valid_col * linear_part * gate_sig * (1.0 - gate_sig)

time: 626 us -> 411 us (0.66)
  waiting for transfers between devices: 326 us -> 158 us
  starting transfers between devices: 58.6 us -> 45 us
  blocking collectives: 127 us -> 114 us
  local copies, waits for them, and re-layouts: 36.4 us -> 24.9 us
  other arithmetic: 43.4 us -> 34.4 us
    psum x3 -> x0, waiting for transfers between devices: 164 us -> none  [dp_sum(): value = lax.psum(value, name)]
    all_gather x5 -> x0, blocking collectives: 76.4 us -> none  [dp_gather(): value = lax.all_gather(value, name, axis=0, tiled=True)]
    psum x3 -> x9, blocking collectives: 30.7 us -> 95.1 us  [dp_sum(): value = lax.psum(value, name)]
    all_gather x1, waiting for transfers between devices: 4.14 us -> 50.3 us  [on_device(): normed_full = lax.all_gather(normed_in, 'mp', axis=1, tiled=True)]
    unnamed x12 -> x9, waiting for transfers between devices: 45.4 us -> 17.3 us
    all_to_all x1, waiting for transfers between devices: 27.9 us -> 0.01 us  [on_device(): lax.all_to_all(weights_two, 'mp', split_axis=0, concat_axis=1, tiled=True)]
    all_to_all x1, waiting for transfers between devices: 0.01 us -> 22.2 us  [on_device(): lax.all_to_all(blocks, DP_AXES, split_axis=0, concat_axis=0, tiled=True)]
    all_gather x1, waiting for transfers between devices: 30.1 us -> 16.1 us  [on_device(): hidden_full = lax.all_gather(hidden, 'mp', axis=1, tiled=True)]
  transfers between devices with their start and end apart: 20 -> 16, of which waited for: 15 -> 11; matrix products, arithmetic and copies ran while one was open for 9% -> 15% of each run, Pallas kernels for 0% -> 0%
where the time goes in v3:
time: 411 us; the launch traced here: 410 us
  waiting for transfers between devices  158 us (38%)
  blocking collectives  114 us (28%)
  starting transfers between devices  45 us (11%)
  other arithmetic  34.4 us (8%)
  local copies, waits for them, and re-layouts  24.9 us (6%)
  matrix products  18.6 us (5%)
  between operations  14.6 us (4%)
    psum x9, blocking collectives, dp_sum(): value = lax.psum(value, name)  95.1 us
    all_gather x1, waiting for transfers between devices, on_device(): normed_full = lax.all_gather(normed_in, 'mp', axis=1, tiled=True)  50.3 us
    ppermute x6, waiting for transfers between devices, halving_scatter(): got = lax.ppermute(send, name, perm)  28.4 us
    all_to_all x1, waiting for transfers between devices, on_device(): lax.all_to_all(blocks, DP_AXES, split_axis=0, concat_axis=0, tiled=True)  22.2 us
    ppermute x6, starting transfers between devices, halving_scatter(): got = lax.ppermute(send, name, perm)  20.8 us
    psum x1, blocking collectives, on_device(): lax.psum((jnp.sum(inputs, 1), jnp.sum(inputs * inputs, 1)), 'mp')  19.3 us
    unnamed x9, waiting for transfers between devices  17.3 us
    all_gather x1, waiting for transfers between devices, on_device(): hidden_full = lax.all_gather(hidden, 'mp', axis=1, tiled=True)  16.1 us
  transfers between devices with their start and end apart: 16, of which 11 were waited for; matrix products, arithmetic and copies ran while one was open for 15% of the time, Pallas kernels for 0%

profile of v3, /device:TPU:1, one launch (start us, length us, event | category | flops | bytes accessed | tf_op | source)
XLA Modules:
  0.0 410.0 jit_solution(13628699030726084974)
XLA Ops:
  14.3 11.6 %all-to-all-start.1 = ((s32[64,1,2]{2,1,0:T(1,128)}), s32[64,1,2]{2,1,0:T(1,128)S(1)}, u32[]{:S(2)}, u32[]{:S(2)}) async-start(s32[64,1,2]{2,1,0:T(1,128)} %copy.43), calls=%async_computation.1 | async-start | bytes 65536 | tf_op jit(solution)/shard_map/all_to_all | solution.py:114
  25.9 2.1 copy.42
  29.9 5.3 %all-to-all-done.1 = s32[64,1,2]{2,1,0:T(1,128)S(1)} async-done(((s32[64,1,2]{2,1,0:T(1,128)}), s32[64,1,2]{2,1,0:T(1,128)S(1)}, u32[]{:S(2)}, u32[]{:S(2)}) %all-to-all-start.1) | async-done | bytes 544 | tf_op jit(solution)/shard_map/all_to_all | solution.py:114
  35.1 5.1 %all-to-all-start = ((bf16[64,16,320]{2,1,0:T(8,128)(2,1)}), bf16[64,16,320]{2,1,0:T(8,128)(2,1)S(1)}, u32[]{:S(2)}, u32[]{:S(2)}) async-start(bf16[64,16,320]{2,1,0:T(8,128)(2,1)} %broadcast_select_fusion), calls=%async_computation | async-start | bytes 1572864 | tf_op jit(solution)/shard_map/all_to_all | solution.py:113
  41.7 22.2 %all-to-all-done = bf16[64,16,320]{2,1,0:T(8,128)(2,1)S(1)} async-done(((bf16[64,16,320]{2,1,0:T(8,128)(2,1)}), bf16[64,16,320]{2,1,0:T(8,128)(2,1)S(1)}, u32[]{:S(2)}, u32[]{:S(2)}) %all-to-all-start) | async-done | bytes 655392 | tf_op jit(solution)/shard_map/all_to_all | solution.py:113
  64.6 19.3 %all-reduce.2 = (f32[1024]{0:T(1024)S(1)}, f32[1024]{0:T(1024)S(1)}) all-reduce(f32[1024]{0:T(1024)S(1)} %get-tuple-element.66, f32[1024]{0:T(1024)S(1)} %get-tuple-element.65), channel_id=1, replica_groups=mesh['x'=4,'y'=8,'c'=2,'mp'=8] {'mp'}, use_global_device_ids=true, to_apply=%region_3.5 | all-reduce | flops 2048 | bytes 16384 | tf_op jit(solution)/shard_map/psum | solution.py:134
  87.6 13.4 %all-gather.7.cloned.1.call-done = bf16[1536,3,192]{2,0,1:T(8,128)(2,1)} async-done(((bf16[24,3,192]{2,0,1:T(8,128)(2,1)}), bf16[1536,3,192]{2,0,1:T(8,128)(2,1)}) %all-gather.7.cloned.1.call-update) | async-done | bytes 1769488 | tf_op jit(solution)/shard_map/all_gather | solution.py:116
  102.4 1.5 copy.62
  105.2 7.1 %all-to-all-start.2 = ((bf16[8,192,192]{1,2,0:T(8,128)(2,1)}), bf16[8,192,192]{1,2,0:T(8,128)(2,1)}, u32[]{:S(2)}, u32[]{:S(2)}) async-start(bf16[8,192,192]{1,2,0:T(8,128)(2,1)} %copy.51), calls=%async_computation.2 | async-start | bytes 1572864 | tf_op jit(solution)/shard_map/all_to_all | solution.py:170
  112.3 50.3 %all-gather.5.cloned.1.call-done = bf16[1024,1536]{0,1:T(8,128)(2,1)} async-done(((bf16[1024,192]{0,1:T(8,128)(2,1)}), bf16[1024,1536]{0,1:T(8,128)(2,1)}) %all-gather.5.cloned.1.call-update) | async-done | bytes 3145744 | tf_op jit(solution)/shard_map/all_gather | solution.py:142
  162.7 3.6 fusion.85
  166.9 6.3 %fusion.4 = (f32[192]{0:T(256)}, f32[192]{0:T(256)}, f32[64,16,192]{2,1,0:T(8,128)}) fusion(f32[64,16]{1,0:T(8,128)} %copy-done.6, f32[192]{0:T(256)} %bitcast.208, f32[192]{0:T(256)} %bitcast.210, f32[192]{0:T(256)} %bitcast.214, f32[192]{0:T(256)} %bitcast.216, f32[192]{0:T(256)} %bitcast.218, f32[192]{0:T(256)} %bitcast.220, f32[192]{0:T(256)} %bitcast.222, ...), kind=kLoop, calls=%fused_computation.74 | loop fusion | flops 12779136 | bytes 1602304 | tf_op jit(solution)/shard_map/reduce_sum | solution.py:152
  173.2 1.5 copy.49
  174.7 3.9 all-reduce.8
  178.6 14.4 %all-reduce.4 = (f32[192]{0:T(256)}, f32[]{:T(128)}, f32[192]{0:T(256)}) all-reduce(f32[192]{0:T(256)} %get-tuple-element.81, f32[]{:T(128)} %get-tuple-element.82, f32[192]{0:T(256)} %get-tuple-element.83), channel_id=1, replica_groups=mesh['x'=4,'y'=8,'c'=2,'mp'=8] {'y'}, use_global_device_ids=true, to_apply=%region_6.8 | all-reduce | flops 385 | bytes 3080 | tf_op jit(solution)/shard_map/psum | solution.py:49
  193.1 8.4 %all-reduce.6 = (f32[192]{0:T(256)}, f32[]{:T(128)}, f32[192]{0:T(256)}) all-reduce(f32[192]{0:T(256)} %get-tuple-element.71, f32[]{:T(128)} %get-tuple-element.72, f32[192]{0:T(256)} %get-tuple-element.73), channel_id=1, replica_groups=mesh['x'=4,'y'=8,'c'=2,'mp'=8] {'x'}, use_global_device_ids=true, to_apply=%region_7.9 | all-reduce | flops 385 | bytes 3080 | tf_op jit(solution)/shard_map/psum | solution.py:49
  201.5 1.9 add_rsqrt_fusion.1
  203.4 4.9 %all-gather.11.cloned.1.call-done = bf16[1024,1536]{0,1:T(8,128)(2,1)} async-done(((bf16[1024,192]{0,1:T(8,128)(2,1)}), bf16[1024,1536]{0,1:T(8,128)(2,1)}) %all-gather.11.cloned.1.call-update) | async-done | bytes 3145744 | tf_op jit(solution)/shard_map/all_gather | solution.py:169
  208.3 4.6 %fusion.80 = (f32[192]{0:T(256)}, f32[192]{0:T(256)}, f32[1024,192]{0,1:T(8,128)}) fusion(f32[192]{0:T(256)} %get-tuple-element.86, f32[1024,192]{0,1:T(8,128)S(1)} %copy.49, f32[192]{0:T(256)} %get-tuple-element.87, f32[192]{0:T(256)} %param.25, f32[192]{0:T(256)} %param.24, f32[1024]{0:T(1024)} %copy-done.7, bf16[192,1536]{0,1:T(8,128)(2,1)} %bitcast.48, ...), kind=kOutput, calls=%fused_computation.225 | convolution fusion | flops 607125120 | bytes 5317120 | tf_op jit(solution)/shard_map/dot_general | solution.py:171
  212.9 3.6 all-reduce.7
  216.6 14.2 %all-reduce.3 = (f32[192]{0:T(256)}, f32[192]{0:T(256)}) all-reduce(f32[192]{0:T(256)} %get-tuple-element.79, f32[192]{0:T(256)} %get-tuple-element.80), channel_id=1, replica_groups=mesh['x'=4,'y'=8,'c'=2,'mp'=8] {'y'}, use_global_device_ids=true, to_apply=%region_22.24 | all-reduce | flops 384 | bytes 3072 | tf_op jit(solution)/shard_map/psum | solution.py:49
  230.8 9.1 %all-reduce.5 = (f32[192]{0:T(256)}, f32[192]{0:T(256)}) all-reduce(f32[192]{0:T(256)} %get-tuple-element.69, f32[192]{0:T(256)} %get-tuple-element.70), channel_id=1, replica_groups=mesh['x'=4,'y'=8,'c'=2,'mp'=8] {'x'}, use_global_device_ids=true, to_apply=%region_23.25 | all-reduce | flops 384 | bytes 3072 | tf_op jit(solution)/shard_map/psum | solution.py:49
  241.1 4.1 %multiply_reduce_fusion.31 = (f32[192]{0:T(256)}, f32[1024,192]{0,1:T(8,128)}, bf16[1024,192]{0,1:T(8,128)(2,1)}) fusion(f32[]{:T(128)} %get-tuple-element.77, f32[192]{0:T(256)} %get-tuple-element.74, f32[1024,192]{0,1:T(8,128)S(1)} %copy.49, f32[192]{0:T(256)} %get-tuple-element.87, f32[1024,192]{0,1:T(8,128)} %get-tuple-element.130, ...), kind=kLoop, calls=%fused_computation.176 | loop fusion | flops 4718400 | bytes 4334852 | tf_op jit(solution)/shard_map/reduce_sum | solution.py:40
  245.5 1.5 copy.53
  247.0 4.3 %fusion.56 = f32[64,16,192]{2,1,0:T(8,128)S(1)} fusion(f32[64,16,192]{2,1,0:T(8,128)S(1)} %bitcast.170, f32[192]{0:T(256)} %bitcast.209, f32[192]{0:T(256)} %bitcast.211, f32[192]{0:T(256)} %bitcast.215, f32[192]{0:T(256)} %bitcast.217, f32[192]{0:T(256)} %bitcast.219, f32[192]{0:T(256)} %bitcast.221, f32[192]{0:T(256)} %bitcast.223, f32[192]{0:T(256)} %bitcast.225, ...), kind=kLoop, calls=%fused_computation.126 | loop fusion | flops 11993088 | bytes 1596672 | tf_op jit(solution)/shard_map/add | solution.py:28
  252.6 2.1 multiply_convert_fusion.1
  255.2 1.8 fusion.68
  258.5 7.9 %collective-permute-start = (f32[4,8,1,1,24,384]{5,4,1,0,3,2:T(8,128)S(1)}, f32[4,8,1,1,24,384]{5,4,1,0,3,2:T(8,128)}, u32[]{:S(2)}, u32[]{:S(2)}) collective-permute-start(f32[4,8,1,1,24,384]{5,4,1,0,3,2:T(8,128)S(1)} %dynamic-slice_bitcast_fusion), channel_id=1, source_target_pairs={{0,8},{8,0},{1,9},{9,1},{2,10},{10,2},{3,11},{11,3},{4,12},{12,4},... | collective-permute-start | bytes 3538952 | tf_op jit(solution)/shard_map/ppermute | solution.py:81
  266.4 2.6 collective-permute-done
  269.0 1.8 bitcast_add_fusion
  271.7 4.7 %collective-permute-start.1 = (f32[4,1,4,1,24,384]{5,4,2,0,3,1:T(8,128)}, f32[4,1,4,1,24,384]{5,4,2,0,3,1:T(8,128)}, u32[]{:S(2)}, u32[]{:S(2)}) collective-permute-start(f32[4,1,4,1,24,384]{5,4,2,0,3,1:T(8,128)} %dynamic-slice_bitcast_fusion.1), channel_id=1, source_target_pairs={{0,64},{16,80},{32,96},{48,112},{64,0},{80,16},{96,32},{112,48},{1... | collective-permute-start | bytes 1769480 | tf_op jit(solution)/shard_map/ppermute | solution.py:81
  276.4 16.1 %all-gather.9.cloned.1.call-done = bf16[1024,1536]{0,1:T(8,128)(2,1)} async-done(((bf16[1024,192]{0,1:T(8,128)(2,1)}), bf16[1024,1536]{0,1:T(8,128)(2,1)}) %all-gather.9.cloned.1.call-update) | async-done | bytes 3145744 | tf_op jit(solution)/shard_map/all_gather | solution.py:164
  292.5 4.1 %fusion.84 = f32[1536,192]{0,1:T(8,128)} fusion(bf16[1024,1536]{0,1:T(8,128)(2,1)} %all-gather.9.cloned.1.call-done, bf16[1024,192]{0,1:T(8,128)(2,1)} %param.27), kind=kOutput, calls=%fused_computation.229 | convolution fusion | flops 603979776 | bytes 4718592 | tf_op jit(solution)/shard_map/dot_general | solution.py:89
  296.7 8.6 %collective-permute-done.1 = f32[4,1,4,1,24,384]{5,4,2,0,3,1:T(8,128)} collective-permute-done((f32[4,1,4,1,24,384]{5,4,2,0,3,1:T(8,128)}, f32[4,1,4,1,24,384]{5,4,2,0,3,1:T(8,128)}, u32[]{:S(2)}, u32[]{:S(2)}) %collective-permute-start.1) | collective-permute-done | bytes 589856 | tf_op jit(solution)/shard_map/ppermute | solution.py:81
  307.3 1.9 collective-permute-start.2
  309.2 15.4 %collective-permute-done.2 = f32[4,1,2,1,24,384]{5,4,2,0,3,1:T(8,128)S(1)} collective-permute-done((f32[4,1,2,1,24,384]{5,4,2,0,3,1:T(8,128)S(1)}, f32[4,1,2,1,24,384]{5,4,2,0,3,1:T(8,128)S(1)}, u32[]{:S(2)}, u32[]{:S(2)}) %collective-permute-start.2) | collective-permute-done | bytes 294944 | tf_op jit(solution)/shard_map/ppermute | solution.py:81
  325.7 2.1 collective-permute-start.3
  327.7 3.0 multiply_reduce_fusion.1
  330.7 1.9 collective-permute-done.3
  332.6 2.3 collective-permute-start.4
  335.0 1.7 multiply_reduce_fusion.2
  336.8 4.9 %psum.157 = f32[31,192]{1,0:T(8,128)S(1)} all-reduce(f32[31,192]{1,0:T(8,128)S(1)} %stack.139), channel_id=1, replica_groups=mesh['x'=4,'y'=8,'c'=2,'mp'=8] {'c'}, use_global_device_ids=true, to_apply=%region_58.60 | all-reduce | flops 5952 | bytes 47616 | tf_op jit(solution)/shard_map/psum | solution.py:49
  341.7 1.9 copy.57
  343.7 1.9 collective-permute-start.5
  345.6 22.5 %psum.158 = f32[31,192]{1,0:T(8,128)S(1)} all-reduce(f32[31,192]{1,0:T(8,128)S(1)} %psum.157), channel_id=1, replica_groups=mesh['x'=4,'y'=8,'c'=2,'mp'=8] {'y'}, use_global_device_ids=true, to_apply=%region_59.61 | all-reduce | flops 5952 | bytes 47616 | tf_op jit(solution)/shard_map/psum | solution.py:49
  368.0 14.1 %psum.159 = f32[31,192]{1,0:T(8,128)} all-reduce(f32[31,192]{1,0:T(8,128)S(1)} %psum.158), channel_id=1, replica_groups=mesh['x'=4,'y'=8,'c'=2,'mp'=8] {'x'}, use_global_device_ids=true, to_apply=%region_60.62 | all-reduce | flops 5952 | bytes 47616 | tf_op jit(solution)/shard_map/psum | solution.py:49
  382.9 3.7 fusion.3
  386.6 16.5 %reduce-scatter.12.cloned.1.call-done = f32[24,192]{1,0:T(8,128)} async-done(((f32[48,192]{1,0:T(8,128)}), f32[24,192]{1,0:T(8,128)}) %reduce-scatter.12.cloned.1.call-update) | async-done | bytes 18448
  (102 shorter events, 27.5 us)
Async XLA Ops:
  7.2 57.0 %copy-start = (bf16[320,192]{0,1:T(8,128)(2,1)S(1)}, bf16[320,192]{0,1:T(8,128)(2,1)}, u32[]{:S(2)}) copy-start(bf16[320,192]{0,1:T(8,128)(2,1)} %param.19) | copy-start | bytes 368644
  7.2 20.9 %copy-start.14 = (s32[1,64]{1,0:T(1,128)S(1)}, s32[1,64]{1,0:T(1,128)}, u32[]{:S(2)}) copy-start(s32[1,64]{1,0:T(1,128)} %param.16) | copy-start | bytes 772
  7.2 93.8 %all-gather.7.cloned.1.call-start = ((), (), s32[]{:S(2)}) async-start(), calls=%async_computation.7 | async-start | bytes 2396160 | tf_op jit(solution)/shard_map/all_gather | solution.py:116
  14.3 20.9 %all-to-all-start.1 = ((s32[64,1,2]{2,1,0:T(1,128)}), s32[64,1,2]{2,1,0:T(1,128)S(1)}, u32[]{:S(2)}, u32[]{:S(2)}) async-start(s32[64,1,2]{2,1,0:T(1,128)} %copy.43), calls=%async_computation.1 | async-start | bytes 65536 | tf_op jit(solution)/shard_map/all_to_all | solution.py:114
  25.9 15.2 %copy-start.10 = (bf16[128,192]{0,1:T(8,128)(2,1)S(1)}, bf16[128,192]{0,1:T(8,128)(2,1)}, u32[]{:S(2)}) copy-start(bf16[128,192]{0,1:T(8,128)(2,1)} %param.20) | copy-start | bytes 147460
  35.1 28.8 %all-to-all-start = ((bf16[64,16,320]{2,1,0:T(8,128)(2,1)}), bf16[64,16,320]{2,1,0:T(8,128)(2,1)S(1)}, u32[]{:S(2)}, u32[]{:S(2)}) async-start(bf16[64,16,320]{2,1,0:T(8,128)(2,1)} %broadcast_select_fusion), calls=%async_computation | async-start | bytes 1572864 | tf_op jit(solution)/shard_map/all_to_all | solution.py:113
  40.2 122.5 %all-gather.5.cloned.1.call-start = ((), (), s32[]{:S(2)}) async-start(), calls=%async_computation.6 | async-start | bytes 3538944 | tf_op jit(solution)/shard_map/all_gather | solution.py:142
  40.4 1.0 copy-start.6
  40.5 0.6 copy-start.7
  41.4 42.6 %copy-start.13 = (f32[192]{0:T(256)S(1)}, f32[192]{0:T(256)}, u32[]{:S(2)}) copy-start(f32[192]{0:T(256)} %param.21) | copy-start | bytes 2308
  41.7 43.9 %copy-start.11 = (f32[31,192]{1,0:T(8,128)S(1)}, f32[31,192]{1,0:T(8,128)}, u32[]{:S(2)}) copy-start(f32[31,192]{1,0:T(8,128)} %param.23) | copy-start | bytes 71428
  64.6 23.0 %copy-start.2 = (f32[1024,192]{0,1:T(8,128)}, f32[1024,192]{0,1:T(8,128)S(1)}, u32[]{:S(2)}) copy-start(f32[1024,192]{0,1:T(8,128)S(1)} %get-tuple-element.129) | copy-start | bytes 2359300
  84.9 123.4 %all-gather.11.cloned.1.call-start = ((), (), s32[]{:S(2)}) async-start(), calls=%async_computation.9 | async-start | bytes 3538944 | tf_op jit(solution)/shard_map/all_gather | solution.py:169
  101.0 1.4 slice-start
  101.0 2.9 slice-start.1
  105.2 98.2 %all-to-all-start.2 = ((bf16[8,192,192]{1,2,0:T(8,128)(2,1)}), bf16[8,192,192]{1,2,0:T(8,128)(2,1)}, u32[]{:S(2)}, u32[]{:S(2)}) async-start(bf16[8,192,192]{1,2,0:T(8,128)(2,1)} %copy.51), calls=%async_computation.2 | async-start | bytes 1572864 | tf_op jit(solution)/shard_map/all_to_all | solution.py:170
  112.3 180.2 %all-gather.9.cloned.1.call-start = ((), (), s32[]{:S(2)}) async-start(), calls=%async_computation.8 | async-start | bytes 3538944 | tf_op jit(solution)/shard_map/all_gather | solution.py:164
  162.7 3.6 copy-start.8
  166.3 78.9 %copy-start.1 = (f32[1024,384]{0,1:T(8,128)}, f32[1024,384]{0,1:T(8,128)S(1)}, u32[]{:S(2)}) copy-start(f32[1024,384]{0,1:T(8,128)S(1)} %fusion.85) | copy-start | bytes 4718596
  245.3 7.3 %copy-start.9 = (f32[1024]{0:T(1024)S(1)}, f32[1024]{0:T(1024)}, u32[]{:S(2)}) copy-start(f32[1024]{0:T(1024)} %copy-done.7) | copy-start | bytes 12292
  245.3 96.4 %reduce-scatter.8.cloned.1.call-start = ((), (), s32[]{:S(2)}) async-start(), calls=%async_computation.10 | async-start | bytes 1474560 | tf_op jit(solution)/shard_map/reduce_scatter | solution.py:61
  252.6 2.6 copy-start.15
  257.0 1.4 copy-start.4
  258.5 10.5 %collective-permute-start = (f32[4,8,1,1,24,384]{5,4,1,0,3,2:T(8,128)S(1)}, f32[4,8,1,1,24,384]{5,4,1,0,3,2:T(8,128)}, u32[]{:S(2)}, u32[]{:S(2)}) collective-permute-start(f32[4,8,1,1,24,384]{5,4,1,0,3,2:T(8,128)S(1)} %dynamic-slice_bitcast_fusion), channel_id=1, source_target_pairs={{0,8},{8,0},{1,9},{9,1},{2,10},{10,2},{3,11},{11,3},{4,12},{12,4},... | collective-permute-start | bytes 3538952 | tf_op jit(solution)/shard_map/ppermute | solution.py:81
  271.7 33.6 %collective-permute-start.1 = (f32[4,1,4,1,24,384]{5,4,2,0,3,1:T(8,128)}, f32[4,1,4,1,24,384]{5,4,2,0,3,1:T(8,128)}, u32[]{:S(2)}, u32[]{:S(2)}) collective-permute-start(f32[4,1,4,1,24,384]{5,4,2,0,3,1:T(8,128)} %dynamic-slice_bitcast_fusion.1), channel_id=1, source_target_pairs={{0,64},{16,80},{32,96},{48,112},{64,0},{80,16},{96,32},{112,48},{1... | collective-permute-start | bytes 1769480 | tf_op jit(solution)/shard_map/ppermute | solution.py:81
  296.6 86.2 %reduce-scatter.10.cloned.1.call-start = ((), (), s32[]{:S(2)}) async-start(), calls=%async_computation.11 | async-start | bytes 442368
  306.4 0.8 copy-start.5
  307.3 29.4 %copy-start.12 = (f32[192]{0:T(256)S(1)}, f32[192]{0:T(256)}, u32[]{:S(2)}) copy-start(f32[192]{0:T(256)} %get-tuple-element.84) | copy-start | bytes 2308
  307.3 17.4 %collective-permute-start.2 = (f32[4,1,2,1,24,384]{5,4,2,0,3,1:T(8,128)S(1)}, f32[4,1,2,1,24,384]{5,4,2,0,3,1:T(8,128)S(1)}, u32[]{:S(2)}, u32[]{:S(2)}) collective-permute-start(f32[4,1,2,1,24,384]{5,4,2,0,3,1:T(8,128)S(1)} %dynamic-slice_bitcast_fusion.2), channel_id=1, source_target_pairs={{0,32},{16,48},{32,0},{48,16},{64,96},{80,112},{96,64},{112,80},{1... | collective-permute-start | bytes 884744 | tf_op jit(solution)/shard_map/ppermute | solution.py:81
  325.7 57.2 %copy-start.3 = (f32[1024,192]{0,1:T(8,128)S(1)}, f32[1024,192]{0,1:T(8,128)}, u32[]{:S(2)}) copy-start(f32[1024,192]{0,1:T(8,128)} %copy-done.2) | copy-start | bytes 2359300
  325.7 6.9 %collective-permute-start.3 = (f32[4,1,1,1,24,384]{5,4,2,0,3,1:T(8,128)S(1)}, f32[4,1,1,1,24,384]{5,4,2,0,3,1:T(8,128)S(1)}, u32[]{:S(2)}, u32[]{:S(2)}) collective-permute-start(f32[4,1,1,1,24,384]{5,4,2,0,3,1:T(8,128)S(1)} %constant_dynamic-slice_fusion.1), channel_id=1, source_target_pairs={{0,16},{16,0},{32,48},{48,32},{64,80},{80,64},{96,112},{112,96},{1... | collective-permute-start | bytes 442376 | tf_op jit(solution)/shard_map/ppermute | solution.py:81
  332.6 11.0 %collective-permute-start.4 = (f32[1,2,1,1,24,384]{5,4,3,2,1,0:T(8,128)S(1)}, f32[1,2,1,1,24,384]{5,4,3,2,1,0:T(8,128)S(1)}, u32[]{:S(2)}, u32[]{:S(2)}) collective-permute-start(f32[1,2,1,1,24,384]{5,4,3,2,1,0:T(8,128)S(1)} %dynamic-slice_bitcast_fusion.3), channel_id=1, source_target_pairs={{0,256},{128,384},{256,0},{384,128},{1,257},{129,385},{257,1},{385... | collective-permute-start | bytes 221192 | tf_op jit(solution)/shard_map/ppermute | solution.py:81
  343.6 59.6 %reduce-scatter.12.cloned.1.call-start = ((), (), s32[]{:S(2)}) async-start(), calls=%async_computation.12 | async-start | bytes 73728
  343.7 38.5 %collective-permute-start.5 = (f32[1,1,1,1,24,384]{5,4,3,2,1,0:T(8,128)S(1)}, f32[1,1,1,1,24,384]{5,4,3,2,1,0:T(8,128)S(1)}, u32[]{:S(2)}, u32[]{:S(2)}) collective-permute-start(f32[1,1,1,1,24,384]{5,4,3,2,1,0:T(8,128)S(1)} %constant_dynamic-slice_fusion), channel_id=1, source_target_pairs={{0,128},{128,0},{256,384},{384,256},{1,129},{129,1},{257,385},{385... | collective-permute-start | bytes 110600 | tf_op jit(solution)/shard_map/ppermute | solution.py:81
Sparse Core Ops, SparseCore 0:
  11.8 89.1 all-gather.6
  103.7 58.9 all-gather.4
  164.7 43.5 all-gather.10
  245.4 47.0 all-gather.8
  296.8 26.1 reduce-scatter.7
  343.7 30.2 reduce-scatter.9
  383.0 20.0 reduce-scatter.11

commit v4 on v3

--- a/solution.py
+++ b/solution.py
@@ -83,6 +83,20 @@
             cur = merged.reshape(shape[:dim] + (span // 2,) + shape[dim + 1 :])
             bit -= 1
     return cur.reshape((-1,) + cols)
+
+
+def doubling_gather(value, name):
+    length = lax.axis_size(name)
+    me = lax.axis_index(name)
+    cur = value[None]
+    bit = 0
+    while (1 << bit) < length:
+        perm = [(i, i ^ (1 << bit)) for i in range(length)]
+        got = lax.ppermute(cur, name, perm)
+        low = ((me >> bit) & 1) == 0
+        cur = jnp.where(low, jnp.concatenate([cur, got]), jnp.concatenate([got, cur]))
+        bit += 1
+    return cur
 
 
 def contract_rows(left, right):
@@ -127,19 +141,24 @@
     onehot = (lang[:, None] == jnp.arange(lang_table.shape[0], dtype=jnp.int32)[None, :]).astype(
         jnp.bfloat16
     )
-    lang_rows = jnp.dot(onehot, lang_table, preferred_element_type=jnp.float32)
-    inputs = jnp.dot(mel, w_in, preferred_element_type=jnp.float32) + jnp.repeat(
+    feats = w_in.shape[0]
+    tables = doubling_gather(jnp.concatenate([w_in, lang_table], 0), "mp")
+    gains = doubling_gather(ln_gain, "mp").reshape(-1)
+    parts, _, cols = tables.shape
+    tables = jnp.transpose(tables, (1, 0, 2)).reshape(-1, parts * cols)
+    w_in_full, lang_full = tables[:feats], tables[feats:]
+    lang_rows = jnp.dot(onehot, lang_full, preferred_element_type=jnp.float32)
+    inputs_full = jnp.dot(mel, w_in_full, preferred_element_type=jnp.float32) + jnp.repeat(
         lang_rows, frames, axis=0
     )
-    row_sum, row_sq = lax.psum((jnp.sum(inputs, 1), jnp.sum(inputs * inputs, 1)), "mp")
-    mean = row_sum / model_width
-    var = row_sq / model_width - mean * mean
-    normed_in = ((inputs - mean[:, None]) * lax.rsqrt(var + EPS)[:, None] * ln_gain).astype(
-        jnp.bfloat16
-    )
+    mean = jnp.sum(inputs_full, 1) / model_width
+    var = jnp.sum(inputs_full * inputs_full, 1) / model_width - mean * mean
+    normed_full = (
+        (inputs_full - mean[:, None]) * lax.rsqrt(var + EPS)[:, None] * gains
+    ).astype(jnp.bfloat16)
+    inputs = lax.dynamic_slice_in_dim(inputs_full, lax.axis_index("mp") * cols, cols, 1)
     weights_one = stacked[:, :2].reshape(model_width, -1)
     half = weights_one.shape[1] // 2
-    normed_full = lax.all_gather(normed_in, "mp", axis=1, tiled=True)
     pre = jnp.dot(normed_full, weights_one, preferred_element_type=jnp.float32)
     linear_part = pre[:, :half]
     gate_part = pre[:, half:]

time: 411 us -> 365 us (0.89)
  waiting for transfers between devices: 158 us -> 98.4 us
  starting transfers between devices: 45 us -> 73.4 us
  blocking collectives: 114 us -> 96.2 us
    all_gather x1 -> x0, waiting for transfers between devices: 50.3 us -> none  [on_device(): normed_full = lax.all_gather(normed_in, 'mp', axis=1, tiled=True)]
    ppermute x0 -> x6, waiting for transfers between devices: none -> 35.2 us  [doubling_gather(): got = lax.ppermute(cur, name, perm)]
    ppermute x0 -> x6, starting transfers between devices: none -> 24.5 us  [doubling_gather(): got = lax.ppermute(cur, name, perm)]
    all_to_all x1, waiting for transfers between devices: 22.2 us -> 0.01 us  [on_device(): lax.all_to_all(blocks, DP_AXES, split_axis=0, concat_axis=0, tiled=True)]
    psum x1 -> x0, blocking collectives: 19.3 us -> none  [on_device(): lax.psum((jnp.sum(inputs, 1), jnp.sum(inputs * inputs, 1)), 'mp')]
    all_gather x1, waiting for transfers between devices: 13.4 us -> 0.01 us  [on_device(): lax.all_gather(jnp.concatenate([w_pw1, w_pw2[:, None, :]], 1), DP_AXES, a...]
    all_to_all x1, starting transfers between devices: 5.06 us -> 10.6 us  [on_device(): lax.all_to_all(blocks, DP_AXES, split_axis=0, concat_axis=0, tiled=True)]
    all_to_all x1, waiting for transfers between devices: 5.27 us -> 0.01 us  [on_device(): lax.all_to_all(meta_send, DP_AXES, split_axis=0, concat_axis=0, tiled=True)]
  transfers between devices with their start and end apart: 16 -> 21, of which waited for: 11 -> 9; matrix products, arithmetic and copies ran while one was open for 15% -> 17% of each run, Pallas kernels for 0% -> 0%
where the time goes in v4:
time: 365 us; the launch traced here: 363 us
  waiting for transfers between devices  98.4 us (27%)
  blocking collectives  96.2 us (26%)
  starting transfers between devices  73.4 us (20%)
  other arithmetic  34.2 us (9%)
  local copies, waits for them, and re-layouts  26.4 us (7%)
  matrix products  20 us (5%)
  between operations  14.8 us (4%)
    psum x9, blocking collectives, dp_sum(): value = lax.psum(value, name)  96.2 us
    ppermute x6, waiting for transfers between devices, doubling_gather(): got = lax.ppermute(cur, name, perm)  35.2 us
    ppermute x6, waiting for transfers between devices, halving_scatter(): got = lax.ppermute(send, name, perm)  26.9 us
    ppermute x6, starting transfers between devices, doubling_gather(): got = lax.ppermute(cur, name, perm)  24.5 us
    ppermute x6, starting transfers between devices, halving_scatter(): got = lax.ppermute(send, name, perm)  20.8 us
    all_gather x1, waiting for transfers between devices, on_device(): hidden_full = lax.all_gather(hidden, 'mp', axis=1, tiled=True)  17.6 us
    unnamed x8, waiting for transfers between devices  16.2 us
    unnamed x37, local copies, waits for them, and re-layouts  12.5 us
  transfers between devices with their start and end apart: 21, of which 9 were waited for; matrix products, arithmetic and copies ran while one was open for 17% of the time, Pallas kernels for 0%

profile of v4, /device:TPU:1, one launch (start us, length us, event | category | flops | bytes accessed | tf_op | source)
XLA Modules:
  0.0 363.2 jit_solution(2901882389190275264)
XLA Ops:
  10.4 4.8 %collective-permute-start = (bf16[1,448,192]{1,2,0:T(8,128)(2,1)S(1)}, bf16[1,448,192]{1,2,0:T(8,128)(2,1)S(1)}, u32[]{:S(2)}, u32[]{:S(2)}) collective-permute-start(bf16[1,448,192]{1,2,0:T(8,128)(2,1)S(1)} %maximum_bitcast_fusion), channel_id=1, source_target_pairs={{0,1},{1,0},{2,3},{3,2},{4,5},{5,4},{6,7},{7,6},{8,9},{9,8},{10,11... | collective-permute-start | bytes 516104 | tf_op jit(solution)/shard_map/ppermute | solution.py:95
  19.5 11.1 %all-to-all-start.1 = ((s32[64,1,2]{2,1,0:T(1,128)}), s32[64,1,2]{2,1,0:T(1,128)S(1)}, u32[]{:S(2)}, u32[]{:S(2)}) async-start(s32[64,1,2]{2,1,0:T(1,128)} %copy.47), calls=%async_computation.1 | async-start | bytes 65536 | tf_op jit(solution)/shard_map/all_to_all | solution.py:128
  30.6 1.9 collective-permute-start.3
  32.6 2.1 copy.46
  36.7 5.8 %collective-permute-start.1 = (bf16[2,448,192]{1,2,0:T(8,128)(2,1)S(1)}, bf16[2,448,192]{1,2,0:T(8,128)(2,1)S(1)}, u32[]{:S(2)}, u32[]{:S(2)}) collective-permute-start(bf16[2,448,192]{1,2,0:T(8,128)(2,1)S(1)} %maximum_select_fusion.2), channel_id=1, source_target_pairs={{0,2},{1,3},{2,0},{3,1},{4,6},{5,7},{6,4},{7,5},{8,10},{9,11},{10,... | collective-permute-start | bytes 1032200 | tf_op jit(solution)/shard_map/ppermute | solution.py:95
  43.1 1.9 collective-permute-start.4
  45.1 10.6 %all-to-all-start = ((bf16[64,16,320]{2,1,0:T(8,128)(2,1)}), bf16[64,16,320]{2,1,0:T(8,128)(2,1)S(1)}, u32[]{:S(2)}, u32[]{:S(2)}) async-start(bf16[64,16,320]{2,1,0:T(8,128)(2,1)} %broadcast_select_fusion), calls=%async_computation | async-start | bytes 1572864 | tf_op jit(solution)/shard_map/all_to_all | solution.py:127
  55.8 4.2 %collective-permute-done.1 = bf16[2,448,192]{1,2,0:T(8,128)(2,1)S(1)} collective-permute-done((bf16[2,448,192]{1,2,0:T(8,128)(2,1)S(1)}, bf16[2,448,192]{1,2,0:T(8,128)(2,1)S(1)}, u32[]{:S(2)}, u32[]{:S(2)}) %collective-permute-start.1) | collective-permute-done | bytes 344096 | tf_op jit(solution)/shard_map/ppermute | solution.py:95
  60.2 8.1 %collective-permute-start.2 = (bf16[4,448,192]{1,2,0:T(8,128)(2,1)S(1)}, bf16[4,448,192]{1,2,0:T(8,128)(2,1)S(1)}, u32[]{:S(2)}, u32[]{:S(2)}) collective-permute-start(bf16[4,448,192]{1,2,0:T(8,128)(2,1)S(1)} %maximum_select_fusion.1), channel_id=1, source_target_pairs={{0,4},{1,5},{2,6},{3,7},{4,0},{5,1},{6,2},{7,3},{8,12},{9,13},{10,... | collective-permute-start | bytes 2064392 | tf_op jit(solution)/shard_map/ppermute | solution.py:95
  68.4 1.9 collective-permute-start.5
  71.0 31.0 %collective-permute-done.5 = f32[4,192]{1,0:T(4,128)S(1)} collective-permute-done((f32[4,192]{1,0:T(4,128)S(1)}, f32[4,192]{1,0:T(4,128)S(1)}, u32[]{:S(2)}, u32[]{:S(2)}) %collective-permute-start.5) | collective-permute-done | bytes 3104 | tf_op jit(solution)/shard_map/ppermute | solution.py:95
  103.3 2.2 fusion.84
  105.6 2.6 copy-done.1
  108.2 2.5 multiply_convert_fusion
  114.8 6.0 %all-to-all-start.2 = ((bf16[8,192,192]{1,2,0:T(8,128)(2,1)}), bf16[8,192,192]{1,2,0:T(8,128)(2,1)}, u32[]{:S(2)}, u32[]{:S(2)}) async-start(bf16[8,192,192]{1,2,0:T(8,128)(2,1)} %copy.55), calls=%async_computation.2 | async-start | bytes 1572864 | tf_op jit(solution)/shard_map/all_to_all | solution.py:189
  121.1 3.7 %fusion.88 = f32[1024,384]{0,1:T(8,128)S(1)} fusion(bf16[1024,1536]{1,0:T(8,128)(2,1)} %multiply_convert_fusion, bf16[1536,384]{0,1:T(8,128)(2,1)} %bitcast.195), kind=kOutput, calls=%fused_computation.238 | convolution fusion | flops 1207959552 | bytes 5898240 | tf_op jit(solution)/shard_map/dot_general | solution.py:162
  125.3 6.0 %fusion.4 = (f32[192]{0:T(256)}, f32[192]{0:T(256)}, f32[64,16,192]{2,1,0:T(8,128)}) fusion(f32[64,16]{1,0:T(8,128)S(1)} %get-tuple-element.127, f32[192]{0:T(256)} %bitcast.257, f32[192]{0:T(256)} %bitcast.259, f32[192]{0:T(256)S(1)} %bitcast.201, f32[192]{0:T(256)S(1)} %bitcast.203, f32[192]{0:T(256)S(1)} %bitcast.205, f32[192]{0:T(256)S(1)} %bitcast.207, ...), kind=kLoop, calls=%fused_computation.76 | loop fusion | flops 12779136 | bytes 1602304 | tf_op jit(solution)/shard_map/reduce_sum | solution.py:171
  132.8 4.2 %all-reduce.7 = (f32[192]{0:T(256)S(1)}, f32[]{:T(128)}, f32[192]{0:T(256)S(1)}) all-reduce(f32[192]{0:T(256)} %get-tuple-element.64, f32[]{:T(128)} %fusion.78, f32[192]{0:T(256)} %get-tuple-element.63), channel_id=1, replica_groups=mesh['x'=4,'y'=8,'c'=2,'mp'=8] {'c'}, use_global_device_ids=true, to_apply=%region_3.5 | all-reduce | flops 385 | bytes 3080 | tf_op jit(solution)/shard_map/psum | solution.py:49
  137.1 15.5 %all-reduce.3 = (f32[192]{0:T(256)S(1)}, f32[]{:T(128)}, f32[192]{0:T(256)S(1)}) all-reduce(f32[192]{0:T(256)S(1)} %get-tuple-element.79, f32[]{:T(128)} %get-tuple-element.80, f32[192]{0:T(256)S(1)} %get-tuple-element.81), channel_id=1, replica_groups=mesh['x'=4,'y'=8,'c'=2,'mp'=8] {'y'}, use_global_device_ids=true, to_apply=%region_4.6 | all-reduce | flops 385 | bytes 3080 | tf_op jit(solution)/shard_map/psum | solution.py:49
  152.5 10.1 %all-reduce.5 = (f32[192]{0:T(256)S(1)}, f32[]{:T(128)}, f32[192]{0:T(256)S(1)}) all-reduce(f32[192]{0:T(256)S(1)} %get-tuple-element.69, f32[]{:T(128)} %get-tuple-element.70, f32[192]{0:T(256)S(1)} %get-tuple-element.71), channel_id=1, replica_groups=mesh['x'=4,'y'=8,'c'=2,'mp'=8] {'x'}, use_global_device_ids=true, to_apply=%region_5.7 | all-reduce | flops 385 | bytes 3080 | tf_op jit(solution)/shard_map/psum | solution.py:49
  163.3 2.5 all-gather.8.cloned.1.call-done
  165.8 4.0 %fusion.85 = (f32[192]{0:T(256)S(1)}, f32[192]{0:T(256)S(1)}, f32[1024,192]{0,1:T(8,128)}) fusion(f32[192]{0:T(256)S(1)} %get-tuple-element.84, f32[1024,192]{0,1:T(8,128)S(1)} %copy.52, f32[192]{0:T(256)S(1)} %get-tuple-element.85, f32[192]{0:T(256)} %param.25, f32[192]{0:T(256)} %param.24, f32[1024]{0:T(1024)S(1)} %reshape.200, ...), kind=kOutput, calls=%fused_computation.235 | convolution fusion | flops 607125120 | bytes 5317120 | tf_op jit(solution)/shard_map/dot_general | solution.py:190
  169.9 3.3 all-reduce.6
  173.2 13.1 %all-reduce.2 = (f32[192]{0:T(256)S(1)}, f32[192]{0:T(256)S(1)}) all-reduce(f32[192]{0:T(256)S(1)} %get-tuple-element.77, f32[192]{0:T(256)S(1)} %get-tuple-element.78), channel_id=1, replica_groups=mesh['x'=4,'y'=8,'c'=2,'mp'=8] {'y'}, use_global_device_ids=true, to_apply=%region_20.22 | all-reduce | flops 384 | bytes 3072 | tf_op jit(solution)/shard_map/psum | solution.py:49
  186.3 8.9 %all-reduce.4 = (f32[192]{0:T(256)}, f32[192]{0:T(256)S(1)}) all-reduce(f32[192]{0:T(256)S(1)} %get-tuple-element.67, f32[192]{0:T(256)S(1)} %get-tuple-element.68), channel_id=1, replica_groups=mesh['x'=4,'y'=8,'c'=2,'mp'=8] {'x'}, use_global_device_ids=true, to_apply=%region_21.23 | all-reduce | flops 384 | bytes 3072 | tf_op jit(solution)/shard_map/psum | solution.py:49
  196.0 3.6 multiply_reduce_fusion.32
  201.2 3.4 fusion.56
  205.9 2.1 multiply_convert_fusion.2
  208.4 1.8 fusion.68
  211.8 7.7 %collective-permute-start.6 = (f32[4,8,1,1,24,384]{5,4,1,0,3,2:T(8,128)S(1)}, f32[4,8,1,1,24,384]{5,4,1,0,3,2:T(8,128)}, u32[]{:S(2)}, u32[]{:S(2)}) collective-permute-start(f32[4,8,1,1,24,384]{5,4,1,0,3,2:T(8,128)S(1)} %dynamic-slice_bitcast_fusion), channel_id=1, source_target_pairs={{0,8},{8,0},{1,9},{9,1},{2,10},{10,2},{3,11},{11,3},{4,12},{12,4},... | collective-permute-start | bytes 3538952 | tf_op jit(solution)/shard_map/ppermute | solution.py:81
  219.5 2.6 collective-permute-done.6
  222.1 1.8 bitcast_add_fusion.1
  224.7 4.8 %collective-permute-start.7 = (f32[4,1,4,1,24,384]{5,4,2,0,3,1:T(8,128)}, f32[4,1,4,1,24,384]{5,4,2,0,3,1:T(8,128)}, u32[]{:S(2)}, u32[]{:S(2)}) collective-permute-start(f32[4,1,4,1,24,384]{5,4,2,0,3,1:T(8,128)} %dynamic-slice_bitcast_fusion.1), channel_id=1, source_target_pairs={{0,64},{16,80},{32,96},{48,112},{64,0},{80,16},{96,32},{112,48},{1... | collective-permute-start | bytes 1769480 | tf_op jit(solution)/shard_map/ppermute | solution.py:81
  229.6 17.6 %all-gather.6.cloned.1.call-done = bf16[1024,1536]{0,1:T(8,128)(2,1)} async-done(((bf16[1024,192]{0,1:T(8,128)(2,1)}), bf16[1024,1536]{0,1:T(8,128)(2,1)}) %all-gather.6.cloned.1.call-update) | async-done | bytes 3145744 | tf_op jit(solution)/shard_map/all_gather | solution.py:183
  247.2 4.1 %fusion.89 = f32[1536,192]{0,1:T(8,128)} fusion(bf16[1024,1536]{0,1:T(8,128)(2,1)} %all-gather.6.cloned.1.call-done, bf16[1024,192]{0,1:T(8,128)(2,1)} %param.27), kind=kOutput, calls=%fused_computation.239 | convolution fusion | flops 603979776 | bytes 4718592 | tf_op jit(solution)/shard_map/dot_general | solution.py:103
  251.4 6.8 %collective-permute-done.7 = f32[4,1,4,1,24,384]{5,4,2,0,3,1:T(8,128)} collective-permute-done((f32[4,1,4,1,24,384]{5,4,2,0,3,1:T(8,128)}, f32[4,1,4,1,24,384]{5,4,2,0,3,1:T(8,128)}, u32[]{:S(2)}, u32[]{:S(2)}) %collective-permute-start.7) | collective-permute-done | bytes 589856 | tf_op jit(solution)/shard_map/ppermute | solution.py:81
  260.2 1.9 collective-permute-start.8
  262.1 15.7 %collective-permute-done.8 = f32[4,1,2,1,24,384]{5,4,2,0,3,1:T(8,128)S(1)} collective-permute-done((f32[4,1,2,1,24,384]{5,4,2,0,3,1:T(8,128)S(1)}, f32[4,1,2,1,24,384]{5,4,2,0,3,1:T(8,128)S(1)}, u32[]{:S(2)}, u32[]{:S(2)}) %collective-permute-start.8) | collective-permute-done | bytes 294944 | tf_op jit(solution)/shard_map/ppermute | solution.py:81
  278.9 2.1 collective-permute-start.9
  281.0 3.0 multiply_reduce_fusion.2
  285.9 2.3 collective-permute-start.10
  289.9 4.9 %psum.141 = f32[31,192]{1,0:T(8,128)S(1)} all-reduce(f32[31,192]{1,0:T(8,128)S(1)} %stack.139), channel_id=1, replica_groups=mesh['x'=4,'y'=8,'c'=2,'mp'=8] {'c'}, use_global_device_ids=true, to_apply=%region_56.58 | all-reduce | flops 5952 | bytes 47616 | tf_op jit(solution)/shard_map/psum | solution.py:49
  294.8 1.9 copy.63
  296.8 1.9 collective-permute-start.11
  298.7 22.3 %psum.142 = f32[31,192]{1,0:T(8,128)S(1)} all-reduce(f32[31,192]{1,0:T(8,128)S(1)} %psum.141), channel_id=1, replica_groups=mesh['x'=4,'y'=8,'c'=2,'mp'=8] {'y'}, use_global_device_ids=true, to_apply=%region_57.59 | all-reduce | flops 5952 | bytes 47616 | tf_op jit(solution)/shard_map/psum | solution.py:49
  321.0 13.8 %psum.143 = f32[31,192]{1,0:T(8,128)} all-reduce(f32[31,192]{1,0:T(8,128)S(1)} %psum.142), channel_id=1, replica_groups=mesh['x'=4,'y'=8,'c'=2,'mp'=8] {'x'}, use_global_device_ids=true, to_apply=%region_58.60 | all-reduce | flops 5952 | bytes 47616 | tf_op jit(solution)/shard_map/psum | solution.py:49
  335.6 3.8 %add_convert_fusion = bf16[1024,192]{1,0:T(8,128)(2,1)S(1)} fusion(f32[1024,1536]{1,0:T(8,128)} %copy-done.1, s32[]{:T(128)S(6)} %select_n.135, bf16[1024,1536]{0,1:T(8,128)(2,1)} %all-gather.6.cloned.1.call-done, bf16[1536,3,192]{2,0,1:T(8,128)(2,1)} %all-gather.4.cloned.1.call-done), kind=kOutput, calls=%fused_computation.167 | convolution fusion | flops 604372992 | bytes 5373956 | tf_op jit(solution)/shard_map/dot_general | solution.py:185
  340.3 16.1 %reduce-scatter.12.cloned.1.call-done = f32[24,192]{1,0:T(8,128)} async-done(((f32[48,192]{1,0:T(8,128)}), f32[24,192]{1,0:T(8,128)}) %reduce-scatter.12.cloned.1.call-update) | async-done | bytes 18448
  (118 shorter events, 34.1 us)
Async XLA Ops:
  7.2 8.7 %copy-start = (s32[128]{0:T(128)S(1)}, s32[128]{0:T(128)}, u32[]{:S(2)}) copy-start(s32[128]{0:T(128)} %param.17) | copy-start | bytes 1540
  7.2 27.6 %copy-start.15 = (s32[1,64]{1,0:T(1,128)S(1)}, s32[1,64]{1,0:T(1,128)}, u32[]{:S(2)}) copy-start(s32[1,64]{1,0:T(1,128)} %param.16) | copy-start | bytes 772
  7.2 103.5 %all-gather.4.cloned.1.call-start = ((), (), s32[]{:S(2)}) async-start(), calls=%async_computation.6 | async-start | bytes 2396160 | tf_op jit(solution)/shard_map/all_gather | solution.py:130
  10.4 26.2 %collective-permute-start = (bf16[1,448,192]{1,2,0:T(8,128)(2,1)S(1)}, bf16[1,448,192]{1,2,0:T(8,128)(2,1)S(1)}, u32[]{:S(2)}, u32[]{:S(2)}) collective-permute-start(bf16[1,448,192]{1,2,0:T(8,128)(2,1)S(1)} %maximum_bitcast_fusion), channel_id=1, source_target_pairs={{0,1},{1,0},{2,3},{3,2},{4,5},{5,4},{6,7},{7,6},{8,9},{9,8},{10,11... | collective-permute-start | bytes 516104 | tf_op jit(solution)/shard_map/ppermute | solution.py:95
  19.5 25.6 %all-to-all-start.1 = ((s32[64,1,2]{2,1,0:T(1,128)}), s32[64,1,2]{2,1,0:T(1,128)S(1)}, u32[]{:S(2)}, u32[]{:S(2)}) async-start(s32[64,1,2]{2,1,0:T(1,128)} %copy.47), calls=%async_computation.1 | async-start | bytes 65536 | tf_op jit(solution)/shard_map/all_to_all | solution.py:128
  30.6 135.3 %all-gather.8.cloned.1.call-start = ((), (), s32[]{:S(2)}) async-start(), calls=%async_computation.8 | async-start | bytes 3538944 | tf_op jit(solution)/shard_map/all_gather | solution.py:188
  30.6 12.5 %collective-permute-start.3 = (f32[1,192]{1,0:T(1,128)}, f32[1,192]{1,0:T(1,128)S(1)}, u32[]{:S(2)}, u32[]{:S(2)}) collective-permute-start(f32[1,192]{1,0:T(1,128)} %bitcast.293), channel_id=1, source_target_pairs={{0,1},{1,0},{2,3},{3,2},{4,5},{5,4},{6,7},{7,6},{8,9},{9,8},{10,11... | collective-permute-start | bytes 2312 | tf_op jit(solution)/shard_map/ppermute | solution.py:95
  32.6 9.9 %copy-start.6 = (f32[31,192]{1,0:T(8,128)S(1)}, f32[31,192]{1,0:T(8,128)}, u32[]{:S(2)}) copy-start(f32[31,192]{1,0:T(8,128)} %param.23) | copy-start | bytes 71428
  32.6 10.5 %copy-start.14 = (f32[192]{0:T(256)S(1)}, f32[192]{0:T(256)}, u32[]{:S(2)}) copy-start(f32[192]{0:T(256)} %param.21) | copy-start | bytes 2308
  36.7 23.3 %collective-permute-start.1 = (bf16[2,448,192]{1,2,0:T(8,128)(2,1)S(1)}, bf16[2,448,192]{1,2,0:T(8,128)(2,1)S(1)}, u32[]{:S(2)}, u32[]{:S(2)}) collective-permute-start(bf16[2,448,192]{1,2,0:T(8,128)(2,1)S(1)} %maximum_select_fusion.2), channel_id=1, source_target_pairs={{0,2},{1,3},{2,0},{3,1},{4,6},{5,7},{6,4},{7,5},{8,10},{9,11},{10,... | collective-permute-start | bytes 1032200 | tf_op jit(solution)/shard_map/ppermute | solution.py:95
  43.1 25.2 %collective-permute-start.4 = (f32[2,192]{1,0:T(2,128)S(1)}, f32[2,192]{1,0:T(2,128)S(1)}, u32[]{:S(2)}, u32[]{:S(2)}) collective-permute-start(f32[2,192]{1,0:T(2,128)S(1)} %maximum_select_fusion.5), channel_id=1, source_target_pairs={{0,2},{1,3},{2,0},{3,1},{4,6},{5,7},{6,4},{7,5},{8,10},{9,11},{10,... | collective-permute-start | bytes 4616 | tf_op jit(solution)/shard_map/ppermute | solution.py:95
  45.1 58.0 %all-to-all-start = ((bf16[64,16,320]{2,1,0:T(8,128)(2,1)}), bf16[64,16,320]{2,1,0:T(8,128)(2,1)S(1)}, u32[]{:S(2)}, u32[]{:S(2)}) async-start(bf16[64,16,320]{2,1,0:T(8,128)(2,1)} %broadcast_select_fusion), calls=%async_computation | async-start | bytes 1572864 | tf_op jit(solution)/shard_map/all_to_all | solution.py:127
  60.2 42.0 %collective-permute-start.2 = (bf16[4,448,192]{1,2,0:T(8,128)(2,1)S(1)}, bf16[4,448,192]{1,2,0:T(8,128)(2,1)S(1)}, u32[]{:S(2)}, u32[]{:S(2)}) collective-permute-start(bf16[4,448,192]{1,2,0:T(8,128)(2,1)S(1)} %maximum_select_fusion.1), channel_id=1, source_target_pairs={{0,4},{1,5},{2,6},{3,7},{4,0},{5,1},{6,2},{7,3},{8,12},{9,13},{10,... | collective-permute-start | bytes 2064392 | tf_op jit(solution)/shard_map/ppermute | solution.py:95
  68.4 33.7 %collective-permute-start.5 = (f32[4,192]{1,0:T(4,128)S(1)}, f32[4,192]{1,0:T(4,128)S(1)}, u32[]{:S(2)}, u32[]{:S(2)}) collective-permute-start(f32[4,192]{1,0:T(4,128)S(1)} %maximum_select_fusion.4), channel_id=1, source_target_pairs={{0,4},{1,5},{2,6},{3,7},{4,0},{5,1},{6,2},{7,3},{8,12},{9,13},{10,... | collective-permute-start | bytes 9224 | tf_op jit(solution)/shard_map/ppermute | solution.py:95
  105.5 2.7 copy-start.1
  110.7 1.4 slice-start
  110.7 2.9 slice-start.1
  114.8 48.5 %all-to-all-start.2 = ((bf16[8,192,192]{1,2,0:T(8,128)(2,1)}), bf16[8,192,192]{1,2,0:T(8,128)(2,1)}, u32[]{:S(2)}, u32[]{:S(2)}) async-start(bf16[8,192,192]{1,2,0:T(8,128)(2,1)} %copy.55), calls=%async_computation.2 | async-start | bytes 1572864 | tf_op jit(solution)/shard_map/all_to_all | solution.py:189
  120.8 126.3 %all-gather.6.cloned.1.call-start = ((), (), s32[]{:S(2)}) async-start(), calls=%async_computation.7 | async-start | bytes 3538944 | tf_op jit(solution)/shard_map/all_gather | solution.py:183
  124.7 74.9 %copy-start.2 = (f32[1024,384]{0,1:T(8,128)}, f32[1024,384]{0,1:T(8,128)S(1)}, u32[]{:S(2)}) copy-start(f32[1024,384]{0,1:T(8,128)S(1)} %fusion.88) | copy-start | bytes 4718596
  163.3 6.6 %copy-start.12 = (f32[192]{0:T(256)}, f32[192]{0:T(256)S(1)}, u32[]{:S(2)}) copy-start(f32[192]{0:T(256)S(1)} %get-tuple-element.85) | copy-start | bytes 2308
  195.3 0.7 copy-start.13
  196.0 5.2 %copy-start.7 = (f32[1,192]{1,0:T(1,128)S(1)}, f32[1,192]{1,0:T(1,128)}, u32[]{:S(2)}) copy-start(f32[1,192]{1,0:T(1,128)} %get-tuple-element.118) | copy-start | bytes 2308
  196.0 5.2 %copy-start.8 = (f32[1,192]{1,0:T(1,128)S(1)}, f32[1,192]{1,0:T(1,128)}, u32[]{:S(2)}) copy-start(f32[1,192]{1,0:T(1,128)} %get-tuple-element.119) | copy-start | bytes 2308
  196.0 5.2 %copy-start.9 = (f32[1,192]{1,0:T(1,128)S(1)}, f32[1,192]{1,0:T(1,128)}, u32[]{:S(2)}) copy-start(f32[1,192]{1,0:T(1,128)} %get-tuple-element.120) | copy-start | bytes 2308
  196.0 5.2 %copy-start.10 = (f32[1,192]{1,0:T(1,128)S(1)}, f32[1,192]{1,0:T(1,128)}, u32[]{:S(2)}) copy-start(f32[1,192]{1,0:T(1,128)} %get-tuple-element.121) | copy-start | bytes 2308
  196.0 5.2 %copy-start.11 = (f32[1,192]{1,0:T(1,128)S(1)}, f32[1,192]{1,0:T(1,128)}, u32[]{:S(2)}) copy-start(f32[1,192]{1,0:T(1,128)} %get-tuple-element.122) | copy-start | bytes 2308
  199.7 95.1 %reduce-scatter.8.cloned.1.call-start = ((), (), s32[]{:S(2)}) async-start(), calls=%async_computation.9 | async-start | bytes 1474560 | tf_op jit(solution)/shard_map/reduce_scatter | solution.py:61
  205.8 2.6 copy-start.3
  210.3 1.4 copy-start.4
  211.8 10.3 %collective-permute-start.6 = (f32[4,8,1,1,24,384]{5,4,1,0,3,2:T(8,128)S(1)}, f32[4,8,1,1,24,384]{5,4,1,0,3,2:T(8,128)}, u32[]{:S(2)}, u32[]{:S(2)}) collective-permute-start(f32[4,8,1,1,24,384]{5,4,1,0,3,2:T(8,128)S(1)} %dynamic-slice_bitcast_fusion), channel_id=1, source_target_pairs={{0,8},{8,0},{1,9},{9,1},{2,10},{10,2},{3,11},{11,3},{4,12},{12,4},... | collective-permute-start | bytes 3538952 | tf_op jit(solution)/shard_map/ppermute | solution.py:81
  224.7 33.4 %collective-permute-start.7 = (f32[4,1,4,1,24,384]{5,4,2,0,3,1:T(8,128)}, f32[4,1,4,1,24,384]{5,4,2,0,3,1:T(8,128)}, u32[]{:S(2)}, u32[]{:S(2)}) collective-permute-start(f32[4,1,4,1,24,384]{5,4,2,0,3,1:T(8,128)} %dynamic-slice_bitcast_fusion.1), channel_id=1, source_target_pairs={{0,64},{16,80},{32,96},{48,112},{64,0},{80,16},{96,32},{112,48},{1... | collective-permute-start | bytes 1769480 | tf_op jit(solution)/shard_map/ppermute | solution.py:81
  251.3 84.3 %reduce-scatter.10.cloned.1.call-start = ((), (), s32[]{:S(2)}) async-start(), calls=%async_computation.10 | async-start | bytes 442368
  259.3 0.8 copy-start.5
  260.2 17.7 %collective-permute-start.8 = (f32[4,1,2,1,24,384]{5,4,2,0,3,1:T(8,128)S(1)}, f32[4,1,2,1,24,384]{5,4,2,0,3,1:T(8,128)S(1)}, u32[]{:S(2)}, u32[]{:S(2)}) collective-permute-start(f32[4,1,2,1,24,384]{5,4,2,0,3,1:T(8,128)S(1)} %dynamic-slice_bitcast_fusion.2), channel_id=1, source_target_pairs={{0,32},{16,48},{32,0},{48,16},{64,96},{80,112},{96,64},{112,80},{1... | collective-permute-start | bytes 884744 | tf_op jit(solution)/shard_map/ppermute | solution.py:81
  278.9 6.9 %collective-permute-start.9 = (f32[4,1,1,1,24,384]{5,4,2,0,3,1:T(8,128)S(1)}, f32[4,1,1,1,24,384]{5,4,2,0,3,1:T(8,128)S(1)}, u32[]{:S(2)}, u32[]{:S(2)}) collective-permute-start(f32[4,1,1,1,24,384]{5,4,2,0,3,1:T(8,128)S(1)} %constant_dynamic-slice_fusion.1), channel_id=1, source_target_pairs={{0,16},{16,0},{32,48},{48,32},{64,80},{80,64},{96,112},{112,96},{1... | collective-permute-start | bytes 442376 | tf_op jit(solution)/shard_map/ppermute | solution.py:81
  285.9 10.9 %collective-permute-start.10 = (f32[1,2,1,1,24,384]{5,4,3,2,1,0:T(8,128)S(1)}, f32[1,2,1,1,24,384]{5,4,3,2,1,0:T(8,128)S(1)}, u32[]{:S(2)}, u32[]{:S(2)}) collective-permute-start(f32[1,2,1,1,24,384]{5,4,3,2,1,0:T(8,128)S(1)} %dynamic-slice_bitcast_fusion.3), channel_id=1, source_target_pairs={{0,256},{128,384},{256,0},{384,128},{1,257},{129,385},{257,1},{385... | collective-permute-start | bytes 221192 | tf_op jit(solution)/shard_map/ppermute | solution.py:81
  296.7 59.7 %reduce-scatter.12.cloned.1.call-start = ((), (), s32[]{:S(2)}) async-start(), calls=%async_computation.11 | async-start | bytes 73728
  296.8 38.0 %collective-permute-start.11 = (f32[1,1,1,1,24,384]{5,4,3,2,1,0:T(8,128)S(1)}, f32[1,1,1,1,24,384]{5,4,3,2,1,0:T(8,128)S(1)}, u32[]{:S(2)}, u32[]{:S(2)}) collective-permute-start(f32[1,1,1,1,24,384]{5,4,3,2,1,0:T(8,128)S(1)} %constant_dynamic-slice_fusion), channel_id=1, source_target_pairs={{0,128},{128,0},{256,384},{384,256},{1,129},{129,1},{257,385},{385... | collective-permute-start | bytes 110600 | tf_op jit(solution)/shard_map/ppermute | solution.py:81
Sparse Core Ops, SparseCore 0:
  11.8 88.8 all-gather.3
  102.8 62.9 all-gather.7
  199.8 47.3 all-gather.5
  251.4 26.1 reduce-scatter.7
  296.8 30.9 reduce-scatter.9
  335.7 20.6 reduce-scatter.11

commit v5 on v4

--- a/solution.py
+++ b/solution.py
@@ -62,9 +62,10 @@
     return value
 
 
-def halving_scatter(value, sizes):
+def halving_scatter(value, sizes, extra):
     cols = value.shape[1:]
     cur = value.reshape(tuple(sizes[a] for a in DP_AXES) + (-1,) + cols)
+    rows = extra.shape[0]
     for dim, name in reversed(list(enumerate(DP_AXES))):
         length = sizes[name]
         me = lax.axis_index(name)
@@ -78,11 +79,13 @@
             keep = lax.dynamic_index_in_dim(pieces, mine, dim + 1, keepdims=False)
             send = lax.dynamic_index_in_dim(pieces, 1 - mine, dim + 1, keepdims=False)
             perm = [(i, i ^ (1 << bit)) for i in range(length)]
-            got = lax.ppermute(send, name, perm)
-            merged = keep + got
+            message = jnp.concatenate([send.reshape((-1,) + cols), extra], 0)
+            got = lax.ppermute(message, name, perm)
+            merged = keep + got[:-rows].reshape(send.shape)
+            extra = extra + got[-rows:]
             cur = merged.reshape(shape[:dim] + (span // 2,) + shape[dim + 1 :])
             bit -= 1
-    return cur.reshape((-1,) + cols)
+    return cur.reshape((-1,) + cols), extra
 
 
 def doubling_gather(value, name):
@@ -195,13 +198,18 @@
     dconv = (
         valid_col * inv_std * bn_gain * (dact - grad_bias / count - normed_conv * grad_gain / count)
     )
-    grad_kernel = dp_sum(kernel_terms(dconv, glu_out, kernel.shape[0], frames))
+    kernel_part = kernel_terms(dconv, glu_out, kernel.shape[0], frames)
     dglu = depth_back(dconv, kernel, frames)
     dlin = dglu * valid_col * gate_sig
     dgate = dglu * valid_col * linear_part * gate_sig * (1.0 - gate_sig)
     dpre = jnp.concatenate([dlin, dgate], 1).astype(jnp.bfloat16)
     sizes = {name: lax.axis_size(name) for name in DP_AXES}
-    grad_pw1 = halving_scatter(contract_rows(normed_full, dpre), sizes)
+    width = dpre.shape[1]
+    flat = kernel_part.reshape(-1)
+    pad = (-flat.shape[0]) % width
+    extra = jnp.pad(flat, (0, pad)).reshape(-1, width)
+    grad_pw1, extra = halving_scatter(contract_rows(normed_full, dpre), sizes, extra)
+    grad_kernel = extra.reshape(-1)[: flat.shape[0]].reshape(kernel_part.shape)
     grad_pw1 = grad_pw1.reshape(grad_pw1.shape[0], 2, half)
     return (encoded, grad_pw1, grad_pw2, grad_kernel, grad_gain, grad_bias)
 

time: 365 us -> 364 us (level)
  waiting for transfers between devices: 98.4 us -> 142 us
  blocking collectives: 96.2 us -> 55.2 us
    psum x9 -> x6, blocking collectives: 96.2 us -> 55.2 us  [dp_sum(): value = lax.psum(value, name)]
    unnamed x8, waiting for transfers between devices: 16.2 us -> 47.1 us
    ppermute x6, waiting for transfers between devices: 26.9 us -> 57.5 us  [halving_scatter(): got = lax.ppermute(message, name, perm)]
    all_gather x1, waiting for transfers between devices: 17.6 us -> 0.02 us  [on_device(): hidden_full = lax.all_gather(hidden, 'mp', axis=1, tiled=True)]
    unnamed x37 -> x39, local copies, waits for them, and re-layouts: 12.5 us -> 10.3 us
  transfers between devices with their start and end apart: 21 -> 21, of which waited for: 9 -> 11; matrix products, arithmetic and copies ran while one was open for 17% -> 16% of each run, Pallas kernels for 0% -> 0%
where the time goes in v5:
time: 364 us; the launch traced here: 363 us
  waiting for transfers between devices  142 us (39%)
  starting transfers between devices  73.9 us (20%)
  blocking collectives  55.2 us (15%)
  other arithmetic  32.3 us (9%)
  local copies, waits for them, and re-layouts  24.4 us (7%)
  matrix products  19.7 us (5%)
  between operations  14.9 us (4%)
    ppermute x6, waiting for transfers between devices, halving_scatter(): got = lax.ppermute(message, name, perm)  57.5 us
    psum x6, blocking collectives, dp_sum(): value = lax.psum(value, name)  55.2 us
    unnamed x8, waiting for transfers between devices  47.1 us
    ppermute x6, waiting for transfers between devices, doubling_gather(): got = lax.ppermute(cur, name, perm)  35.2 us
    ppermute x6, starting transfers between devices, doubling_gather(): got = lax.ppermute(cur, name, perm)  24.5 us
    ppermute x6, starting transfers between devices, halving_scatter(): got = lax.ppermute(message, name, perm)  21 us
    all_to_all x1, starting transfers between devices, on_device(): lax.all_to_all(meta_send, DP_AXES, split_axis=0, concat_axis=0, tiled=True)  11.1 us
    all_to_all x1, starting transfers between devices, on_device(): lax.all_to_all(blocks, DP_AXES, split_axis=0, concat_axis=0, tiled=True)  10.6 us
  transfers between devices with their start and end apart: 21, of which 11 were waited for; matrix products, arithmetic and copies ran while one was open for 16% of the time, Pallas kernels for 0%

profile of v5, /device:TPU:1, one launch (start us, length us, event | category | flops | bytes accessed | tf_op | source)
XLA Modules:
  0.0 362.6 jit_solution(12312200568947819006)
XLA Ops:
  10.4 4.8 %collective-permute-start = (bf16[1,448,192]{1,2,0:T(8,128)(2,1)S(1)}, bf16[1,448,192]{1,2,0:T(8,128)(2,1)S(1)}, u32[]{:S(2)}, u32[]{:S(2)}) collective-permute-start(bf16[1,448,192]{1,2,0:T(8,128)(2,1)S(1)} %maximum_bitcast_fusion), channel_id=1, source_target_pairs={{0,1},{1,0},{2,3},{3,2},{4,5},{5,4},{6,7},{7,6},{8,9},{9,8},{10,11... | collective-permute-start | bytes 516104 | tf_op jit(solution)/shard_map/ppermute | solution.py:98
  19.5 11.1 %all-to-all-start.1 = ((s32[64,1,2]{2,1,0:T(1,128)}), s32[64,1,2]{2,1,0:T(1,128)S(1)}, u32[]{:S(2)}, u32[]{:S(2)}) async-start(s32[64,1,2]{2,1,0:T(1,128)} %copy.46), calls=%async_computation.1 | async-start | bytes 65536 | tf_op jit(solution)/shard_map/all_to_all | solution.py:131
  30.6 1.9 collective-permute-start.3
  32.6 2.1 copy.45
  36.6 5.8 %collective-permute-start.1 = (bf16[2,448,192]{1,2,0:T(8,128)(2,1)S(1)}, bf16[2,448,192]{1,2,0:T(8,128)(2,1)S(1)}, u32[]{:S(2)}, u32[]{:S(2)}) collective-permute-start(bf16[2,448,192]{1,2,0:T(8,128)(2,1)S(1)} %maximum_select_fusion.2), channel_id=1, source_target_pairs={{0,2},{1,3},{2,0},{3,1},{4,6},{5,7},{6,4},{7,5},{8,10},{9,11},{10,... | collective-permute-start | bytes 1032200 | tf_op jit(solution)/shard_map/ppermute | solution.py:98
  43.1 1.9 collective-permute-start.4
  45.1 10.6 %all-to-all-start = ((bf16[64,16,320]{2,1,0:T(8,128)(2,1)}), bf16[64,16,320]{2,1,0:T(8,128)(2,1)S(1)}, u32[]{:S(2)}, u32[]{:S(2)}) async-start(bf16[64,16,320]{2,1,0:T(8,128)(2,1)} %broadcast_select_fusion), calls=%async_computation | async-start | bytes 1572864 | tf_op jit(solution)/shard_map/all_to_all | solution.py:130
  55.8 4.2 %collective-permute-done.1 = bf16[2,448,192]{1,2,0:T(8,128)(2,1)S(1)} collective-permute-done((bf16[2,448,192]{1,2,0:T(8,128)(2,1)S(1)}, bf16[2,448,192]{1,2,0:T(8,128)(2,1)S(1)}, u32[]{:S(2)}, u32[]{:S(2)}) %collective-permute-start.1) | collective-permute-done | bytes 344096 | tf_op jit(solution)/shard_map/ppermute | solution.py:98
  60.1 8.1 %collective-permute-start.2 = (bf16[4,448,192]{1,2,0:T(8,128)(2,1)S(1)}, bf16[4,448,192]{1,2,0:T(8,128)(2,1)S(1)}, u32[]{:S(2)}, u32[]{:S(2)}) collective-permute-start(bf16[4,448,192]{1,2,0:T(8,128)(2,1)S(1)} %maximum_select_fusion.1), channel_id=1, source_target_pairs={{0,4},{1,5},{2,6},{3,7},{4,0},{5,1},{6,2},{7,3},{8,12},{9,13},{10,... | collective-permute-start | bytes 2064392 | tf_op jit(solution)/shard_map/ppermute | solution.py:98
  68.3 1.9 collective-permute-start.5
  71.0 31.0 %collective-permute-done.5 = f32[4,192]{1,0:T(4,128)S(1)} collective-permute-done((f32[4,192]{1,0:T(4,128)S(1)}, f32[4,192]{1,0:T(4,128)S(1)}, u32[]{:S(2)}, u32[]{:S(2)}) %collective-permute-start.5) | collective-permute-done | bytes 3104 | tf_op jit(solution)/shard_map/ppermute | solution.py:98
  103.3 2.2 fusion.84
  105.6 2.6 copy-done.1
  108.2 2.6 multiply_convert_fusion
  114.9 6.1 %all-to-all-start.2 = ((bf16[8,192,192]{1,2,0:T(8,128)(2,1)}), bf16[8,192,192]{1,2,0:T(8,128)(2,1)}, u32[]{:S(2)}, u32[]{:S(2)}) async-start(bf16[8,192,192]{1,2,0:T(8,128)(2,1)} %copy.54), calls=%async_computation.2 | async-start | bytes 1572864 | tf_op jit(solution)/shard_map/all_to_all | solution.py:192
  121.1 3.7 %fusion.88 = f32[1024,384]{0,1:T(8,128)S(1)} fusion(bf16[1024,1536]{1,0:T(8,128)(2,1)} %multiply_convert_fusion, bf16[1536,384]{0,1:T(8,128)(2,1)} %bitcast.204), kind=kOutput, calls=%fused_computation.251 | convolution fusion | flops 1207959552 | bytes 5898240 | tf_op jit(solution)/shard_map/dot_general | solution.py:165
  125.4 6.0 %fusion.4 = (f32[192]{0:T(256)}, f32[192]{0:T(256)}, f32[64,16,192]{2,1,0:T(8,128)}) fusion(f32[64,16]{1,0:T(8,128)S(1)} %get-tuple-element.127, f32[192]{0:T(256)S(1)} %bitcast.233, f32[192]{0:T(256)S(1)} %bitcast.235, f32[192]{0:T(256)S(1)} %bitcast.239, f32[192]{0:T(256)S(1)} %bitcast.241, f32[192]{0:T(256)S(1)} %bitcast.243, f32[192]{0:T(256)S(1)} %bitcast.245, ...), kind=kLoop, calls=%fused_computation.75 | loop fusion | flops 12779136 | bytes 1602304 | tf_op jit(solution)/shard_map/reduce_sum | solution.py:174
  132.9 4.2 %all-reduce.8 = (f32[192]{0:T(256)S(1)}, f32[]{:T(128)}, f32[192]{0:T(256)S(1)}) all-reduce(f32[192]{0:T(256)} %get-tuple-element.58, f32[]{:T(128)} %fusion.78, f32[192]{0:T(256)} %get-tuple-element.57), channel_id=1, replica_groups=mesh['x'=4,'y'=8,'c'=2,'mp'=8] {'c'}, use_global_device_ids=true, to_apply=%region_3.5 | all-reduce | flops 385 | bytes 3080 | tf_op jit(solution)/shard_map/psum | solution.py:49
  137.2 15.5 %all-reduce.4 = (f32[192]{0:T(256)S(1)}, f32[]{:T(128)}, f32[192]{0:T(256)S(1)}) all-reduce(f32[192]{0:T(256)S(1)} %get-tuple-element.73, f32[]{:T(128)} %get-tuple-element.74, f32[192]{0:T(256)S(1)} %get-tuple-element.75), channel_id=1, replica_groups=mesh['x'=4,'y'=8,'c'=2,'mp'=8] {'y'}, use_global_device_ids=true, to_apply=%region_4.6 | all-reduce | flops 385 | bytes 3080 | tf_op jit(solution)/shard_map/psum | solution.py:49
  152.6 10.1 %all-reduce.6 = (f32[192]{0:T(256)S(1)}, f32[]{:T(128)}, f32[192]{0:T(256)S(1)}) all-reduce(f32[192]{0:T(256)S(1)} %get-tuple-element.63, f32[]{:T(128)} %get-tuple-element.64, f32[192]{0:T(256)S(1)} %get-tuple-element.65), channel_id=1, replica_groups=mesh['x'=4,'y'=8,'c'=2,'mp'=8] {'x'}, use_global_device_ids=true, to_apply=%region_5.7 | all-reduce | flops 385 | bytes 3080 | tf_op jit(solution)/shard_map/psum | solution.py:49
  163.4 2.4 all-gather.8.cloned.1.call-done
  165.8 4.0 %fusion.85 = (f32[192]{0:T(256)S(1)}, f32[192]{0:T(256)S(1)}, f32[1024,192]{0,1:T(8,128)}) fusion(f32[192]{0:T(256)S(1)} %get-tuple-element.78, f32[1024,192]{0,1:T(8,128)S(1)} %copy.51, f32[192]{0:T(256)S(1)} %get-tuple-element.79, f32[192]{0:T(256)} %param.25, f32[192]{0:T(256)} %param.24, f32[1024]{0:T(1024)S(1)} %reshape.354, ...), kind=kOutput, calls=%fused_computation.248 | convolution fusion | flops 607125120 | bytes 5317120 | tf_op jit(solution)/shard_map/dot_general | solution.py:193
  169.9 3.4 all-reduce.7
  173.3 13.0 %all-reduce.3 = (f32[192]{0:T(256)S(1)}, f32[192]{0:T(256)S(1)}) all-reduce(f32[192]{0:T(256)S(1)} %get-tuple-element.71, f32[192]{0:T(256)S(1)} %get-tuple-element.72), channel_id=1, replica_groups=mesh['x'=4,'y'=8,'c'=2,'mp'=8] {'y'}, use_global_device_ids=true, to_apply=%region_20.22 | all-reduce | flops 384 | bytes 3072 | tf_op jit(solution)/shard_map/psum | solution.py:49
  186.4 8.9 %all-reduce.5 = (f32[192]{0:T(256)}, f32[192]{0:T(256)S(1)}) all-reduce(f32[192]{0:T(256)S(1)} %get-tuple-element.61, f32[192]{0:T(256)S(1)} %get-tuple-element.62), channel_id=1, replica_groups=mesh['x'=4,'y'=8,'c'=2,'mp'=8] {'x'}, use_global_device_ids=true, to_apply=%region_21.23 | all-reduce | flops 384 | bytes 3072 | tf_op jit(solution)/shard_map/psum | solution.py:49
  196.0 3.6 multiply_reduce_fusion.32
  201.5 3.4 fusion.56
  206.1 1.6 multiply_reduce_fusion.3
  207.7 3.0 multiply_reduce_fusion.2
  210.9 1.9 multiply_convert_fusion.2
  213.3 1.8 fusion.68
  216.4 7.7 %collective-permute-start.6 = (f32[784,384]{1,0:T(8,128)}, f32[784,384]{1,0:T(8,128)S(1)}, u32[]{:S(2)}, u32[]{:S(2)}) collective-permute-start(f32[784,384]{1,0:T(8,128)} %pad_maximum_fusion), channel_id=1, source_target_pairs={{0,8},{8,0},{1,9},{9,1},{2,10},{10,2},{3,11},{11,3},{4,12},{12,4},... | collective-permute-start | bytes 3612680 | tf_op jit(solution)/shard_map/ppermute | solution.py:83
  224.2 2.7 collective-permute-done.6
  227.3 5.1 %collective-permute-start.7 = (f32[400,384]{1,0:T(8,128)S(1)}, f32[400,384]{1,0:T(8,128)S(1)}, u32[]{:S(2)}, u32[]{:S(2)}) collective-permute-start(f32[400,384]{1,0:T(8,128)S(1)} %pad_maximum_fusion.1), channel_id=1, source_target_pairs={{0,64},{16,80},{32,96},{48,112},{64,0},{80,16},{96,32},{112,48},{1... | collective-permute-start | bytes 1843208 | tf_op jit(solution)/shard_map/ppermute | solution.py:83
  232.4 29.1 %collective-permute-done.7 = f32[400,384]{1,0:T(8,128)S(1)} collective-permute-done((f32[400,384]{1,0:T(8,128)S(1)}, f32[400,384]{1,0:T(8,128)S(1)}, u32[]{:S(2)}, u32[]{:S(2)}) %collective-permute-start.7) | collective-permute-done | bytes 614432 | tf_op jit(solution)/shard_map/ppermute | solution.py:83
  262.4 1.9 collective-permute-start.8
  264.3 4.1 %fusion.89 = f32[1536,192]{0,1:T(8,128)} fusion(bf16[1024,1536]{0,1:T(8,128)(2,1)} %all-gather.6.cloned.1.call-done, bf16[1024,192]{0,1:T(8,128)(2,1)S(1)} %copy-done.6), kind=kOutput, calls=%fused_computation.252 | convolution fusion | flops 603979776 | bytes 4718592 | tf_op jit(solution)/shard_map/dot_general | solution.py:106
  268.5 12.8 %collective-permute-done.8 = f32[208,384]{1,0:T(8,128)S(1)} collective-permute-done((f32[208,384]{1,0:T(8,128)}, f32[208,384]{1,0:T(8,128)S(1)}, u32[]{:S(2)}, u32[]{:S(2)}) %collective-permute-start.8) | collective-permute-done | bytes 319520 | tf_op jit(solution)/shard_map/ppermute | solution.py:83
  281.4 1.9 collective-permute-start.9
  283.4 5.5 %collective-permute-done.9 = f32[112,384]{1,0:T(8,128)S(1)} collective-permute-done((f32[112,384]{1,0:T(8,128)S(1)}, f32[112,384]{1,0:T(8,128)S(1)}, u32[]{:S(2)}, u32[]{:S(2)}) %collective-permute-start.9) | collective-permute-done | bytes 172064 | tf_op jit(solution)/shard_map/ppermute | solution.py:83
  289.0 2.5 collective-permute-start.10
  291.4 4.4 %collective-permute-done.10 = f32[64,384]{1,0:T(8,128)S(1)} collective-permute-done((f32[64,384]{1,0:T(8,128)S(1)}, f32[64,384]{1,0:T(8,128)S(1)}, u32[]{:S(2)}, u32[]{:S(2)}) %collective-permute-start.10) | collective-permute-done | bytes 98336 | tf_op jit(solution)/shard_map/ppermute | solution.py:83
  295.9 1.9 copy.67
  297.9 1.9 collective-permute-start.11
  299.8 3.0 collective-permute-done.11
  304.3 27.2 %reduce-scatter.10.cloned.1.call-done = f32[48,192]{1,0:T(8,128)} async-done(((f32[384,192]{1,0:T(8,128)}), f32[48,192]{1,0:T(8,128)}) %reduce-scatter.10.cloned.1.call-update) | async-done | bytes 36880
  331.5 3.5 add_convert_fusion
  336.0 19.8 %reduce-scatter.12.cloned.1.call-done = f32[24,192]{1,0:T(8,128)} async-done(((f32[48,192]{1,0:T(8,128)}), f32[24,192]{1,0:T(8,128)}) %reduce-scatter.12.cloned.1.call-update) | async-done | bytes 18448
  (138 shorter events, 29.0 us)
Async XLA Ops:
  7.2 8.7 %copy-start = (s32[128]{0:T(128)S(1)}, s32[128]{0:T(128)}, u32[]{:S(2)}) copy-start(s32[128]{0:T(128)} %param.17) | copy-start | bytes 1540
  7.2 27.6 %copy-start.16 = (s32[1,64]{1,0:T(1,128)S(1)}, s32[1,64]{1,0:T(1,128)}, u32[]{:S(2)}) copy-start(s32[1,64]{1,0:T(1,128)} %param.16) | copy-start | bytes 772
  7.2 103.6 %all-gather.4.cloned.1.call-start = ((), (), s32[]{:S(2)}) async-start(), calls=%async_computation.6 | async-start | bytes 2396160 | tf_op jit(solution)/shard_map/all_gather | solution.py:133
  10.4 26.2 %collective-permute-start = (bf16[1,448,192]{1,2,0:T(8,128)(2,1)S(1)}, bf16[1,448,192]{1,2,0:T(8,128)(2,1)S(1)}, u32[]{:S(2)}, u32[]{:S(2)}) collective-permute-start(bf16[1,448,192]{1,2,0:T(8,128)(2,1)S(1)} %maximum_bitcast_fusion), channel_id=1, source_target_pairs={{0,1},{1,0},{2,3},{3,2},{4,5},{5,4},{6,7},{7,6},{8,9},{9,8},{10,11... | collective-permute-start | bytes 516104 | tf_op jit(solution)/shard_map/ppermute | solution.py:98
  19.5 25.6 %all-to-all-start.1 = ((s32[64,1,2]{2,1,0:T(1,128)}), s32[64,1,2]{2,1,0:T(1,128)S(1)}, u32[]{:S(2)}, u32[]{:S(2)}) async-start(s32[64,1,2]{2,1,0:T(1,128)} %copy.46), calls=%async_computation.1 | async-start | bytes 65536 | tf_op jit(solution)/shard_map/all_to_all | solution.py:131
  30.6 135.3 %all-gather.8.cloned.1.call-start = ((), (), s32[]{:S(2)}) async-start(), calls=%async_computation.8 | async-start | bytes 3538944 | tf_op jit(solution)/shard_map/all_gather | solution.py:191
  30.6 12.5 %collective-permute-start.3 = (f32[1,192]{1,0:T(1,128)}, f32[1,192]{1,0:T(1,128)S(1)}, u32[]{:S(2)}, u32[]{:S(2)}) collective-permute-start(f32[1,192]{1,0:T(1,128)} %bitcast.307), channel_id=1, source_target_pairs={{0,1},{1,0},{2,3},{3,2},{4,5},{5,4},{6,7},{7,6},{8,9},{9,8},{10,11... | collective-permute-start | bytes 2312 | tf_op jit(solution)/shard_map/ppermute | solution.py:98
  32.6 9.9 %copy-start.7 = (f32[31,192]{1,0:T(8,128)S(1)}, f32[31,192]{1,0:T(8,128)}, u32[]{:S(2)}) copy-start(f32[31,192]{1,0:T(8,128)} %param.23) | copy-start | bytes 71428
  32.6 10.5 %copy-start.15 = (f32[192]{0:T(256)S(1)}, f32[192]{0:T(256)}, u32[]{:S(2)}) copy-start(f32[192]{0:T(256)} %param.21) | copy-start | bytes 2308
  36.6 23.3 %collective-permute-start.1 = (bf16[2,448,192]{1,2,0:T(8,128)(2,1)S(1)}, bf16[2,448,192]{1,2,0:T(8,128)(2,1)S(1)}, u32[]{:S(2)}, u32[]{:S(2)}) collective-permute-start(bf16[2,448,192]{1,2,0:T(8,128)(2,1)S(1)} %maximum_select_fusion.2), channel_id=1, source_target_pairs={{0,2},{1,3},{2,0},{3,1},{4,6},{5,7},{6,4},{7,5},{8,10},{9,11},{10,... | collective-permute-start | bytes 1032200 | tf_op jit(solution)/shard_map/ppermute | solution.py:98
  43.1 25.2 %collective-permute-start.4 = (f32[2,192]{1,0:T(2,128)S(1)}, f32[2,192]{1,0:T(2,128)S(1)}, u32[]{:S(2)}, u32[]{:S(2)}) collective-permute-start(f32[2,192]{1,0:T(2,128)S(1)} %maximum_select_fusion.5), channel_id=1, source_target_pairs={{0,2},{1,3},{2,0},{3,1},{4,6},{5,7},{6,4},{7,5},{8,10},{9,11},{10,... | collective-permute-start | bytes 4616 | tf_op jit(solution)/shard_map/ppermute | solution.py:98
  45.1 58.0 %all-to-all-start = ((bf16[64,16,320]{2,1,0:T(8,128)(2,1)}), bf16[64,16,320]{2,1,0:T(8,128)(2,1)S(1)}, u32[]{:S(2)}, u32[]{:S(2)}) async-start(bf16[64,16,320]{2,1,0:T(8,128)(2,1)} %broadcast_select_fusion), calls=%async_computation | async-start | bytes 1572864 | tf_op jit(solution)/shard_map/all_to_all | solution.py:130
  60.1 42.0 %collective-permute-start.2 = (bf16[4,448,192]{1,2,0:T(8,128)(2,1)S(1)}, bf16[4,448,192]{1,2,0:T(8,128)(2,1)S(1)}, u32[]{:S(2)}, u32[]{:S(2)}) collective-permute-start(bf16[4,448,192]{1,2,0:T(8,128)(2,1)S(1)} %maximum_select_fusion.1), channel_id=1, source_target_pairs={{0,4},{1,5},{2,6},{3,7},{4,0},{5,1},{6,2},{7,3},{8,12},{9,13},{10,... | collective-permute-start | bytes 2064392 | tf_op jit(solution)/shard_map/ppermute | solution.py:98
  68.3 33.7 %collective-permute-start.5 = (f32[4,192]{1,0:T(4,128)S(1)}, f32[4,192]{1,0:T(4,128)S(1)}, u32[]{:S(2)}, u32[]{:S(2)}) collective-permute-start(f32[4,192]{1,0:T(4,128)S(1)} %maximum_select_fusion.4), channel_id=1, source_target_pairs={{0,4},{1,5},{2,6},{3,7},{4,0},{5,1},{6,2},{7,3},{8,12},{9,13},{10,... | collective-permute-start | bytes 9224 | tf_op jit(solution)/shard_map/ppermute | solution.py:98
  105.5 2.7 copy-start.1
  110.7 1.4 slice-start
  110.7 2.9 slice-start.1
  114.9 48.5 %all-to-all-start.2 = ((bf16[8,192,192]{1,2,0:T(8,128)(2,1)}), bf16[8,192,192]{1,2,0:T(8,128)(2,1)}, u32[]{:S(2)}, u32[]{:S(2)}) async-start(bf16[8,192,192]{1,2,0:T(8,128)(2,1)} %copy.54), calls=%async_computation.2 | async-start | bytes 1572864 | tf_op jit(solution)/shard_map/all_to_all | solution.py:192
  120.9 143.4 %all-gather.6.cloned.1.call-start = ((), (), s32[]{:S(2)}) async-start(), calls=%async_computation.7 | async-start | bytes 3538944 | tf_op jit(solution)/shard_map/all_gather | solution.py:186
  124.8 74.8 %copy-start.2 = (f32[1024,384]{0,1:T(8,128)}, f32[1024,384]{0,1:T(8,128)S(1)}, u32[]{:S(2)}) copy-start(f32[1024,384]{0,1:T(8,128)S(1)} %fusion.88) | copy-start | bytes 4718596
  163.4 6.5 %copy-start.13 = (f32[192]{0:T(256)}, f32[192]{0:T(256)S(1)}, u32[]{:S(2)}) copy-start(f32[192]{0:T(256)S(1)} %get-tuple-element.79) | copy-start | bytes 2308
  195.3 0.7 copy-start.14
  196.0 5.4 %copy-start.8 = (f32[1,192]{1,0:T(1,128)S(1)}, f32[1,192]{1,0:T(1,128)}, u32[]{:S(2)}) copy-start(f32[1,192]{1,0:T(1,128)} %get-tuple-element.106) | copy-start | bytes 2308
  196.0 5.4 %copy-start.9 = (f32[1,192]{1,0:T(1,128)S(1)}, f32[1,192]{1,0:T(1,128)}, u32[]{:S(2)}) copy-start(f32[1,192]{1,0:T(1,128)} %get-tuple-element.107) | copy-start | bytes 2308
  196.0 5.4 %copy-start.10 = (f32[1,192]{1,0:T(1,128)S(1)}, f32[1,192]{1,0:T(1,128)}, u32[]{:S(2)}) copy-start(f32[1,192]{1,0:T(1,128)} %get-tuple-element.108) | copy-start | bytes 2308
  196.0 5.4 %copy-start.11 = (f32[1,192]{1,0:T(1,128)S(1)}, f32[1,192]{1,0:T(1,128)}, u32[]{:S(2)}) copy-start(f32[1,192]{1,0:T(1,128)} %get-tuple-element.109) | copy-start | bytes 2308
  196.0 5.4 %copy-start.12 = (f32[1,192]{1,0:T(1,128)S(1)}, f32[1,192]{1,0:T(1,128)}, u32[]{:S(2)}) copy-start(f32[1,192]{1,0:T(1,128)} %get-tuple-element.110) | copy-start | bytes 2308
  201.1 94.8 %reduce-scatter.8.cloned.1.call-start = ((), (), s32[]{:S(2)}) async-start(), calls=%async_computation.9 | async-start | bytes 1474560 | tf_op jit(solution)/shard_map/reduce_scatter | solution.py:61
  206.1 4.9 %copy-start.4 = (f32[1024,192]{0,1:T(8,128)S(1)}, f32[1024,192]{0,1:T(8,128)}, u32[]{:S(2)}) copy-start(f32[1024,192]{0,1:T(8,128)} %copy.57) | copy-start | bytes 2359300
  210.9 2.4 copy-start.5
  216.4 10.4 %collective-permute-start.6 = (f32[784,384]{1,0:T(8,128)}, f32[784,384]{1,0:T(8,128)S(1)}, u32[]{:S(2)}, u32[]{:S(2)}) collective-permute-start(f32[784,384]{1,0:T(8,128)} %pad_maximum_fusion), channel_id=1, source_target_pairs={{0,8},{8,0},{1,9},{9,1},{2,10},{10,2},{3,11},{11,3},{4,12},{12,4},... | collective-permute-start | bytes 3612680 | tf_op jit(solution)/shard_map/ppermute | solution.py:83
  227.2 37.1 %copy-start.6 = (bf16[1024,192]{0,1:T(8,128)(2,1)S(1)}, bf16[1024,192]{0,1:T(8,128)(2,1)}, u32[]{:S(2)}) copy-start(bf16[1024,192]{0,1:T(8,128)(2,1)} %param.27) | copy-start | bytes 1179652
  227.3 34.2 %collective-permute-start.7 = (f32[400,384]{1,0:T(8,128)S(1)}, f32[400,384]{1,0:T(8,128)S(1)}, u32[]{:S(2)}, u32[]{:S(2)}) collective-permute-start(f32[400,384]{1,0:T(8,128)S(1)} %pad_maximum_fusion.1), channel_id=1, source_target_pairs={{0,64},{16,80},{32,96},{48,112},{64,0},{80,16},{96,32},{112,48},{1... | collective-permute-start | bytes 1843208 | tf_op jit(solution)/shard_map/ppermute | solution.py:83
  262.4 18.9 %collective-permute-start.8 = (f32[208,384]{1,0:T(8,128)}, f32[208,384]{1,0:T(8,128)S(1)}, u32[]{:S(2)}, u32[]{:S(2)}) collective-permute-start(f32[208,384]{1,0:T(8,128)} %pad_maximum_fusion.2), channel_id=1, source_target_pairs={{0,32},{16,48},{32,0},{48,16},{64,96},{80,112},{96,64},{112,80},{1... | collective-permute-start | bytes 958472 | tf_op jit(solution)/shard_map/ppermute | solution.py:83
  268.5 63.1 %copy-start.3 = (bf16[1536,3,192]{2,0,1:T(8,128)(2,1)S(1)}, bf16[1536,3,192]{2,0,1:T(8,128)(2,1)}, u32[]{:S(2)}) copy-start(bf16[1536,3,192]{2,0,1:T(8,128)(2,1)} %all-gather.4.cloned.1.call-done) | copy-start | bytes 5308420
  268.5 63.0 %reduce-scatter.10.cloned.1.call-start = ((), (), s32[]{:S(2)}) async-start(), calls=%async_computation.10 | async-start | bytes 442368
  281.4 7.4 %collective-permute-start.9 = (f32[112,384]{1,0:T(8,128)S(1)}, f32[112,384]{1,0:T(8,128)S(1)}, u32[]{:S(2)}, u32[]{:S(2)}) collective-permute-start(f32[112,384]{1,0:T(8,128)S(1)} %pad_maximum_fusion.3), channel_id=1, source_target_pairs={{0,16},{16,0},{32,48},{48,32},{64,80},{80,64},{96,112},{112,96},{1... | collective-permute-start | bytes 516104 | tf_op jit(solution)/shard_map/ppermute | solution.py:83
  289.0 6.9 %collective-permute-start.10 = (f32[64,384]{1,0:T(8,128)S(1)}, f32[64,384]{1,0:T(8,128)S(1)}, u32[]{:S(2)}, u32[]{:S(2)}) collective-permute-start(f32[64,384]{1,0:T(8,128)S(1)} %pad_maximum_fusion.4), channel_id=1, source_target_pairs={{0,256},{128,384},{256,0},{384,128},{1,257},{129,385},{257,1},{385... | collective-permute-start | bytes 294920 | tf_op jit(solution)/shard_map/ppermute | solution.py:83
  297.8 58.0 %reduce-scatter.12.cloned.1.call-start = ((), (), s32[]{:S(2)}) async-start(), calls=%async_computation.11 | async-start | bytes 73728
  297.9 5.0 %collective-permute-start.11 = (f32[40,384]{1,0:T(8,128)S(1)}, f32[40,384]{1,0:T(8,128)S(1)}, u32[]{:S(2)}, u32[]{:S(2)}) collective-permute-start(f32[40,384]{1,0:T(8,128)S(1)} %pad_maximum_fusion.5), channel_id=1, source_target_pairs={{0,128},{128,0},{256,384},{384,256},{1,129},{129,1},{257,385},{385... | collective-permute-start | bytes 184328 | tf_op jit(solution)/shard_map/ppermute | solution.py:83
Sparse Core Ops, SparseCore 0:
  11.8 88.8 all-gather.3
  102.8 62.9 all-gather.7
  201.3 47.4 all-gather.5
  268.6 22.9 reduce-scatter.7
  297.9 33.5 reduce-scatter.9
  334.7 21.0 reduce-scatter.11

commit v6 on v5

--- a/solution.py
+++ b/solution.py
@@ -65,7 +65,7 @@
 def halving_scatter(value, sizes, extra):
     cols = value.shape[1:]
     cur = value.reshape(tuple(sizes[a] for a in DP_AXES) + (-1,) + cols)
-    rows = extra.shape[0]
+    rows = None if extra is None else extra.shape[0]
     for dim, name in reversed(list(enumerate(DP_AXES))):
         length = sizes[name]
         me = lax.axis_index(name)
@@ -79,10 +79,13 @@
             keep = lax.dynamic_index_in_dim(pieces, mine, dim + 1, keepdims=False)
             send = lax.dynamic_index_in_dim(pieces, 1 - mine, dim + 1, keepdims=False)
             perm = [(i, i ^ (1 << bit)) for i in range(length)]
-            message = jnp.concatenate([send.reshape((-1,) + cols), extra], 0)
-            got = lax.ppermute(message, name, perm)
-            merged = keep + got[:-rows].reshape(send.shape)
-            extra = extra + got[-rows:]
+            if extra is None:
+                merged = keep + lax.ppermute(send, name, perm)
+            else:
+                message = jnp.concatenate([send.reshape((-1,) + cols), extra], 0)
+                got = lax.ppermute(message, name, perm)
+                merged = keep + got[:-rows].reshape(send.shape)
+                extra = extra + got[-rows:]
             cur = merged.reshape(shape[:dim] + (span // 2,) + shape[dim + 1 :])
             bit -= 1
     return cur.reshape((-1,) + cols), extra
@@ -187,7 +190,8 @@
     encoded = (
         inputs + jnp.dot(hidden_full, weights_two, preferred_element_type=jnp.float32)
     ).astype(jnp.bfloat16)
-    grad_pw2 = dp_scatter(contract_rows(hidden_full, cotangent))
+    sizes = {name: lax.axis_size(name) for name in DP_AXES}
+    grad_pw2, _ = halving_scatter(contract_rows(hidden_full, cotangent), sizes, None)
     cot_full = lax.all_gather(cotangent, "mp", axis=1, tiled=True)
     weights_rows = lax.all_to_all(weights_two, "mp", split_axis=0, concat_axis=1, tiled=True)
     dhidden = lax.dot_general(

time: 364 us -> 363 us (level)
  starting transfers between devices: 73.9 us -> 91.9 us
  waiting for transfers between devices: 142 us -> 125 us
    unnamed x8 -> x3, waiting for transfers between devices: 47.1 us -> 0.05 us
    ppermute x0 -> x6, waiting for transfers between devices: none -> 33.2 us  [halving_scatter(): merged = keep + lax.ppermute(send, name, perm)]
    ppermute x0 -> x6, starting transfers between devices: none -> 18.5 us  [halving_scatter(): merged = keep + lax.ppermute(send, name, perm)]
    unnamed x39 -> x36, local copies, waits for them, and re-layouts: 10.3 us -> 8.45 us
  transfers between devices with their start and end apart: 21 -> 24, of which waited for: 11 -> 11; matrix products, arithmetic and copies ran while one was open for 16% -> 13% of each run, Pallas kernels for 0% -> 0%
where the time goes in v6:
time: 363 us; the launch traced here: 360 us
  waiting for transfers between devices  125 us (34%)
  starting transfers between devices  91.9 us (25%)
  blocking collectives  55.2 us (15%)
  other arithmetic  32.4 us (9%)
  local copies, waits for them, and re-layouts  22.7 us (6%)
  matrix products  18.5 us (5%)
  between operations  14.7 us (4%)
    psum x6, blocking collectives, dp_sum(): value = lax.psum(value, name)  55.2 us
    ppermute x6, waiting for transfers between devices, halving_scatter(): got = lax.ppermute(message, name, perm)  54.1 us
    ppermute x6, waiting for transfers between devices, doubling_gather(): got = lax.ppermute(cur, name, perm)  35.2 us
    ppermute x6, waiting for transfers between devices, halving_scatter(): merged = keep + lax.ppermute(send, name, perm)  33.2 us
    ppermute x6, starting transfers between devices, doubling_gather(): got = lax.ppermute(cur, name, perm)  24.5 us
    ppermute x6, starting transfers between devices, halving_scatter(): got = lax.ppermute(message, name, perm)  20.9 us
    ppermute x6, starting transfers between devices, halving_scatter(): merged = keep + lax.ppermute(send, name, perm)  18.5 us
    all_to_all x1, starting transfers between devices, on_device(): lax.all_to_all(meta_send, DP_AXES, split_axis=0, concat_axis=0, tiled=True)  11.1 us
  transfers between devices with their start and end apart: 24, of which 11 were waited for; matrix products, arithmetic and copies ran while one was open for 13% of the time, Pallas kernels for 0%

profile of v6, /device:TPU:1, one launch (start us, length us, event | category | flops | bytes accessed | tf_op | source)
XLA Modules:
  0.0 360.3 jit_solution(1503472718862800708)
XLA Ops:
  10.4 4.8 %collective-permute-start = (bf16[1,448,192]{1,2,0:T(8,128)(2,1)S(1)}, bf16[1,448,192]{1,2,0:T(8,128)(2,1)S(1)}, u32[]{:S(2)}, u32[]{:S(2)}) collective-permute-start(bf16[1,448,192]{1,2,0:T(8,128)(2,1)S(1)} %maximum_bitcast_fusion), channel_id=1, source_target_pairs={{0,1},{1,0},{2,3},{3,2},{4,5},{5,4},{6,7},{7,6},{8,9},{9,8},{10,11... | collective-permute-start | bytes 516104 | tf_op jit(solution)/shard_map/ppermute | solution.py:101
  19.5 11.1 %all-to-all-start.1 = ((s32[64,1,2]{2,1,0:T(1,128)}), s32[64,1,2]{2,1,0:T(1,128)S(1)}, u32[]{:S(2)}, u32[]{:S(2)}) async-start(s32[64,1,2]{2,1,0:T(1,128)} %copy.63), calls=%async_computation.1 | async-start | bytes 65536 | tf_op jit(solution)/shard_map/all_to_all | solution.py:134
  30.6 1.9 collective-permute-start.3
  32.6 2.1 copy.62
  36.7 5.8 %collective-permute-start.1 = (bf16[2,448,192]{1,2,0:T(8,128)(2,1)S(1)}, bf16[2,448,192]{1,2,0:T(8,128)(2,1)S(1)}, u32[]{:S(2)}, u32[]{:S(2)}) collective-permute-start(bf16[2,448,192]{1,2,0:T(8,128)(2,1)S(1)} %maximum_select_fusion.2), channel_id=1, source_target_pairs={{0,2},{1,3},{2,0},{3,1},{4,6},{5,7},{6,4},{7,5},{8,10},{9,11},{10,... | collective-permute-start | bytes 1032200 | tf_op jit(solution)/shard_map/ppermute | solution.py:101
  43.1 1.9 collective-permute-start.4
  45.1 10.6 %all-to-all-start = ((bf16[64,16,320]{2,1,0:T(8,128)(2,1)}), bf16[64,16,320]{2,1,0:T(8,128)(2,1)S(1)}, u32[]{:S(2)}, u32[]{:S(2)}) async-start(bf16[64,16,320]{2,1,0:T(8,128)(2,1)} %broadcast_select_fusion), calls=%async_computation | async-start | bytes 1572864 | tf_op jit(solution)/shard_map/all_to_all | solution.py:133
  55.8 4.2 %collective-permute-done.1 = bf16[2,448,192]{1,2,0:T(8,128)(2,1)S(1)} collective-permute-done((bf16[2,448,192]{1,2,0:T(8,128)(2,1)S(1)}, bf16[2,448,192]{1,2,0:T(8,128)(2,1)S(1)}, u32[]{:S(2)}, u32[]{:S(2)}) %collective-permute-start.1) | collective-permute-done | bytes 344096 | tf_op jit(solution)/shard_map/ppermute | solution.py:101
  60.2 8.1 %collective-permute-start.2 = (bf16[4,448,192]{1,2,0:T(8,128)(2,1)S(1)}, bf16[4,448,192]{1,2,0:T(8,128)(2,1)S(1)}, u32[]{:S(2)}, u32[]{:S(2)}) collective-permute-start(bf16[4,448,192]{1,2,0:T(8,128)(2,1)S(1)} %maximum_select_fusion.1), channel_id=1, source_target_pairs={{0,4},{1,5},{2,6},{3,7},{4,0},{5,1},{6,2},{7,3},{8,12},{9,13},{10,... | collective-permute-start | bytes 2064392 | tf_op jit(solution)/shard_map/ppermute | solution.py:101
  68.4 1.9 collective-permute-start.5
  71.0 31.0 %collective-permute-done.5 = f32[4,192]{1,0:T(4,128)S(1)} collective-permute-done((f32[4,192]{1,0:T(4,128)S(1)}, f32[4,192]{1,0:T(4,128)S(1)}, u32[]{:S(2)}, u32[]{:S(2)}) %collective-permute-start.5) | collective-permute-done | bytes 3104 | tf_op jit(solution)/shard_map/ppermute | solution.py:101
  103.3 2.2 fusion.84
  105.6 2.6 copy-done.2
  108.2 2.6 multiply_convert_fusion
  114.9 6.1 %all-to-all-start.2 = ((bf16[8,192,192]{1,2,0:T(8,128)(2,1)}), bf16[8,192,192]{1,2,0:T(8,128)(2,1)}, u32[]{:S(2)}, u32[]{:S(2)}) async-start(bf16[8,192,192]{1,2,0:T(8,128)(2,1)} %copy.71), calls=%async_computation.2 | async-start | bytes 1572864 | tf_op jit(solution)/shard_map/all_to_all | solution.py:196
  121.1 3.7 %fusion.88 = f32[1024,384]{0,1:T(8,128)S(1)} fusion(bf16[1024,1536]{1,0:T(8,128)(2,1)} %multiply_convert_fusion, bf16[1536,384]{0,1:T(8,128)(2,1)} %bitcast.234), kind=kOutput, calls=%fused_computation.263 | convolution fusion | flops 1207959552 | bytes 5898240 | tf_op jit(solution)/shard_map/dot_general | solution.py:168
  125.4 6.0 %fusion.4 = (f32[192]{0:T(256)}, f32[192]{0:T(256)}, f32[64,16,192]{2,1,0:T(8,128)}) fusion(f32[64,16]{1,0:T(8,128)S(1)} %get-tuple-element.133, f32[192]{0:T(256)S(1)} %bitcast.265, f32[192]{0:T(256)S(1)} %bitcast.267, f32[192]{0:T(256)S(1)} %bitcast.271, f32[192]{0:T(256)S(1)} %bitcast.273, f32[192]{0:T(256)S(1)} %bitcast.275, f32[192]{0:T(256)S(1)} %bitcast.277, ...), kind=kLoop, calls=%fused_computation.75 | loop fusion | flops 12779136 | bytes 1602304 | tf_op jit(solution)/shard_map/reduce_sum | solution.py:177
  132.9 4.2 %all-reduce.8 = (f32[192]{0:T(256)S(1)}, f32[]{:T(128)}, f32[192]{0:T(256)S(1)}) all-reduce(f32[192]{0:T(256)} %get-tuple-element.64, f32[]{:T(128)} %fusion.78, f32[192]{0:T(256)} %get-tuple-element.63), channel_id=1, replica_groups=mesh['x'=4,'y'=8,'c'=2,'mp'=8] {'c'}, use_global_device_ids=true, to_apply=%region_3.5 | all-reduce | flops 385 | bytes 3080 | tf_op jit(solution)/shard_map/psum | solution.py:49
  137.1 15.4 %all-reduce.4 = (f32[192]{0:T(256)S(1)}, f32[]{:T(128)}, f32[192]{0:T(256)S(1)}) all-reduce(f32[192]{0:T(256)S(1)} %get-tuple-element.79, f32[]{:T(128)} %get-tuple-element.80, f32[192]{0:T(256)S(1)} %get-tuple-element.81), channel_id=1, replica_groups=mesh['x'=4,'y'=8,'c'=2,'mp'=8] {'y'}, use_global_device_ids=true, to_apply=%region_4.6 | all-reduce | flops 385 | bytes 3080 | tf_op jit(solution)/shard_map/psum | solution.py:49
  152.6 10.1 %all-reduce.6 = (f32[192]{0:T(256)S(1)}, f32[]{:T(128)}, f32[192]{0:T(256)S(1)}) all-reduce(f32[192]{0:T(256)S(1)} %get-tuple-element.69, f32[]{:T(128)} %get-tuple-element.70, f32[192]{0:T(256)S(1)} %get-tuple-element.71), channel_id=1, replica_groups=mesh['x'=4,'y'=8,'c'=2,'mp'=8] {'x'}, use_global_device_ids=true, to_apply=%region_5.7 | all-reduce | flops 385 | bytes 3080 | tf_op jit(solution)/shard_map/psum | solution.py:49
  163.4 2.4 all-gather.8.cloned.1.call-done
  165.7 4.0 %fusion.85 = (f32[192]{0:T(256)S(1)}, f32[192]{0:T(256)S(1)}, f32[1024,192]{0,1:T(8,128)}) fusion(f32[192]{0:T(256)S(1)} %get-tuple-element.84, f32[1024,192]{0,1:T(8,128)S(1)} %copy.68, f32[192]{0:T(256)S(1)} %get-tuple-element.85, f32[192]{0:T(256)} %param.25, f32[192]{0:T(256)} %param.24, f32[1024]{0:T(1024)S(1)} %reshape.362, ...), kind=kOutput, calls=%fused_computation.260 | convolution fusion | flops 607125120 | bytes 5317120 | tf_op jit(solution)/shard_map/dot_general | solution.py:197
  169.8 3.5 all-reduce.7
  173.3 13.0 %all-reduce.3 = (f32[192]{0:T(256)S(1)}, f32[192]{0:T(256)S(1)}) all-reduce(f32[192]{0:T(256)S(1)} %get-tuple-element.77, f32[192]{0:T(256)S(1)} %get-tuple-element.78), channel_id=1, replica_groups=mesh['x'=4,'y'=8,'c'=2,'mp'=8] {'y'}, use_global_device_ids=true, to_apply=%region_20.22 | all-reduce | flops 384 | bytes 3072 | tf_op jit(solution)/shard_map/psum | solution.py:49
  186.2 9.0 %all-reduce.5 = (f32[192]{0:T(256)}, f32[192]{0:T(256)S(1)}) all-reduce(f32[192]{0:T(256)S(1)} %get-tuple-element.67, f32[192]{0:T(256)S(1)} %get-tuple-element.68), channel_id=1, replica_groups=mesh['x'=4,'y'=8,'c'=2,'mp'=8] {'x'}, use_global_device_ids=true, to_apply=%region_21.23 | all-reduce | flops 384 | bytes 3072 | tf_op jit(solution)/shard_map/psum | solution.py:49
  195.9 3.6 multiply_reduce_fusion.32
  202.7 3.4 fusion.56
  207.3 3.0 multiply_reduce_fusion.2
  216.0 7.7 %collective-permute-start.6 = (f32[784,384]{1,0:T(8,128)}, f32[784,384]{1,0:T(8,128)S(1)}, u32[]{:S(2)}, u32[]{:S(2)}) collective-permute-start(f32[784,384]{1,0:T(8,128)} %pad_maximum_fusion), channel_id=1, source_target_pairs={{0,8},{8,0},{1,9},{9,1},{2,10},{10,2},{3,11},{11,3},{4,12},{12,4},... | collective-permute-start | bytes 3612680 | tf_op jit(solution)/shard_map/ppermute | solution.py:86
  223.8 2.7 collective-permute-done.6
  226.8 4.8 %collective-permute-start.7 = (f32[400,384]{1,0:T(8,128)S(1)}, f32[400,384]{1,0:T(8,128)S(1)}, u32[]{:S(2)}, u32[]{:S(2)}) collective-permute-start(f32[400,384]{1,0:T(8,128)S(1)} %pad_maximum_fusion.1), channel_id=1, source_target_pairs={{0,64},{16,80},{32,96},{48,112},{64,0},{80,16},{96,32},{112,48},{1... | collective-permute-start | bytes 1843208 | tf_op jit(solution)/shard_map/ppermute | solution.py:86
  231.7 29.4 %collective-permute-done.7 = f32[400,384]{1,0:T(8,128)S(1)} collective-permute-done((f32[400,384]{1,0:T(8,128)S(1)}, f32[400,384]{1,0:T(8,128)S(1)}, u32[]{:S(2)}, u32[]{:S(2)}) %collective-permute-start.7) | collective-permute-done | bytes 614432 | tf_op jit(solution)/shard_map/ppermute | solution.py:86
  261.3 1.9 collective-permute-start.8
  263.2 16.6 %collective-permute-done.8 = f32[208,384]{1,0:T(8,128)S(1)} collective-permute-done((f32[208,384]{1,0:T(8,128)S(1)}, f32[208,384]{1,0:T(8,128)S(1)}, u32[]{:S(2)}, u32[]{:S(2)}) %collective-permute-start.8) | collective-permute-done | bytes 319520 | tf_op jit(solution)/shard_map/ppermute | solution.py:86
  280.0 1.9 collective-permute-start.9
  281.9 5.4 %collective-permute-done.9 = f32[112,384]{1,0:T(8,128)S(1)} collective-permute-done((f32[112,384]{1,0:T(8,128)S(1)}, f32[112,384]{1,0:T(8,128)S(1)}, u32[]{:S(2)}, u32[]{:S(2)}) %collective-permute-start.9) | collective-permute-done | bytes 172064 | tf_op jit(solution)/shard_map/ppermute | solution.py:86
  287.4 2.9 fusion.89
  290.3 3.3 collective-permute-start.12
  293.7 2.6 collective-permute-start.10
  296.5 5.2 %collective-permute-start.13 = (f32[4,1,4,1,24,192]{5,4,2,0,3,1:T(8,128)S(1)}, f32[4,1,4,1,24,192]{5,4,2,0,3,1:T(8,128)S(1)}, u32[]{:S(2)}, u32[]{:S(2)}) collective-permute-start(f32[4,1,4,1,24,192]{5,4,2,0,3,1:T(8,128)S(1)} %dynamic-slice_bitcast_fusion.1), channel_id=1, source_target_pairs={{0,64},{16,80},{32,96},{48,112},{64,0},{80,16},{96,32},{112,48},{1... | collective-permute-start | bytes 884744 | tf_op jit(solution)/shard_map/ppermute | solution.py:83
  301.7 19.4 %collective-permute-done.13 = f32[4,1,4,1,24,192]{5,4,2,0,3,1:T(8,128)S(1)} collective-permute-done((f32[4,1,4,1,24,192]{5,4,2,0,3,1:T(8,128)S(1)}, f32[4,1,4,1,24,192]{5,4,2,0,3,1:T(8,128)S(1)}, u32[]{:S(2)}, u32[]{:S(2)}) %collective-permute-start.13) | collective-permute-done | bytes 294944 | tf_op jit(solution)/shard_map/ppermute | solution.py:83
  321.2 1.9 collective-permute-start.14
  325.1 9.5 %collective-permute-done.14 = f32[4,1,2,1,24,192]{5,4,2,0,3,1:T(8,128)S(1)} collective-permute-done((f32[4,1,2,1,24,192]{5,4,2,0,3,1:T(8,128)S(1)}, f32[4,1,2,1,24,192]{5,4,2,0,3,1:T(8,128)S(1)}, u32[]{:S(2)}, u32[]{:S(2)}) %collective-permute-start.14) | collective-permute-done | bytes 147488 | tf_op jit(solution)/shard_map/ppermute | solution.py:83
  334.6 1.9 collective-permute-start.15
  336.6 3.8 %collective-permute-done.15 = f32[4,1,1,1,24,192]{5,4,2,0,3,1:T(8,128)S(1)} collective-permute-done((f32[4,1,1,1,24,192]{5,4,2,0,3,1:T(8,128)S(1)}, f32[4,1,1,1,24,192]{5,4,2,0,3,1:T(8,128)S(1)}, u32[]{:S(2)}, u32[]{:S(2)}) %collective-permute-start.15) | collective-permute-done | bytes 73760 | tf_op jit(solution)/shard_map/ppermute | solution.py:83
  340.4 4.3 %collective-permute-start.16 = (f32[1,2,1,1,24,192]{5,4,3,2,1,0:T(8,128)S(1)}, f32[1,2,1,1,24,192]{5,4,3,2,1,0:T(8,128)S(1)}, u32[]{:S(2)}, u32[]{:S(2)}) collective-permute-start(f32[1,2,1,1,24,192]{5,4,3,2,1,0:T(8,128)S(1)} %dynamic-slice_bitcast_fusion.3), channel_id=1, source_target_pairs={{0,256},{128,384},{256,0},{384,128},{1,257},{129,385},{257,1},{385... | collective-permute-start | bytes 110600 | tf_op jit(solution)/shard_map/ppermute | solution.py:83
  346.8 1.9 collective-permute-start.17
  348.7 3.5 add_convert_fusion
  (150 shorter events, 36.9 us)
Async XLA Ops:
  7.2 8.7 %copy-start = (s32[128]{0:T(128)S(1)}, s32[128]{0:T(128)}, u32[]{:S(2)}) copy-start(s32[128]{0:T(128)} %param.17) | copy-start | bytes 1540
  7.2 27.6 %copy-start.15 = (s32[1,64]{1,0:T(1,128)S(1)}, s32[1,64]{1,0:T(1,128)}, u32[]{:S(2)}) copy-start(s32[1,64]{1,0:T(1,128)} %param.16) | copy-start | bytes 772
  7.2 103.6 %all-gather.4.cloned.1.call-start = ((), (), s32[]{:S(2)}) async-start(), calls=%async_computation.3 | async-start | bytes 2396160 | tf_op jit(solution)/shard_map/all_gather | solution.py:136
  10.4 26.2 %collective-permute-start = (bf16[1,448,192]{1,2,0:T(8,128)(2,1)S(1)}, bf16[1,448,192]{1,2,0:T(8,128)(2,1)S(1)}, u32[]{:S(2)}, u32[]{:S(2)}) collective-permute-start(bf16[1,448,192]{1,2,0:T(8,128)(2,1)S(1)} %maximum_bitcast_fusion), channel_id=1, source_target_pairs={{0,1},{1,0},{2,3},{3,2},{4,5},{5,4},{6,7},{7,6},{8,9},{9,8},{10,11... | collective-permute-start | bytes 516104 | tf_op jit(solution)/shard_map/ppermute | solution.py:101
  19.5 25.6 %all-to-all-start.1 = ((s32[64,1,2]{2,1,0:T(1,128)}), s32[64,1,2]{2,1,0:T(1,128)S(1)}, u32[]{:S(2)}, u32[]{:S(2)}) async-start(s32[64,1,2]{2,1,0:T(1,128)} %copy.63), calls=%async_computation.1 | async-start | bytes 65536 | tf_op jit(solution)/shard_map/all_to_all | solution.py:134
  30.6 135.2 %all-gather.8.cloned.1.call-start = ((), (), s32[]{:S(2)}) async-start(), calls=%async_computation.5 | async-start | bytes 3538944 | tf_op jit(solution)/shard_map/all_gather | solution.py:195
  30.6 12.5 %collective-permute-start.3 = (f32[1,192]{1,0:T(1,128)}, f32[1,192]{1,0:T(1,128)S(1)}, u32[]{:S(2)}, u32[]{:S(2)}) collective-permute-start(f32[1,192]{1,0:T(1,128)} %bitcast.339), channel_id=1, source_target_pairs={{0,1},{1,0},{2,3},{3,2},{4,5},{5,4},{6,7},{7,6},{8,9},{9,8},{10,11... | collective-permute-start | bytes 2312 | tf_op jit(solution)/shard_map/ppermute | solution.py:101
  32.6 9.9 %copy-start.8 = (f32[31,192]{1,0:T(8,128)S(1)}, f32[31,192]{1,0:T(8,128)}, u32[]{:S(2)}) copy-start(f32[31,192]{1,0:T(8,128)} %param.23) | copy-start | bytes 71428
  32.6 10.5 %copy-start.14 = (f32[192]{0:T(256)S(1)}, f32[192]{0:T(256)}, u32[]{:S(2)}) copy-start(f32[192]{0:T(256)} %param.21) | copy-start | bytes 2308
  36.7 23.3 %collective-permute-start.1 = (bf16[2,448,192]{1,2,0:T(8,128)(2,1)S(1)}, bf16[2,448,192]{1,2,0:T(8,128)(2,1)S(1)}, u32[]{:S(2)}, u32[]{:S(2)}) collective-permute-start(bf16[2,448,192]{1,2,0:T(8,128)(2,1)S(1)} %maximum_select_fusion.2), channel_id=1, source_target_pairs={{0,2},{1,3},{2,0},{3,1},{4,6},{5,7},{6,4},{7,5},{8,10},{9,11},{10,... | collective-permute-start | bytes 1032200 | tf_op jit(solution)/shard_map/ppermute | solution.py:101
  43.1 25.2 %collective-permute-start.4 = (f32[2,192]{1,0:T(2,128)S(1)}, f32[2,192]{1,0:T(2,128)S(1)}, u32[]{:S(2)}, u32[]{:S(2)}) collective-permute-start(f32[2,192]{1,0:T(2,128)S(1)} %maximum_select_fusion.5), channel_id=1, source_target_pairs={{0,2},{1,3},{2,0},{3,1},{4,6},{5,7},{6,4},{7,5},{8,10},{9,11},{10,... | collective-permute-start | bytes 4616 | tf_op jit(solution)/shard_map/ppermute | solution.py:101
  45.1 58.0 %all-to-all-start = ((bf16[64,16,320]{2,1,0:T(8,128)(2,1)}), bf16[64,16,320]{2,1,0:T(8,128)(2,1)S(1)}, u32[]{:S(2)}, u32[]{:S(2)}) async-start(bf16[64,16,320]{2,1,0:T(8,128)(2,1)} %broadcast_select_fusion), calls=%async_computation | async-start | bytes 1572864 | tf_op jit(solution)/shard_map/all_to_all | solution.py:133
  60.2 42.0 %collective-permute-start.2 = (bf16[4,448,192]{1,2,0:T(8,128)(2,1)S(1)}, bf16[4,448,192]{1,2,0:T(8,128)(2,1)S(1)}, u32[]{:S(2)}, u32[]{:S(2)}) collective-permute-start(bf16[4,448,192]{1,2,0:T(8,128)(2,1)S(1)} %maximum_select_fusion.1), channel_id=1, source_target_pairs={{0,4},{1,5},{2,6},{3,7},{4,0},{5,1},{6,2},{7,3},{8,12},{9,13},{10,... | collective-permute-start | bytes 2064392 | tf_op jit(solution)/shard_map/ppermute | solution.py:101
  68.4 33.7 %collective-permute-start.5 = (f32[4,192]{1,0:T(4,128)S(1)}, f32[4,192]{1,0:T(4,128)S(1)}, u32[]{:S(2)}, u32[]{:S(2)}) collective-permute-start(f32[4,192]{1,0:T(4,128)S(1)} %maximum_select_fusion.4), channel_id=1, source_target_pairs={{0,4},{1,5},{2,6},{3,7},{4,0},{5,1},{6,2},{7,3},{8,12},{9,13},{10,... | collective-permute-start | bytes 9224 | tf_op jit(solution)/shard_map/ppermute | solution.py:101
  105.5 2.7 copy-start.2
  110.8 1.4 slice-start
  110.8 2.9 slice-start.1
  114.9 48.5 %all-to-all-start.2 = ((bf16[8,192,192]{1,2,0:T(8,128)(2,1)}), bf16[8,192,192]{1,2,0:T(8,128)(2,1)}, u32[]{:S(2)}, u32[]{:S(2)}) async-start(bf16[8,192,192]{1,2,0:T(8,128)(2,1)} %copy.71), calls=%async_computation.2 | async-start | bytes 1572864 | tf_op jit(solution)/shard_map/all_to_all | solution.py:196
  120.9 166.4 %all-gather.6.cloned.1.call-start = ((), (), s32[]{:S(2)}) async-start(), calls=%async_computation.4 | async-start | bytes 3538944 | tf_op jit(solution)/shard_map/all_gather | solution.py:189
  124.8 74.7 %copy-start.3 = (f32[1024,384]{0,1:T(8,128)}, f32[1024,384]{0,1:T(8,128)S(1)}, u32[]{:S(2)}) copy-start(f32[1024,384]{0,1:T(8,128)S(1)} %fusion.88) | copy-start | bytes 4718596
  195.2 0.7 copy-start.13
  195.9 6.8 %copy-start.9 = (f32[1,192]{1,0:T(1,128)S(1)}, f32[1,192]{1,0:T(1,128)}, u32[]{:S(2)}) copy-start(f32[1,192]{1,0:T(1,128)} %get-tuple-element.113) | copy-start | bytes 2308
  195.9 6.8 %copy-start.10 = (f32[1,192]{1,0:T(1,128)S(1)}, f32[1,192]{1,0:T(1,128)}, u32[]{:S(2)}) copy-start(f32[1,192]{1,0:T(1,128)} %get-tuple-element.114) | copy-start | bytes 2308
  195.9 6.8 %copy-start.11 = (f32[1,192]{1,0:T(1,128)S(1)}, f32[1,192]{1,0:T(1,128)}, u32[]{:S(2)}) copy-start(f32[1,192]{1,0:T(1,128)} %get-tuple-element.115) | copy-start | bytes 2308
  195.9 6.8 %copy-start.12 = (f32[1,192]{1,0:T(1,128)S(1)}, f32[1,192]{1,0:T(1,128)}, u32[]{:S(2)}) copy-start(f32[1,192]{1,0:T(1,128)} %get-tuple-element.116) | copy-start | bytes 2308
  207.3 3.2 copy-start.5
  210.5 2.4 copy-start.6
  216.0 10.4 %collective-permute-start.6 = (f32[784,384]{1,0:T(8,128)}, f32[784,384]{1,0:T(8,128)S(1)}, u32[]{:S(2)}, u32[]{:S(2)}) collective-permute-start(f32[784,384]{1,0:T(8,128)} %pad_maximum_fusion), channel_id=1, source_target_pairs={{0,8},{8,0},{1,9},{9,1},{2,10},{10,2},{3,11},{11,3},{4,12},{12,4},... | collective-permute-start | bytes 3612680 | tf_op jit(solution)/shard_map/ppermute | solution.py:86
  226.8 34.2 %collective-permute-start.7 = (f32[400,384]{1,0:T(8,128)S(1)}, f32[400,384]{1,0:T(8,128)S(1)}, u32[]{:S(2)}, u32[]{:S(2)}) collective-permute-start(f32[400,384]{1,0:T(8,128)S(1)} %pad_maximum_fusion.1), channel_id=1, source_target_pairs={{0,64},{16,80},{32,96},{48,112},{64,0},{80,16},{96,32},{112,48},{1... | collective-permute-start | bytes 1843208 | tf_op jit(solution)/shard_map/ppermute | solution.py:86
  261.1 26.3 %copy-start.7 = (bf16[1024,192]{0,1:T(8,128)(2,1)S(1)}, bf16[1024,192]{0,1:T(8,128)(2,1)}, u32[]{:S(2)}) copy-start(bf16[1024,192]{0,1:T(8,128)(2,1)} %param.27) | copy-start | bytes 1179652
  261.3 18.6 %collective-permute-start.8 = (f32[208,384]{1,0:T(8,128)S(1)}, f32[208,384]{1,0:T(8,128)S(1)}, u32[]{:S(2)}, u32[]{:S(2)}) collective-permute-start(f32[208,384]{1,0:T(8,128)S(1)} %pad_maximum_fusion.2), channel_id=1, source_target_pairs={{0,32},{16,48},{32,0},{48,16},{64,96},{80,112},{96,64},{112,80},{1... | collective-permute-start | bytes 958472 | tf_op jit(solution)/shard_map/ppermute | solution.py:86
  280.0 7.3 %collective-permute-start.9 = (f32[112,384]{1,0:T(8,128)S(1)}, f32[112,384]{1,0:T(8,128)S(1)}, u32[]{:S(2)}, u32[]{:S(2)}) collective-permute-start(f32[112,384]{1,0:T(8,128)S(1)} %pad_maximum_fusion.3), channel_id=1, source_target_pairs={{0,16},{16,0},{32,48},{48,32},{64,80},{80,64},{96,112},{112,96},{1... | collective-permute-start | bytes 516104 | tf_op jit(solution)/shard_map/ppermute | solution.py:86
  290.3 6.0 %collective-permute-start.12 = (f32[4,8,1,1,24,192]{5,4,1,0,3,2:T(8,128)S(1)}, f32[4,8,1,1,24,192]{5,4,1,0,3,2:T(8,128)S(1)}, u32[]{:S(2)}, u32[]{:S(2)}) collective-permute-start(f32[4,8,1,1,24,192]{5,4,1,0,3,2:T(8,128)S(1)} %dynamic-slice_bitcast_fusion), channel_id=1, source_target_pairs={{0,8},{8,0},{1,9},{9,1},{2,10},{10,2},{3,11},{11,3},{4,12},{12,4},... | collective-permute-start | bytes 1769480 | tf_op jit(solution)/shard_map/ppermute | solution.py:83
  293.7 55.0 %copy-start.4 = (bf16[1536,3,192]{2,0,1:T(8,128)(2,1)S(1)}, bf16[1536,3,192]{2,0,1:T(8,128)(2,1)}, u32[]{:S(2)}) copy-start(bf16[1536,3,192]{2,0,1:T(8,128)(2,1)} %all-gather.4.cloned.1.call-done) | copy-start | bytes 5308420
  293.7 8.0 %collective-permute-start.10 = (f32[64,384]{1,0:T(8,128)S(1)}, f32[64,384]{1,0:T(8,128)S(1)}, u32[]{:S(2)}, u32[]{:S(2)}) collective-permute-start(f32[64,384]{1,0:T(8,128)S(1)} %pad_maximum_fusion.4), channel_id=1, source_target_pairs={{0,256},{128,384},{256,0},{384,128},{1,257},{129,385},{257,1},{385... | collective-permute-start | bytes 294920 | tf_op jit(solution)/shard_map/ppermute | solution.py:86
  296.5 24.6 %collective-permute-start.13 = (f32[4,1,4,1,24,192]{5,4,2,0,3,1:T(8,128)S(1)}, f32[4,1,4,1,24,192]{5,4,2,0,3,1:T(8,128)S(1)}, u32[]{:S(2)}, u32[]{:S(2)}) collective-permute-start(f32[4,1,4,1,24,192]{5,4,2,0,3,1:T(8,128)S(1)} %dynamic-slice_bitcast_fusion.1), channel_id=1, source_target_pairs={{0,64},{16,80},{32,96},{48,112},{64,0},{80,16},{96,32},{112,48},{1... | collective-permute-start | bytes 884744 | tf_op jit(solution)/shard_map/ppermute | solution.py:83
  321.2 13.4 %collective-permute-start.14 = (f32[4,1,2,1,24,192]{5,4,2,0,3,1:T(8,128)S(1)}, f32[4,1,2,1,24,192]{5,4,2,0,3,1:T(8,128)S(1)}, u32[]{:S(2)}, u32[]{:S(2)}) collective-permute-start(f32[4,1,2,1,24,192]{5,4,2,0,3,1:T(8,128)S(1)} %dynamic-slice_bitcast_fusion.2), channel_id=1, source_target_pairs={{0,32},{16,48},{32,0},{48,16},{64,96},{80,112},{96,64},{112,80},{1... | collective-permute-start | bytes 442376 | tf_op jit(solution)/shard_map/ppermute | solution.py:83
  323.2 13.4 %collective-permute-start.11 = (f32[40,384]{1,0:T(8,128)S(1)}, f32[40,384]{1,0:T(8,128)S(1)}, u32[]{:S(2)}, u32[]{:S(2)}) collective-permute-start(f32[40,384]{1,0:T(8,128)S(1)} %pad_maximum_fusion.5), channel_id=1, source_target_pairs={{0,128},{128,0},{256,384},{384,256},{1,129},{129,1},{257,385},{385... | collective-permute-start | bytes 184328 | tf_op jit(solution)/shard_map/ppermute | solution.py:86
  334.6 5.8 %collective-permute-start.15 = (f32[4,1,1,1,24,192]{5,4,2,0,3,1:T(8,128)S(1)}, f32[4,1,1,1,24,192]{5,4,2,0,3,1:T(8,128)S(1)}, u32[]{:S(2)}, u32[]{:S(2)}) collective-permute-start(f32[4,1,1,1,24,192]{5,4,2,0,3,1:T(8,128)S(1)} %constant_dynamic-slice_fusion.1), channel_id=1, source_target_pairs={{0,16},{16,0},{32,48},{48,32},{64,80},{80,64},{96,112},{112,96},{1... | collective-permute-start | bytes 221192 | tf_op jit(solution)/shard_map/ppermute | solution.py:83
  340.4 6.3 %collective-permute-start.16 = (f32[1,2,1,1,24,192]{5,4,3,2,1,0:T(8,128)S(1)}, f32[1,2,1,1,24,192]{5,4,3,2,1,0:T(8,128)S(1)}, u32[]{:S(2)}, u32[]{:S(2)}) collective-permute-start(f32[1,2,1,1,24,192]{5,4,3,2,1,0:T(8,128)S(1)} %dynamic-slice_bitcast_fusion.3), channel_id=1, source_target_pairs={{0,256},{128,384},{256,0},{384,128},{1,257},{129,385},{257,1},{385... | collective-permute-start | bytes 110600 | tf_op jit(solution)/shard_map/ppermute | solution.py:83
  346.7 7.1 %copy-start.1 = (s32[128]{0:T(128)S(1)}, s32[128]{0:T(128)}, u32[]{:S(2)}) copy-start(s32[128]{0:T(128)} %param.17) | copy-start | bytes 1540
  346.8 6.4 %collective-permute-start.17 = (f32[1,1,1,1,24,192]{5,4,3,2,1,0:T(8,128)S(1)}, f32[1,1,1,1,24,192]{5,4,3,2,1,0:T(8,128)S(1)}, u32[]{:S(2)}, u32[]{:S(2)}) collective-permute-start(f32[1,1,1,1,24,192]{5,4,3,2,1,0:T(8,128)S(1)} %constant_dynamic-slice_fusion), channel_id=1, source_target_pairs={{0,128},{128,0},{256,384},{384,256},{1,129},{129,1},{257,385},{385... | collective-permute-start | bytes 55304 | tf_op jit(solution)/shard_map/ppermute | solution.py:83
Sparse Core Ops, SparseCore 0:
  11.8 88.8 all-gather.3
  102.8 62.8 all-gather.7
  207.4 47.4 all-gather.5

commit v7 on v6

--- a/solution.py
+++ b/solution.py
@@ -69,11 +69,10 @@
     for dim, name in reversed(list(enumerate(DP_AXES))):
         length = sizes[name]
         me = lax.axis_index(name)
-        bit = length.bit_length() - 2
-        while bit >= 0:
+        for bit in range(length.bit_length() - 1):
             shape = cur.shape
             span = shape[dim]
-            split = shape[:dim] + (span >> (bit + 1), 2, 1 << bit) + shape[dim + 1 :]
+            split = shape[:dim] + (span // 2, 2) + shape[dim + 1 :]
             pieces = cur.reshape(split)
             mine = (me >> bit) & 1
             keep = lax.dynamic_index_in_dim(pieces, mine, dim + 1, keepdims=False)
@@ -87,7 +86,6 @@
                 merged = keep + got[:-rows].reshape(send.shape)
                 extra = extra + got[-rows:]
             cur = merged.reshape(shape[:dim] + (span // 2,) + shape[dim + 1 :])
-            bit -= 1
     return cur.reshape((-1,) + cols), extra
 
 

time: 363 us -> 347 us (0.956)
  waiting for transfers between devices: 125 us -> 109 us
    ppermute x6, waiting for transfers between devices: 33.2 us -> 24.9 us  [halving_scatter(): merged = keep + lax.ppermute(send, name, perm)]
    ppermute x6, waiting for transfers between devices: 54.1 us -> 46.9 us  [halving_scatter(): got = lax.ppermute(message, name, perm)]
    unnamed x36 -> x40, local copies, waits for them, and re-layouts: 8.45 us -> 8.46 us
  transfers between devices with their start and end apart: 24 -> 24, of which waited for: 11 -> 12; matrix products, arithmetic and copies ran while one was open for 13% -> 13% of each run, Pallas kernels for 0% -> 0%
where the time goes in v7:
time: 347 us; the launch traced here: 344 us
  waiting for transfers between devices  109 us (31%)
  starting transfers between devices  91 us (26%)
  blocking collectives  55.2 us (16%)
  other arithmetic  33 us (10%)
  local copies, waits for them, and re-layouts  22.7 us (7%)
  matrix products  18.5 us (5%)
  between operations  14.7 us (4%)
    psum x6, blocking collectives, dp_sum(): value = lax.psum(value, name)  55.2 us
    ppermute x6, waiting for transfers between devices, halving_scatter(): got = lax.ppermute(message, name, perm)  46.9 us
    ppermute x6, waiting for transfers between devices, doubling_gather(): got = lax.ppermute(cur, name, perm)  35.2 us
    ppermute x6, waiting for transfers between devices, halving_scatter(): merged = keep + lax.ppermute(send, name, perm)  24.9 us
    ppermute x6, starting transfers between devices, doubling_gather(): got = lax.ppermute(cur, name, perm)  24.5 us
    ppermute x6, starting transfers between devices, halving_scatter(): got = lax.ppermute(message, name, perm)  21 us
    ppermute x6, starting transfers between devices, halving_scatter(): merged = keep + lax.ppermute(send, name, perm)  17.5 us
    all_to_all x1, starting transfers between devices, on_device(): lax.all_to_all(meta_send, DP_AXES, split_axis=0, concat_axis=0, tiled=True)  11.1 us
  transfers between devices with their start and end apart: 24, of which 12 were waited for; matrix products, arithmetic and copies ran while one was open for 13% of the time, Pallas kernels for 0%

profile of v7, /device:TPU:1, one launch (start us, length us, event | category | flops | bytes accessed | tf_op | source)
XLA Modules:
  0.0 344.4 jit_solution(4283826386758350840)
XLA Ops:
  10.4 4.8 %collective-permute-start = (bf16[1,448,192]{1,2,0:T(8,128)(2,1)S(1)}, bf16[1,448,192]{1,2,0:T(8,128)(2,1)S(1)}, u32[]{:S(2)}, u32[]{:S(2)}) collective-permute-start(bf16[1,448,192]{1,2,0:T(8,128)(2,1)S(1)} %maximum_bitcast_fusion), channel_id=1, source_target_pairs={{0,1},{1,0},{2,3},{3,2},{4,5},{5,4},{6,7},{7,6},{8,9},{9,8},{10,11... | collective-permute-start | bytes 516104 | tf_op jit(solution)/shard_map/ppermute | solution.py:99
  19.5 11.1 %all-to-all-start.1 = ((s32[64,1,2]{2,1,0:T(1,128)}), s32[64,1,2]{2,1,0:T(1,128)S(1)}, u32[]{:S(2)}, u32[]{:S(2)}) async-start(s32[64,1,2]{2,1,0:T(1,128)} %copy.77), calls=%async_computation.1 | async-start | bytes 65536 | tf_op jit(solution)/shard_map/all_to_all | solution.py:132
  30.6 1.9 collective-permute-start.3
  32.6 2.1 copy.76
  36.7 5.8 %collective-permute-start.1 = (bf16[2,448,192]{1,2,0:T(8,128)(2,1)S(1)}, bf16[2,448,192]{1,2,0:T(8,128)(2,1)S(1)}, u32[]{:S(2)}, u32[]{:S(2)}) collective-permute-start(bf16[2,448,192]{1,2,0:T(8,128)(2,1)S(1)} %maximum_select_fusion.2), channel_id=1, source_target_pairs={{0,2},{1,3},{2,0},{3,1},{4,6},{5,7},{6,4},{7,5},{8,10},{9,11},{10,... | collective-permute-start | bytes 1032200 | tf_op jit(solution)/shard_map/ppermute | solution.py:99
  43.1 1.9 collective-permute-start.4
  45.1 10.6 %all-to-all-start = ((bf16[64,16,320]{2,1,0:T(8,128)(2,1)}), bf16[64,16,320]{2,1,0:T(8,128)(2,1)S(1)}, u32[]{:S(2)}, u32[]{:S(2)}) async-start(bf16[64,16,320]{2,1,0:T(8,128)(2,1)} %broadcast_select_fusion), calls=%async_computation | async-start | bytes 1572864 | tf_op jit(solution)/shard_map/all_to_all | solution.py:131
  55.8 4.2 %collective-permute-done.1 = bf16[2,448,192]{1,2,0:T(8,128)(2,1)S(1)} collective-permute-done((bf16[2,448,192]{1,2,0:T(8,128)(2,1)S(1)}, bf16[2,448,192]{1,2,0:T(8,128)(2,1)S(1)}, u32[]{:S(2)}, u32[]{:S(2)}) %collective-permute-start.1) | collective-permute-done | bytes 344096 | tf_op jit(solution)/shard_map/ppermute | solution.py:99
  60.1 8.1 %collective-permute-start.2 = (bf16[4,448,192]{1,2,0:T(8,128)(2,1)S(1)}, bf16[4,448,192]{1,2,0:T(8,128)(2,1)S(1)}, u32[]{:S(2)}, u32[]{:S(2)}) collective-permute-start(bf16[4,448,192]{1,2,0:T(8,128)(2,1)S(1)} %maximum_select_fusion.1), channel_id=1, source_target_pairs={{0,4},{1,5},{2,6},{3,7},{4,0},{5,1},{6,2},{7,3},{8,12},{9,13},{10,... | collective-permute-start | bytes 2064392 | tf_op jit(solution)/shard_map/ppermute | solution.py:99
  71.0 31.0 %collective-permute-done.5 = f32[4,192]{1,0:T(4,128)S(1)} collective-permute-done((f32[4,192]{1,0:T(4,128)S(1)}, f32[4,192]{1,0:T(4,128)S(1)}, u32[]{:S(2)}, u32[]{:S(2)}) %collective-permute-start.5) | collective-permute-done | bytes 3104 | tf_op jit(solution)/shard_map/ppermute | solution.py:99
  103.3 2.2 fusion.84
  105.6 2.6 copy-done.2
  108.2 2.6 multiply_convert_fusion
  114.9 6.0 %all-to-all-start.2 = ((bf16[8,192,192]{1,2,0:T(8,128)(2,1)}), bf16[8,192,192]{1,2,0:T(8,128)(2,1)}, u32[]{:S(2)}, u32[]{:S(2)}) async-start(bf16[8,192,192]{1,2,0:T(8,128)(2,1)} %copy.85), calls=%async_computation.2 | async-start | bytes 1572864 | tf_op jit(solution)/shard_map/all_to_all | solution.py:194
  121.1 3.7 %fusion.88 = f32[1024,384]{0,1:T(8,128)S(1)} fusion(bf16[1024,1536]{1,0:T(8,128)(2,1)} %multiply_convert_fusion, bf16[1536,384]{0,1:T(8,128)(2,1)} %bitcast.233), kind=kOutput, calls=%fused_computation.264 | convolution fusion | flops 1207959552 | bytes 5898240 | tf_op jit(solution)/shard_map/dot_general | solution.py:166
  125.4 6.0 %fusion.4 = (f32[192]{0:T(256)}, f32[192]{0:T(256)}, f32[64,16,192]{2,1,0:T(8,128)}) fusion(f32[64,16]{1,0:T(8,128)S(1)} %get-tuple-element.139, f32[192]{0:T(256)S(1)} %bitcast.264, f32[192]{0:T(256)S(1)} %bitcast.266, f32[192]{0:T(256)S(1)} %bitcast.270, f32[192]{0:T(256)S(1)} %bitcast.272, f32[192]{0:T(256)S(1)} %bitcast.274, f32[192]{0:T(256)S(1)} %bitcast.276, ...), kind=kLoop, calls=%fused_computation.75 | loop fusion | flops 12779136 | bytes 1602304 | tf_op jit(solution)/shard_map/reduce_sum | solution.py:175
  132.9 4.2 %all-reduce.8 = (f32[192]{0:T(256)S(1)}, f32[]{:T(128)}, f32[192]{0:T(256)S(1)}) all-reduce(f32[192]{0:T(256)} %get-tuple-element.70, f32[]{:T(128)} %fusion.78, f32[192]{0:T(256)} %get-tuple-element.69), channel_id=1, replica_groups=mesh['x'=4,'y'=8,'c'=2,'mp'=8] {'c'}, use_global_device_ids=true, to_apply=%region_3.5 | all-reduce | flops 385 | bytes 3080 | tf_op jit(solution)/shard_map/psum | solution.py:49
  137.1 15.5 %all-reduce.4 = (f32[192]{0:T(256)S(1)}, f32[]{:T(128)}, f32[192]{0:T(256)S(1)}) all-reduce(f32[192]{0:T(256)S(1)} %get-tuple-element.85, f32[]{:T(128)} %get-tuple-element.86, f32[192]{0:T(256)S(1)} %get-tuple-element.87), channel_id=1, replica_groups=mesh['x'=4,'y'=8,'c'=2,'mp'=8] {'y'}, use_global_device_ids=true, to_apply=%region_4.6 | all-reduce | flops 385 | bytes 3080 | tf_op jit(solution)/shard_map/psum | solution.py:49
  152.6 10.1 %all-reduce.6 = (f32[192]{0:T(256)S(1)}, f32[]{:T(128)}, f32[192]{0:T(256)S(1)}) all-reduce(f32[192]{0:T(256)S(1)} %get-tuple-element.75, f32[]{:T(128)} %get-tuple-element.76, f32[192]{0:T(256)S(1)} %get-tuple-element.77), channel_id=1, replica_groups=mesh['x'=4,'y'=8,'c'=2,'mp'=8] {'x'}, use_global_device_ids=true, to_apply=%region_5.7 | all-reduce | flops 385 | bytes 3080 | tf_op jit(solution)/shard_map/psum | solution.py:49
  163.4 2.4 all-gather.8.cloned.1.call-done
  165.7 4.1 %fusion.85 = (f32[192]{0:T(256)S(1)}, f32[192]{0:T(256)S(1)}, f32[1024,192]{0,1:T(8,128)}) fusion(f32[192]{0:T(256)S(1)} %get-tuple-element.90, f32[1024,192]{0,1:T(8,128)S(1)} %copy.82, f32[192]{0:T(256)S(1)} %get-tuple-element.91, f32[192]{0:T(256)} %param.25, f32[192]{0:T(256)} %param.24, f32[1024]{0:T(1024)S(1)} %reshape.388, ...), kind=kOutput, calls=%fused_computation.261 | convolution fusion | flops 607125120 | bytes 5317120 | tf_op jit(solution)/shard_map/dot_general | solution.py:195
  169.8 3.5 %all-reduce.7 = (f32[192]{0:T(256)S(1)}, f32[192]{0:T(256)S(1)}) all-reduce(f32[192]{0:T(256)S(1)} %get-tuple-element.72, f32[192]{0:T(256)S(1)} %get-tuple-element.71), channel_id=1, replica_groups=mesh['x'=4,'y'=8,'c'=2,'mp'=8] {'c'}, use_global_device_ids=true, to_apply=%region_19.21 | all-reduce | flops 384 | bytes 3072 | tf_op jit(solution)/shard_map/psum | solution.py:49
  173.3 13.0 %all-reduce.3 = (f32[192]{0:T(256)S(1)}, f32[192]{0:T(256)S(1)}) all-reduce(f32[192]{0:T(256)S(1)} %get-tuple-element.83, f32[192]{0:T(256)S(1)} %get-tuple-element.84), channel_id=1, replica_groups=mesh['x'=4,'y'=8,'c'=2,'mp'=8] {'y'}, use_global_device_ids=true, to_apply=%region_20.22 | all-reduce | flops 384 | bytes 3072 | tf_op jit(solution)/shard_map/psum | solution.py:49
  186.3 8.9 %all-reduce.5 = (f32[192]{0:T(256)}, f32[192]{0:T(256)S(1)}) all-reduce(f32[192]{0:T(256)S(1)} %get-tuple-element.73, f32[192]{0:T(256)S(1)} %get-tuple-element.74), channel_id=1, replica_groups=mesh['x'=4,'y'=8,'c'=2,'mp'=8] {'x'}, use_global_device_ids=true, to_apply=%region_21.23 | all-reduce | flops 384 | bytes 3072 | tf_op jit(solution)/shard_map/psum | solution.py:49
  195.9 4.1 %multiply_reduce_fusion.32 = (f32[192]{0:T(256)}, f32[1024,192]{0,1:T(8,128)}, bf16[1024,192]{0,1:T(8,128)(2,1)}) fusion(f32[]{:T(128)} %get-tuple-element.81, f32[192]{0:T(256)} %get-tuple-element.78, f32[1024,192]{0,1:T(8,128)S(1)} %copy.82, f32[192]{0:T(256)S(1)} %get-tuple-element.91, f32[1024,192]{0,1:T(8,128)} %get-tuple-element.142, ...), kind=kLoop, calls=%fused_computation.181 | loop fusion | flops 4718400 | bytes 4334852 | tf_op jit(solution)/shard_map/reduce_sum | solution.py:40
  201.5 3.0 multiply_reduce_fusion.2
  204.6 3.4 fusion.56
  216.6 7.7 %collective-permute-start.6 = (f32[784,384]{1,0:T(8,128)}, f32[784,384]{1,0:T(8,128)S(1)}, u32[]{:S(2)}, u32[]{:S(2)}) collective-permute-start(f32[784,384]{1,0:T(8,128)} %pad_maximum_fusion), channel_id=1, source_target_pairs={{0,8},{8,0},{1,9},{9,1},{2,10},{10,2},{3,11},{11,3},{4,12},{12,4},... | collective-permute-start | bytes 3612680 | tf_op jit(solution)/shard_map/ppermute | solution.py:85
  224.3 2.7 collective-permute-done.6
  229.4 15.1 %collective-permute-done.7 = f32[400,384]{1,0:T(8,128)S(1)} collective-permute-done((f32[400,384]{1,0:T(8,128)S(1)}, f32[400,384]{1,0:T(8,128)S(1)}, u32[]{:S(2)}, u32[]{:S(2)}) %collective-permute-start.7) | collective-permute-done | bytes 614432 | tf_op jit(solution)/shard_map/ppermute | solution.py:85
  244.7 2.7 collective-permute-start.8
  247.4 16.1 %collective-permute-done.8 = f32[208,384]{1,0:T(8,128)S(1)} collective-permute-done((f32[208,384]{1,0:T(8,128)S(1)}, f32[208,384]{1,0:T(8,128)S(1)}, u32[]{:S(2)}, u32[]{:S(2)}) %collective-permute-start.8) | collective-permute-done | bytes 319520 | tf_op jit(solution)/shard_map/ppermute | solution.py:85
  263.7 4.2 %collective-permute-start.9 = (f32[112,384]{1,0:T(8,128)S(1)}, f32[112,384]{1,0:T(8,128)S(1)}, u32[]{:S(2)}, u32[]{:S(2)}) collective-permute-start(f32[112,384]{1,0:T(8,128)S(1)} %pad_maximum_fusion.3), channel_id=1, source_target_pairs={{0,64},{16,80},{32,96},{48,112},{64,0},{80,16},{96,32},{112,48},{1... | collective-permute-start | bytes 516104 | tf_op jit(solution)/shard_map/ppermute | solution.py:85
  268.0 10.8 %collective-permute-done.9 = f32[112,384]{1,0:T(8,128)S(1)} collective-permute-done((f32[112,384]{1,0:T(8,128)S(1)}, f32[112,384]{1,0:T(8,128)S(1)}, u32[]{:S(2)}, u32[]{:S(2)}) %collective-permute-start.9) | collective-permute-done | bytes 172064 | tf_op jit(solution)/shard_map/ppermute | solution.py:85
  278.8 2.9 fusion.89
  281.7 2.4 collective-permute-start.12
  284.2 2.1 collective-permute-start.10
  286.5 1.9 collective-permute-start.13
  288.4 2.2 collective-permute-done.10
  290.6 8.3 %collective-permute-done.13 = f32[4,4,1,24,192]{4,3,1,0,2:T(8,128)S(1)} collective-permute-done((f32[4,4,1,24,192]{4,3,1,0,2:T(8,128)S(1)}, f32[4,4,1,24,192]{4,3,1,0,2:T(8,128)S(1)}, u32[]{:S(2)}, u32[]{:S(2)}) %collective-permute-start.13) | collective-permute-done | bytes 294944 | tf_op jit(solution)/shard_map/ppermute | solution.py:82
  299.0 2.7 collective-permute-start.14
  301.8 2.3 collective-permute-start.11
  304.1 8.7 %collective-permute-done.14 = f32[4,2,1,24,192]{4,3,1,0,2:T(8,128)S(1)} collective-permute-done((f32[4,2,1,24,192]{4,3,1,0,2:T(8,128)S(1)}, f32[4,2,1,24,192]{4,3,1,0,2:T(8,128)S(1)}, u32[]{:S(2)}, u32[]{:S(2)}) %collective-permute-start.14) | collective-permute-done | bytes 147488 | tf_op jit(solution)/shard_map/ppermute | solution.py:82
  312.9 5.0 %collective-permute-start.15 = (f32[4,1,1,24,192]{4,3,1,0,2:T(8,128)S(1)}, f32[4,1,1,24,192]{4,3,1,0,2:T(8,128)S(1)}, u32[]{:S(2)}, u32[]{:S(2)}) collective-permute-start(f32[4,1,1,24,192]{4,3,1,0,2:T(8,128)S(1)} %constant_dynamic-slice_fusion.1), channel_id=1, source_target_pairs={{0,64},{16,80},{32,96},{48,112},{64,0},{80,16},{96,32},{112,48},{1... | collective-permute-start | bytes 221192 | tf_op jit(solution)/shard_map/ppermute | solution.py:82
  317.9 7.6 %collective-permute-done.15 = f32[4,1,1,24,192]{4,3,1,0,2:T(8,128)S(1)} collective-permute-done((f32[4,1,1,24,192]{4,3,1,0,2:T(8,128)S(1)}, f32[4,1,1,24,192]{4,3,1,0,2:T(8,128)S(1)}, u32[]{:S(2)}, u32[]{:S(2)}) %collective-permute-start.15) | collective-permute-done | bytes 73760 | tf_op jit(solution)/shard_map/ppermute | solution.py:82
  325.6 3.2 collective-permute-start.16
  330.4 2.3 collective-permute-start.17
  332.8 3.5 %add_convert_fusion = bf16[1024,192]{1,0:T(8,128)(2,1)S(1)} fusion(f32[1024,1536]{1,0:T(8,128)} %copy-done.2, s32[]{:T(128)S(6)} %select_n.153, bf16[1024,1536]{0,1:T(8,128)(2,1)} %all-gather.6.cloned.1.call-done, bf16[1536,3,192]{2,0,1:T(8,128)(2,1)S(1)} %copy-done.4), kind=kOutput, calls=%fused_computation.166 | convolution fusion | flops 604372992 | bytes 5111812 | tf_op jit(solution)/shard_map/dot_general | solution.py:189
  (154 shorter events, 38.4 us)
Async XLA Ops:
  7.2 8.7 %copy-start = (s32[128]{0:T(128)S(1)}, s32[128]{0:T(128)}, u32[]{:S(2)}) copy-start(s32[128]{0:T(128)} %param.17) | copy-start | bytes 1540
  7.2 27.6 %copy-start.17 = (s32[1,64]{1,0:T(1,128)S(1)}, s32[1,64]{1,0:T(1,128)}, u32[]{:S(2)}) copy-start(s32[1,64]{1,0:T(1,128)} %param.16) | copy-start | bytes 772
  7.2 103.6 %all-gather.4.cloned.1.call-start = ((), (), s32[]{:S(2)}) async-start(), calls=%async_computation.3 | async-start | bytes 2396160 | tf_op jit(solution)/shard_map/all_gather | solution.py:134
  10.4 26.2 %collective-permute-start = (bf16[1,448,192]{1,2,0:T(8,128)(2,1)S(1)}, bf16[1,448,192]{1,2,0:T(8,128)(2,1)S(1)}, u32[]{:S(2)}, u32[]{:S(2)}) collective-permute-start(bf16[1,448,192]{1,2,0:T(8,128)(2,1)S(1)} %maximum_bitcast_fusion), channel_id=1, source_target_pairs={{0,1},{1,0},{2,3},{3,2},{4,5},{5,4},{6,7},{7,6},{8,9},{9,8},{10,11... | collective-permute-start | bytes 516104 | tf_op jit(solution)/shard_map/ppermute | solution.py:99
  19.5 25.6 %all-to-all-start.1 = ((s32[64,1,2]{2,1,0:T(1,128)}), s32[64,1,2]{2,1,0:T(1,128)S(1)}, u32[]{:S(2)}, u32[]{:S(2)}) async-start(s32[64,1,2]{2,1,0:T(1,128)} %copy.77), calls=%async_computation.1 | async-start | bytes 65536 | tf_op jit(solution)/shard_map/all_to_all | solution.py:132
  30.6 135.2 %all-gather.8.cloned.1.call-start = ((), (), s32[]{:S(2)}) async-start(), calls=%async_computation.5 | async-start | bytes 3538944 | tf_op jit(solution)/shard_map/all_gather | solution.py:193
  30.6 12.5 %collective-permute-start.3 = (f32[1,192]{1,0:T(1,128)}, f32[1,192]{1,0:T(1,128)S(1)}, u32[]{:S(2)}, u32[]{:S(2)}) collective-permute-start(f32[1,192]{1,0:T(1,128)} %bitcast.338), channel_id=1, source_target_pairs={{0,1},{1,0},{2,3},{3,2},{4,5},{5,4},{6,7},{7,6},{8,9},{9,8},{10,11... | collective-permute-start | bytes 2312 | tf_op jit(solution)/shard_map/ppermute | solution.py:99
  32.6 9.9 %copy-start.8 = (f32[31,192]{1,0:T(8,128)S(1)}, f32[31,192]{1,0:T(8,128)}, u32[]{:S(2)}) copy-start(f32[31,192]{1,0:T(8,128)} %param.23) | copy-start | bytes 71428
  32.6 10.5 %copy-start.16 = (f32[192]{0:T(256)S(1)}, f32[192]{0:T(256)}, u32[]{:S(2)}) copy-start(f32[192]{0:T(256)} %param.21) | copy-start | bytes 2308
  36.7 23.3 %collective-permute-start.1 = (bf16[2,448,192]{1,2,0:T(8,128)(2,1)S(1)}, bf16[2,448,192]{1,2,0:T(8,128)(2,1)S(1)}, u32[]{:S(2)}, u32[]{:S(2)}) collective-permute-start(bf16[2,448,192]{1,2,0:T(8,128)(2,1)S(1)} %maximum_select_fusion.2), channel_id=1, source_target_pairs={{0,2},{1,3},{2,0},{3,1},{4,6},{5,7},{6,4},{7,5},{8,10},{9,11},{10,... | collective-permute-start | bytes 1032200 | tf_op jit(solution)/shard_map/ppermute | solution.py:99
  43.1 25.2 %collective-permute-start.4 = (f32[2,192]{1,0:T(2,128)S(1)}, f32[2,192]{1,0:T(2,128)S(1)}, u32[]{:S(2)}, u32[]{:S(2)}) collective-permute-start(f32[2,192]{1,0:T(2,128)S(1)} %maximum_select_fusion.5), channel_id=1, source_target_pairs={{0,2},{1,3},{2,0},{3,1},{4,6},{5,7},{6,4},{7,5},{8,10},{9,11},{10,... | collective-permute-start | bytes 4616 | tf_op jit(solution)/shard_map/ppermute | solution.py:99
  45.1 58.0 %all-to-all-start = ((bf16[64,16,320]{2,1,0:T(8,128)(2,1)}), bf16[64,16,320]{2,1,0:T(8,128)(2,1)S(1)}, u32[]{:S(2)}, u32[]{:S(2)}) async-start(bf16[64,16,320]{2,1,0:T(8,128)(2,1)} %broadcast_select_fusion), calls=%async_computation | async-start | bytes 1572864 | tf_op jit(solution)/shard_map/all_to_all | solution.py:131
  60.1 42.0 %collective-permute-start.2 = (bf16[4,448,192]{1,2,0:T(8,128)(2,1)S(1)}, bf16[4,448,192]{1,2,0:T(8,128)(2,1)S(1)}, u32[]{:S(2)}, u32[]{:S(2)}) collective-permute-start(bf16[4,448,192]{1,2,0:T(8,128)(2,1)S(1)} %maximum_select_fusion.1), channel_id=1, source_target_pairs={{0,4},{1,5},{2,6},{3,7},{4,0},{5,1},{6,2},{7,3},{8,12},{9,13},{10,... | collective-permute-start | bytes 2064392 | tf_op jit(solution)/shard_map/ppermute | solution.py:99
  68.3 33.7 %collective-permute-start.5 = (f32[4,192]{1,0:T(4,128)S(1)}, f32[4,192]{1,0:T(4,128)S(1)}, u32[]{:S(2)}, u32[]{:S(2)}) collective-permute-start(f32[4,192]{1,0:T(4,128)S(1)} %maximum_select_fusion.4), channel_id=1, source_target_pairs={{0,4},{1,5},{2,6},{3,7},{4,0},{5,1},{6,2},{7,3},{8,12},{9,13},{10,... | collective-permute-start | bytes 9224 | tf_op jit(solution)/shard_map/ppermute | solution.py:99
  105.5 2.7 copy-start.2
  110.8 1.4 slice-start
  110.8 2.9 slice-start.1
  114.9 48.5 %all-to-all-start.2 = ((bf16[8,192,192]{1,2,0:T(8,128)(2,1)}), bf16[8,192,192]{1,2,0:T(8,128)(2,1)}, u32[]{:S(2)}, u32[]{:S(2)}) async-start(bf16[8,192,192]{1,2,0:T(8,128)(2,1)} %copy.85), calls=%async_computation.2 | async-start | bytes 1572864 | tf_op jit(solution)/shard_map/all_to_all | solution.py:194
  120.9 157.8 %all-gather.6.cloned.1.call-start = ((), (), s32[]{:S(2)}) async-start(), calls=%async_computation.4 | async-start | bytes 3538944 | tf_op jit(solution)/shard_map/all_gather | solution.py:187
  124.8 75.3 %copy-start.3 = (f32[1024,384]{0,1:T(8,128)}, f32[1024,384]{0,1:T(8,128)S(1)}, u32[]{:S(2)}) copy-start(f32[1024,384]{0,1:T(8,128)S(1)} %fusion.88) | copy-start | bytes 4718596
  165.7 30.1 %copy-start.14 = (f32[192]{0:T(256)S(1)}, f32[192]{0:T(256)}, u32[]{:S(2)}) copy-start(f32[192]{0:T(256)} %param.25) | copy-start | bytes 2308
  195.2 0.7 copy-start.15
  195.9 8.7 %copy-start.9 = (f32[1,192]{1,0:T(1,128)S(1)}, f32[1,192]{1,0:T(1,128)}, u32[]{:S(2)}) copy-start(f32[1,192]{1,0:T(1,128)} %get-tuple-element.119) | copy-start | bytes 2308
  195.9 8.7 %copy-start.10 = (f32[1,192]{1,0:T(1,128)S(1)}, f32[1,192]{1,0:T(1,128)}, u32[]{:S(2)}) copy-start(f32[1,192]{1,0:T(1,128)} %get-tuple-element.120) | copy-start | bytes 2308
  195.9 8.7 %copy-start.11 = (f32[1,192]{1,0:T(1,128)S(1)}, f32[1,192]{1,0:T(1,128)}, u32[]{:S(2)}) copy-start(f32[1,192]{1,0:T(1,128)} %get-tuple-element.121) | copy-start | bytes 2308
  195.9 8.7 %copy-start.12 = (f32[1,192]{1,0:T(1,128)S(1)}, f32[1,192]{1,0:T(1,128)}, u32[]{:S(2)}) copy-start(f32[1,192]{1,0:T(1,128)} %get-tuple-element.122) | copy-start | bytes 2308
  204.6 6.3 %copy-start.13 = (f32[192]{0:T(256)S(1)}, f32[192]{0:T(256)}, u32[]{:S(2)}) copy-start(f32[192]{0:T(256)} %get-tuple-element.88) | copy-start | bytes 2308
  209.2 1.9 copy-start.5
  211.1 2.4 copy-start.6
  216.6 10.4 %collective-permute-start.6 = (f32[784,384]{1,0:T(8,128)}, f32[784,384]{1,0:T(8,128)S(1)}, u32[]{:S(2)}, u32[]{:S(2)}) collective-permute-start(f32[784,384]{1,0:T(8,128)} %pad_maximum_fusion), channel_id=1, source_target_pairs={{0,8},{8,0},{1,9},{9,1},{2,10},{10,2},{3,11},{11,3},{4,12},{12,4},... | collective-permute-start | bytes 3612680 | tf_op jit(solution)/shard_map/ppermute | solution.py:85
  227.4 17.0 %collective-permute-start.7 = (f32[400,384]{1,0:T(8,128)S(1)}, f32[400,384]{1,0:T(8,128)S(1)}, u32[]{:S(2)}, u32[]{:S(2)}) collective-permute-start(f32[400,384]{1,0:T(8,128)S(1)} %pad_maximum_fusion.1), channel_id=1, source_target_pairs={{0,16},{16,0},{32,48},{48,32},{64,80},{80,64},{96,112},{112,96},{1... | collective-permute-start | bytes 1843208 | tf_op jit(solution)/shard_map/ppermute | solution.py:85
  244.5 34.2 %copy-start.7 = (bf16[1024,192]{0,1:T(8,128)(2,1)S(1)}, bf16[1024,192]{0,1:T(8,128)(2,1)}, u32[]{:S(2)}) copy-start(bf16[1024,192]{0,1:T(8,128)(2,1)} %param.27) | copy-start | bytes 1179652
  244.7 18.9 %collective-permute-start.8 = (f32[208,384]{1,0:T(8,128)S(1)}, f32[208,384]{1,0:T(8,128)S(1)}, u32[]{:S(2)}, u32[]{:S(2)}) collective-permute-start(f32[208,384]{1,0:T(8,128)S(1)} %pad_maximum_fusion.2), channel_id=1, source_target_pairs={{0,32},{16,48},{32,0},{48,16},{64,96},{80,112},{96,64},{112,80},{1... | collective-permute-start | bytes 958472 | tf_op jit(solution)/shard_map/ppermute | solution.py:85
  263.7 15.0 %collective-permute-start.9 = (f32[112,384]{1,0:T(8,128)S(1)}, f32[112,384]{1,0:T(8,128)S(1)}, u32[]{:S(2)}, u32[]{:S(2)}) collective-permute-start(f32[112,384]{1,0:T(8,128)S(1)} %pad_maximum_fusion.3), channel_id=1, source_target_pairs={{0,64},{16,80},{32,96},{48,112},{64,0},{80,16},{96,32},{112,48},{1... | collective-permute-start | bytes 516104 | tf_op jit(solution)/shard_map/ppermute | solution.py:85
  281.7 4.6 %collective-permute-start.12 = (f32[4,8,1,24,192]{4,3,1,0,2:T(8,128)S(1)}, f32[4,8,1,24,192]{4,3,1,0,2:T(8,128)S(1)}, u32[]{:S(2)}, u32[]{:S(2)}) collective-permute-start(f32[4,8,1,24,192]{4,3,1,0,2:T(8,128)S(1)} %dynamic-slice_bitcast_fusion), channel_id=1, source_target_pairs={{0,8},{8,0},{1,9},{9,1},{2,10},{10,2},{3,11},{11,3},{4,12},{12,4},... | collective-permute-start | bytes 1769480 | tf_op jit(solution)/shard_map/ppermute | solution.py:82
  284.2 48.6 %copy-start.4 = (bf16[1536,3,192]{2,0,1:T(8,128)(2,1)S(1)}, bf16[1536,3,192]{2,0,1:T(8,128)(2,1)}, u32[]{:S(2)}) copy-start(bf16[1536,3,192]{2,0,1:T(8,128)(2,1)} %all-gather.4.cloned.1.call-done) | copy-start | bytes 5308420
  284.2 6.4 %collective-permute-start.10 = (f32[64,384]{1,0:T(8,128)S(1)}, f32[64,384]{1,0:T(8,128)S(1)}, u32[]{:S(2)}, u32[]{:S(2)}) collective-permute-start(f32[64,384]{1,0:T(8,128)S(1)} %pad_maximum_fusion.4), channel_id=1, source_target_pairs={{0,128},{128,0},{256,384},{384,256},{1,129},{129,1},{257,385},{385... | collective-permute-start | bytes 294920 | tf_op jit(solution)/shard_map/ppermute | solution.py:85
  286.5 12.5 %collective-permute-start.13 = (f32[4,4,1,24,192]{4,3,1,0,2:T(8,128)S(1)}, f32[4,4,1,24,192]{4,3,1,0,2:T(8,128)S(1)}, u32[]{:S(2)}, u32[]{:S(2)}) collective-permute-start(f32[4,4,1,24,192]{4,3,1,0,2:T(8,128)S(1)} %dynamic-slice_bitcast_fusion.1), channel_id=1, source_target_pairs={{0,16},{16,0},{32,48},{48,32},{64,80},{80,64},{96,112},{112,96},{1... | collective-permute-start | bytes 884744 | tf_op jit(solution)/shard_map/ppermute | solution.py:82
  299.0 13.8 %collective-permute-start.14 = (f32[4,2,1,24,192]{4,3,1,0,2:T(8,128)S(1)}, f32[4,2,1,24,192]{4,3,1,0,2:T(8,128)S(1)}, u32[]{:S(2)}, u32[]{:S(2)}) collective-permute-start(f32[4,2,1,24,192]{4,3,1,0,2:T(8,128)S(1)} %dynamic-slice_bitcast_fusion.2), channel_id=1, source_target_pairs={{0,32},{16,48},{32,0},{48,16},{64,96},{80,112},{96,64},{112,80},{1... | collective-permute-start | bytes 442376 | tf_op jit(solution)/shard_map/ppermute | solution.py:82
  301.8 16.1 %collective-permute-start.11 = (f32[40,384]{1,0:T(8,128)S(1)}, f32[40,384]{1,0:T(8,128)S(1)}, u32[]{:S(2)}, u32[]{:S(2)}) collective-permute-start(f32[40,384]{1,0:T(8,128)S(1)} %pad_maximum_fusion.5), channel_id=1, source_target_pairs={{0,256},{128,384},{256,0},{384,128},{1,257},{129,385},{257,1},{385... | collective-permute-start | bytes 184328 | tf_op jit(solution)/shard_map/ppermute | solution.py:85
  312.9 12.6 %collective-permute-start.15 = (f32[4,1,1,24,192]{4,3,1,0,2:T(8,128)S(1)}, f32[4,1,1,24,192]{4,3,1,0,2:T(8,128)S(1)}, u32[]{:S(2)}, u32[]{:S(2)}) collective-permute-start(f32[4,1,1,24,192]{4,3,1,0,2:T(8,128)S(1)} %constant_dynamic-slice_fusion.1), channel_id=1, source_target_pairs={{0,64},{16,80},{32,96},{48,112},{64,0},{80,16},{96,32},{112,48},{1... | collective-permute-start | bytes 221192 | tf_op jit(solution)/shard_map/ppermute | solution.py:82
  325.6 4.8 %collective-permute-start.16 = (f32[2,1,1,24,192]{4,3,2,1,0:T(8,128)S(1)}, f32[2,1,1,24,192]{4,3,2,1,0:T(8,128)S(1)}, u32[]{:S(2)}, u32[]{:S(2)}) collective-permute-start(f32[2,1,1,24,192]{4,3,2,1,0:T(8,128)S(1)} %dynamic-slice_bitcast_fusion.3), channel_id=1, source_target_pairs={{0,128},{128,0},{256,384},{384,256},{1,129},{129,1},{257,385},{385... | collective-permute-start | bytes 110600 | tf_op jit(solution)/shard_map/ppermute | solution.py:82
  330.4 7.5 %copy-start.1 = (s32[128]{0:T(128)S(1)}, s32[128]{0:T(128)}, u32[]{:S(2)}) copy-start(s32[128]{0:T(128)} %param.17) | copy-start | bytes 1540
  330.4 6.9 %collective-permute-start.17 = (f32[1,1,1,24,192]{4,3,2,1,0:T(8,128)S(1)}, f32[1,1,1,24,192]{4,3,2,1,0:T(8,128)S(1)}, u32[]{:S(2)}, u32[]{:S(2)}) collective-permute-start(f32[1,1,1,24,192]{4,3,2,1,0:T(8,128)S(1)} %constant_dynamic-slice_fusion), channel_id=1, source_target_pairs={{0,256},{128,384},{256,0},{384,128},{1,257},{129,385},{257,1},{385... | collective-permute-start | bytes 55304 | tf_op jit(solution)/shard_map/ppermute | solution.py:82
Sparse Core Ops, SparseCore 0:
  11.8 88.8 all-gather.3
  102.8 62.8 all-gather.7
  209.4 47.4 all-gather.5

commit v8 on v7

--- a/solution.py
+++ b/solution.py
@@ -66,10 +66,15 @@
     cols = value.shape[1:]
     cur = value.reshape(tuple(sizes[a] for a in DP_AXES) + (-1,) + cols)
     rows = None if extra is None else extra.shape[0]
-    for dim, name in reversed(list(enumerate(DP_AXES))):
+    steps = []
+    for bit in range(max(n.bit_length() for n in sizes.values())):
+        for dim, name in reversed(list(enumerate(DP_AXES))):
+            if bit < sizes[name].bit_length() - 1:
+                steps.append((dim, name, bit))
+    for dim, name, bit in steps:
         length = sizes[name]
         me = lax.axis_index(name)
-        for bit in range(length.bit_length() - 1):
+        if True:
             shape = cur.shape
             span = shape[dim]
             split = shape[:dim] + (span // 2, 2) + shape[dim + 1 :]

time: 347 us -> 331 us (0.954)
  waiting for transfers between devices: 109 us -> 87.8 us
  starting transfers between devices: 91 us -> 96.2 us
    ppermute x6, waiting for transfers between devices: 24.9 us -> 11.7 us  [halving_scatter(): merged = keep + lax.ppermute(send, name, perm)]
    ppermute x6, waiting for transfers between devices: 46.9 us -> 38.4 us  [halving_scatter(): got = lax.ppermute(message, name, perm)]
    ppermute x6, starting transfers between devices: 17.5 us -> 21.2 us  [halving_scatter(): merged = keep + lax.ppermute(send, name, perm)]
    unnamed x40 -> x34, local copies, waits for them, and re-layouts: 8.46 us -> 8.25 us
  transfers between devices with their start and end apart: 24 -> 24, of which waited for: 12 -> 13; matrix products, arithmetic and copies ran while one was open for 13% -> 15% of each run, Pallas kernels for 0% -> 0%
where the time goes in v8:
time: 331 us; the launch traced here: 328 us
  starting transfers between devices  96.2 us (29%)
  waiting for transfers between devices  87.8 us (27%)
  blocking collectives  56.2 us (17%)
  other arithmetic  32.6 us (10%)
  local copies, waits for them, and re-layouts  22.5 us (7%)
  matrix products  18.5 us (6%)
  between operations  14.6 us (4%)
    psum x6, blocking collectives, dp_sum(): value = lax.psum(value, name)  56.2 us
    ppermute x6, waiting for transfers between devices, halving_scatter(): got = lax.ppermute(message, name, perm)  38.4 us
    ppermute x6, waiting for transfers between devices, doubling_gather(): got = lax.ppermute(cur, name, perm)  35.2 us
    ppermute x6, starting transfers between devices, doubling_gather(): got = lax.ppermute(cur, name, perm)  24.5 us
    ppermute x6, starting transfers between devices, halving_scatter(): got = lax.ppermute(message, name, perm)  22.6 us
    ppermute x6, starting transfers between devices, halving_scatter(): merged = keep + lax.ppermute(send, name, perm)  21.2 us
    ppermute x6, waiting for transfers between devices, halving_scatter(): merged = keep + lax.ppermute(send, name, perm)  11.7 us
    all_to_all x1, starting transfers between devices, on_device(): lax.all_to_all(meta_send, DP_AXES, split_axis=0, concat_axis=0, tiled=True)  11.1 us
  transfers between devices with their start and end apart: 24, of which 13 were waited for; matrix products, arithmetic and copies ran while one was open for 15% of the time, Pallas kernels for 0%

profile of v8, /device:TPU:1, one launch (start us, length us, event | category | flops | bytes accessed | tf_op | source)
XLA Modules:
  0.0 328.5 jit_solution(14066429094704885782)
XLA Ops:
  10.4 4.8 %collective-permute-start = (bf16[1,448,192]{1,2,0:T(8,128)(2,1)S(1)}, bf16[1,448,192]{1,2,0:T(8,128)(2,1)S(1)}, u32[]{:S(2)}, u32[]{:S(2)}) collective-permute-start(bf16[1,448,192]{1,2,0:T(8,128)(2,1)S(1)} %maximum_bitcast_fusion), channel_id=1, source_target_pairs={{0,1},{1,0},{2,3},{3,2},{4,5},{5,4},{6,7},{7,6},{8,9},{9,8},{10,11... | collective-permute-start | bytes 516104 | tf_op jit(solution)/shard_map/ppermute | solution.py:104
  19.5 11.1 %all-to-all-start.1 = ((s32[64,1,2]{2,1,0:T(1,128)}), s32[64,1,2]{2,1,0:T(1,128)S(1)}, u32[]{:S(2)}, u32[]{:S(2)}) async-start(s32[64,1,2]{2,1,0:T(1,128)} %copy.65), calls=%async_computation.1 | async-start | bytes 65536 | tf_op jit(solution)/shard_map/all_to_all | solution.py:137
  30.6 1.9 collective-permute-start.3
  32.6 2.1 copy.64
  36.7 5.8 %collective-permute-start.1 = (bf16[2,448,192]{1,2,0:T(8,128)(2,1)S(1)}, bf16[2,448,192]{1,2,0:T(8,128)(2,1)S(1)}, u32[]{:S(2)}, u32[]{:S(2)}) collective-permute-start(bf16[2,448,192]{1,2,0:T(8,128)(2,1)S(1)} %maximum_select_fusion.2), channel_id=1, source_target_pairs={{0,2},{1,3},{2,0},{3,1},{4,6},{5,7},{6,4},{7,5},{8,10},{9,11},{10,... | collective-permute-start | bytes 1032200 | tf_op jit(solution)/shard_map/ppermute | solution.py:104
  43.1 1.9 collective-permute-start.4
  45.1 10.6 %all-to-all-start = ((bf16[64,16,320]{2,1,0:T(8,128)(2,1)}), bf16[64,16,320]{2,1,0:T(8,128)(2,1)S(1)}, u32[]{:S(2)}, u32[]{:S(2)}) async-start(bf16[64,16,320]{2,1,0:T(8,128)(2,1)} %broadcast_select_fusion), calls=%async_computation | async-start | bytes 1572864 | tf_op jit(solution)/shard_map/all_to_all | solution.py:136
  55.8 4.2 %collective-permute-done.1 = bf16[2,448,192]{1,2,0:T(8,128)(2,1)S(1)} collective-permute-done((bf16[2,448,192]{1,2,0:T(8,128)(2,1)S(1)}, bf16[2,448,192]{1,2,0:T(8,128)(2,1)S(1)}, u32[]{:S(2)}, u32[]{:S(2)}) %collective-permute-start.1) | collective-permute-done | bytes 344096 | tf_op jit(solution)/shard_map/ppermute | solution.py:104
  60.1 8.1 %collective-permute-start.2 = (bf16[4,448,192]{1,2,0:T(8,128)(2,1)S(1)}, bf16[4,448,192]{1,2,0:T(8,128)(2,1)S(1)}, u32[]{:S(2)}, u32[]{:S(2)}) collective-permute-start(bf16[4,448,192]{1,2,0:T(8,128)(2,1)S(1)} %maximum_select_fusion.1), channel_id=1, source_target_pairs={{0,4},{1,5},{2,6},{3,7},{4,0},{5,1},{6,2},{7,3},{8,12},{9,13},{10,... | collective-permute-start | bytes 2064392 | tf_op jit(solution)/shard_map/ppermute | solution.py:104
  68.3 1.9 collective-permute-start.5
  71.0 31.0 %collective-permute-done.5 = f32[4,192]{1,0:T(4,128)S(1)} collective-permute-done((f32[4,192]{1,0:T(4,128)S(1)}, f32[4,192]{1,0:T(4,128)S(1)}, u32[]{:S(2)}, u32[]{:S(2)}) %collective-permute-start.5) | collective-permute-done | bytes 3104 | tf_op jit(solution)/shard_map/ppermute | solution.py:104
  103.3 2.2 fusion.84
  105.6 2.6 copy-done.2
  108.2 2.6 multiply_convert_fusion
  114.9 6.0 %all-to-all-start.2 = ((bf16[8,192,192]{1,2,0:T(8,128)(2,1)}), bf16[8,192,192]{1,2,0:T(8,128)(2,1)}, u32[]{:S(2)}, u32[]{:S(2)}) async-start(bf16[8,192,192]{1,2,0:T(8,128)(2,1)} %copy.73), calls=%async_computation.2 | async-start | bytes 1572864 | tf_op jit(solution)/shard_map/all_to_all | solution.py:199
  121.1 3.7 %fusion.88 = f32[1024,384]{0,1:T(8,128)S(1)} fusion(bf16[1024,1536]{1,0:T(8,128)(2,1)} %multiply_convert_fusion, bf16[1536,384]{0,1:T(8,128)(2,1)} %bitcast.228), kind=kOutput, calls=%fused_computation.262 | convolution fusion | flops 1207959552 | bytes 5898240 | tf_op jit(solution)/shard_map/dot_general | solution.py:171
  125.4 6.0 %fusion.4 = (f32[192]{0:T(256)}, f32[192]{0:T(256)}, f32[64,16,192]{2,1,0:T(8,128)}) fusion(f32[64,16]{1,0:T(8,128)S(1)} %get-tuple-element.139, f32[192]{0:T(256)S(1)} %bitcast.257, f32[192]{0:T(256)S(1)} %bitcast.259, f32[192]{0:T(256)S(1)} %bitcast.263, f32[192]{0:T(256)S(1)} %bitcast.265, f32[192]{0:T(256)S(1)} %bitcast.267, f32[192]{0:T(256)S(1)} %bitcast.269, ...), kind=kLoop, calls=%fused_computation.75 | loop fusion | flops 12779136 | bytes 1602304 | tf_op jit(solution)/shard_map/reduce_sum | solution.py:180
  132.9 4.2 %all-reduce.8 = (f32[192]{0:T(256)S(1)}, f32[]{:T(128)}, f32[192]{0:T(256)S(1)}) all-reduce(f32[192]{0:T(256)} %get-tuple-element.70, f32[]{:T(128)} %fusion.78, f32[192]{0:T(256)} %get-tuple-element.69), channel_id=1, replica_groups=mesh['x'=4,'y'=8,'c'=2,'mp'=8] {'c'}, use_global_device_ids=true, to_apply=%region_3.5 | all-reduce | flops 385 | bytes 3080 | tf_op jit(solution)/shard_map/psum | solution.py:49
  137.1 15.5 %all-reduce.4 = (f32[192]{0:T(256)S(1)}, f32[]{:T(128)}, f32[192]{0:T(256)S(1)}) all-reduce(f32[192]{0:T(256)S(1)} %get-tuple-element.85, f32[]{:T(128)} %get-tuple-element.86, f32[192]{0:T(256)S(1)} %get-tuple-element.87), channel_id=1, replica_groups=mesh['x'=4,'y'=8,'c'=2,'mp'=8] {'y'}, use_global_device_ids=true, to_apply=%region_4.6 | all-reduce | flops 385 | bytes 3080 | tf_op jit(solution)/shard_map/psum | solution.py:49
  152.6 10.1 %all-reduce.6 = (f32[192]{0:T(256)S(1)}, f32[]{:T(128)}, f32[192]{0:T(256)S(1)}) all-reduce(f32[192]{0:T(256)S(1)} %get-tuple-element.75, f32[]{:T(128)} %get-tuple-element.76, f32[192]{0:T(256)S(1)} %get-tuple-element.77), channel_id=1, replica_groups=mesh['x'=4,'y'=8,'c'=2,'mp'=8] {'x'}, use_global_device_ids=true, to_apply=%region_5.7 | all-reduce | flops 385 | bytes 3080 | tf_op jit(solution)/shard_map/psum | solution.py:49
  163.4 2.4 all-gather.8.cloned.1.call-done
  165.7 4.1 %fusion.85 = (f32[192]{0:T(256)S(1)}, f32[192]{0:T(256)S(1)}, f32[1024,192]{0,1:T(8,128)}) fusion(f32[192]{0:T(256)S(1)} %get-tuple-element.90, f32[1024,192]{0,1:T(8,128)S(1)} %copy.70, f32[192]{0:T(256)S(1)} %get-tuple-element.91, f32[192]{0:T(256)} %param.25, f32[192]{0:T(256)} %param.24, f32[1024]{0:T(1024)S(1)} %reshape.387, ...), kind=kOutput, calls=%fused_computation.259 | convolution fusion | flops 607125120 | bytes 5317120 | tf_op jit(solution)/shard_map/dot_general | solution.py:200
  169.8 4.0 %all-reduce.7 = (f32[192]{0:T(256)}, f32[192]{0:T(256)}) all-reduce(f32[192]{0:T(256)S(1)} %get-tuple-element.72, f32[192]{0:T(256)S(1)} %get-tuple-element.71), channel_id=1, replica_groups=mesh['x'=4,'y'=8,'c'=2,'mp'=8] {'c'}, use_global_device_ids=true, to_apply=%region_19.21 | all-reduce | flops 384 | bytes 3072 | tf_op jit(solution)/shard_map/psum | solution.py:49
  173.9 13.7 %all-reduce.3 = (f32[192]{0:T(256)S(1)}, f32[192]{0:T(256)}) all-reduce(f32[192]{0:T(256)} %get-tuple-element.83, f32[192]{0:T(256)} %get-tuple-element.84), channel_id=1, replica_groups=mesh['x'=4,'y'=8,'c'=2,'mp'=8] {'y'}, use_global_device_ids=true, to_apply=%region_20.22 | all-reduce | flops 384 | bytes 3072 | tf_op jit(solution)/shard_map/psum | solution.py:49
  187.5 8.7 %all-reduce.5 = (f32[192]{0:T(256)}, f32[192]{0:T(256)S(1)}) all-reduce(f32[192]{0:T(256)S(1)} %get-tuple-element.73, f32[192]{0:T(256)} %get-tuple-element.74), channel_id=1, replica_groups=mesh['x'=4,'y'=8,'c'=2,'mp'=8] {'x'}, use_global_device_ids=true, to_apply=%region_21.23 | all-reduce | flops 384 | bytes 3072 | tf_op jit(solution)/shard_map/psum | solution.py:49
  197.0 3.6 %multiply_reduce_fusion.32 = (f32[192]{0:T(256)S(1)}, f32[1024,192]{0,1:T(8,128)}, bf16[1024,192]{0,1:T(8,128)(2,1)}) fusion(f32[]{:T(128)} %get-tuple-element.81, f32[192]{0:T(256)} %get-tuple-element.78, f32[1024,192]{0,1:T(8,128)S(1)} %copy.70, f32[192]{0:T(256)S(1)} %get-tuple-element.91, f32[1024,192]{0,1:T(8,128)} %get-tuple-element.142, ...), kind=kLoop, calls=%fused_computation.181 | loop fusion | flops 4718400 | bytes 4334852 | tf_op jit(solution)/shard_map/reduce_sum | solution.py:40
  202.1 3.4 %fusion.56 = f32[64,16,192]{2,1,0:T(8,128)S(1)} fusion(f32[64,16,192]{2,1,0:T(8,128)S(1)} %bitcast.202, f32[192]{0:T(256)S(1)} %bitcast.258, f32[192]{0:T(256)S(1)} %bitcast.260, f32[192]{0:T(256)S(1)} %bitcast.264, f32[192]{0:T(256)S(1)} %bitcast.266, f32[192]{0:T(256)S(1)} %bitcast.268, f32[192]{0:T(256)S(1)} %bitcast.270, f32[192]{0:T(256)S(1)} %bitcast.272, ...), kind=kLoop, calls=%fused_computation.127 | loop fusion | flops 11993088 | bytes 1596672 | tf_op jit(solution)/shard_map/add | solution.py:28
  208.4 3.0 multiply_reduce_fusion.2
  211.6 2.1 multiply_convert_fusion.2
  217.1 8.0 %collective-permute-start.6 = (f32[784,384]{1,0:T(8,128)}, f32[784,384]{1,0:T(8,128)S(1)}, u32[]{:S(2)}, u32[]{:S(2)}) collective-permute-start(f32[784,384]{1,0:T(8,128)} %pad_maximum_fusion), channel_id=1, source_target_pairs={{0,8},{8,0},{1,9},{9,1},{2,10},{10,2},{3,11},{11,3},{4,12},{12,4},... | collective-permute-start | bytes 3612680 | tf_op jit(solution)/shard_map/ppermute | solution.py:90
  225.1 2.7 collective-permute-done.6
  228.2 1.9 collective-permute-start.7
  230.2 15.1 %collective-permute-done.7 = f32[400,384]{1,0:T(8,128)S(1)} collective-permute-done((f32[400,384]{1,0:T(8,128)S(1)}, f32[400,384]{1,0:T(8,128)S(1)}, u32[]{:S(2)}, u32[]{:S(2)}) %collective-permute-start.7) | collective-permute-done | bytes 614432 | tf_op jit(solution)/shard_map/ppermute | solution.py:90
  245.5 1.9 collective-permute-start.8
  247.4 7.9 %collective-permute-done.8 = f32[208,384]{1,0:T(8,128)S(1)} collective-permute-done((f32[208,384]{1,0:T(8,128)S(1)}, f32[208,384]{1,0:T(8,128)S(1)}, u32[]{:S(2)}, u32[]{:S(2)}) %collective-permute-start.8) | collective-permute-done | bytes 319520 | tf_op jit(solution)/shard_map/ppermute | solution.py:90
  255.5 3.0 collective-permute-start.9
  258.5 9.2 %collective-permute-done.9 = f32[112,384]{1,0:T(8,128)S(1)} collective-permute-done((f32[112,384]{1,0:T(8,128)S(1)}, f32[112,384]{1,0:T(8,128)S(1)}, u32[]{:S(2)}, u32[]{:S(2)}) %collective-permute-start.9) | collective-permute-done | bytes 172064 | tf_op jit(solution)/shard_map/ppermute | solution.py:90
  267.7 2.9 fusion.89
  270.7 2.9 collective-permute-start.12
  273.6 2.7 collective-permute-start.10
  278.5 3.0 collective-permute-done.10
  281.5 7.3 %collective-permute-done.13 = f32[4,4,1,24,192]{4,3,1,0,2:T(8,128)S(1)} collective-permute-done((f32[4,4,1,24,192]{4,3,1,0,2:T(8,128)S(1)}, f32[4,4,1,24,192]{4,3,1,0,2:T(8,128)S(1)}, u32[]{:S(2)}, u32[]{:S(2)}) %collective-permute-start.13) | collective-permute-done | bytes 294944 | tf_op jit(solution)/shard_map/ppermute | solution.py:87
  290.9 5.0 %collective-permute-start.11 = (f32[40,384]{1,0:T(8,128)S(1)}, f32[40,384]{1,0:T(8,128)S(1)}, u32[]{:S(2)}, u32[]{:S(2)}) collective-permute-start(f32[40,384]{1,0:T(8,128)S(1)} %pad_maximum_fusion.5), channel_id=1, source_target_pairs={{0,64},{16,80},{32,96},{48,112},{64,0},{80,16},{96,32},{112,48},{1... | collective-permute-start | bytes 184328 | tf_op jit(solution)/shard_map/ppermute | solution.py:90
  296.1 3.2 collective-permute-start.15
  299.8 4.0 %collective-permute-done.15 = f32[2,2,1,24,192]{4,3,2,1,0:T(8,128)S(1)} collective-permute-done((f32[2,2,1,24,192]{4,3,2,1,0:T(8,128)S(1)}, f32[2,2,1,24,192]{4,3,2,1,0:T(8,128)S(1)}, u32[]{:S(2)}, u32[]{:S(2)}) %collective-permute-start.15) | collective-permute-done | bytes 73760 | tf_op jit(solution)/shard_map/ppermute | solution.py:87
  303.8 7.5 %collective-permute-start.16 = (f32[1,2,1,24,192]{4,3,2,1,0:T(8,128)S(1)}, f32[1,2,1,24,192]{4,3,2,1,0:T(8,128)S(1)}, u32[]{:S(2)}, u32[]{:S(2)}) collective-permute-start(f32[1,2,1,24,192]{4,3,2,1,0:T(8,128)S(1)} %constant_dynamic-slice_fusion.1), channel_id=1, source_target_pairs={{0,256},{128,384},{256,0},{384,128},{1,257},{129,385},{257,1},{385... | collective-permute-start | bytes 110600 | tf_op jit(solution)/shard_map/ppermute | solution.py:87
  312.8 3.8 %collective-permute-start.17 = (f32[1,1,1,24,192]{4,3,2,1,0:T(8,128)S(1)}, f32[1,1,1,24,192]{4,3,2,1,0:T(8,128)S(1)}, u32[]{:S(2)}, u32[]{:S(2)}) collective-permute-start(f32[1,1,1,24,192]{4,3,2,1,0:T(8,128)S(1)} %constant_dynamic-slice_fusion), channel_id=1, source_target_pairs={{0,64},{16,80},{32,96},{48,112},{64,0},{80,16},{96,32},{112,48},{1... | collective-permute-start | bytes 55304 | tf_op jit(solution)/shard_map/ppermute | solution.py:87
  316.7 3.5 %add_convert_fusion = bf16[1024,192]{1,0:T(8,128)(2,1)S(1)} fusion(f32[1024,1536]{1,0:T(8,128)} %copy-done.2, s32[]{:T(128)S(6)} %select_n.153, bf16[1024,1536]{0,1:T(8,128)(2,1)} %all-gather.6.cloned.1.call-done, bf16[1536,3,192]{2,0,1:T(8,128)(2,1)S(1)} %copy-done.4), kind=kOutput, calls=%fused_computation.166 | convolution fusion | flops 604372992 | bytes 5111812 | tf_op jit(solution)/shard_map/dot_general | solution.py:194
  (148 shorter events, 37.0 us)
Async XLA Ops:
  7.2 8.7 %copy-start = (s32[128]{0:T(128)S(1)}, s32[128]{0:T(128)}, u32[]{:S(2)}) copy-start(s32[128]{0:T(128)} %param.17) | copy-start | bytes 1540
  7.2 27.6 %copy-start.14 = (s32[1,64]{1,0:T(1,128)S(1)}, s32[1,64]{1,0:T(1,128)}, u32[]{:S(2)}) copy-start(s32[1,64]{1,0:T(1,128)} %param.16) | copy-start | bytes 772
  7.2 103.6 %all-gather.4.cloned.1.call-start = ((), (), s32[]{:S(2)}) async-start(), calls=%async_computation.3 | async-start | bytes 2396160 | tf_op jit(solution)/shard_map/all_gather | solution.py:139
  10.4 26.2 %collective-permute-start = (bf16[1,448,192]{1,2,0:T(8,128)(2,1)S(1)}, bf16[1,448,192]{1,2,0:T(8,128)(2,1)S(1)}, u32[]{:S(2)}, u32[]{:S(2)}) collective-permute-start(bf16[1,448,192]{1,2,0:T(8,128)(2,1)S(1)} %maximum_bitcast_fusion), channel_id=1, source_target_pairs={{0,1},{1,0},{2,3},{3,2},{4,5},{5,4},{6,7},{7,6},{8,9},{9,8},{10,11... | collective-permute-start | bytes 516104 | tf_op jit(solution)/shard_map/ppermute | solution.py:104
  19.5 25.6 %all-to-all-start.1 = ((s32[64,1,2]{2,1,0:T(1,128)}), s32[64,1,2]{2,1,0:T(1,128)S(1)}, u32[]{:S(2)}, u32[]{:S(2)}) async-start(s32[64,1,2]{2,1,0:T(1,128)} %copy.65), calls=%async_computation.1 | async-start | bytes 65536 | tf_op jit(solution)/shard_map/all_to_all | solution.py:137
  30.6 135.2 %all-gather.8.cloned.1.call-start = ((), (), s32[]{:S(2)}) async-start(), calls=%async_computation.5 | async-start | bytes 3538944 | tf_op jit(solution)/shard_map/all_gather | solution.py:198
  30.6 12.5 %collective-permute-start.3 = (f32[1,192]{1,0:T(1,128)}, f32[1,192]{1,0:T(1,128)S(1)}, u32[]{:S(2)}, u32[]{:S(2)}) collective-permute-start(f32[1,192]{1,0:T(1,128)} %bitcast.331), channel_id=1, source_target_pairs={{0,1},{1,0},{2,3},{3,2},{4,5},{5,4},{6,7},{7,6},{8,9},{9,8},{10,11... | collective-permute-start | bytes 2312 | tf_op jit(solution)/shard_map/ppermute | solution.py:104
  32.6 9.9 %copy-start.7 = (f32[31,192]{1,0:T(8,128)S(1)}, f32[31,192]{1,0:T(8,128)}, u32[]{:S(2)}) copy-start(f32[31,192]{1,0:T(8,128)} %param.23) | copy-start | bytes 71428
  32.6 10.5 %copy-start.13 = (f32[192]{0:T(256)S(1)}, f32[192]{0:T(256)}, u32[]{:S(2)}) copy-start(f32[192]{0:T(256)} %param.21) | copy-start | bytes 2308
  36.7 23.3 %collective-permute-start.1 = (bf16[2,448,192]{1,2,0:T(8,128)(2,1)S(1)}, bf16[2,448,192]{1,2,0:T(8,128)(2,1)S(1)}, u32[]{:S(2)}, u32[]{:S(2)}) collective-permute-start(bf16[2,448,192]{1,2,0:T(8,128)(2,1)S(1)} %maximum_select_fusion.2), channel_id=1, source_target_pairs={{0,2},{1,3},{2,0},{3,1},{4,6},{5,7},{6,4},{7,5},{8,10},{9,11},{10,... | collective-permute-start | bytes 1032200 | tf_op jit(solution)/shard_map/ppermute | solution.py:104
  43.1 25.2 %collective-permute-start.4 = (f32[2,192]{1,0:T(2,128)S(1)}, f32[2,192]{1,0:T(2,128)S(1)}, u32[]{:S(2)}, u32[]{:S(2)}) collective-permute-start(f32[2,192]{1,0:T(2,128)S(1)} %maximum_select_fusion.5), channel_id=1, source_target_pairs={{0,2},{1,3},{2,0},{3,1},{4,6},{5,7},{6,4},{7,5},{8,10},{9,11},{10,... | collective-permute-start | bytes 4616 | tf_op jit(solution)/shard_map/ppermute | solution.py:104
  45.1 58.0 %all-to-all-start = ((bf16[64,16,320]{2,1,0:T(8,128)(2,1)}), bf16[64,16,320]{2,1,0:T(8,128)(2,1)S(1)}, u32[]{:S(2)}, u32[]{:S(2)}) async-start(bf16[64,16,320]{2,1,0:T(8,128)(2,1)} %broadcast_select_fusion), calls=%async_computation | async-start | bytes 1572864 | tf_op jit(solution)/shard_map/all_to_all | solution.py:136
  60.1 42.0 %collective-permute-start.2 = (bf16[4,448,192]{1,2,0:T(8,128)(2,1)S(1)}, bf16[4,448,192]{1,2,0:T(8,128)(2,1)S(1)}, u32[]{:S(2)}, u32[]{:S(2)}) collective-permute-start(bf16[4,448,192]{1,2,0:T(8,128)(2,1)S(1)} %maximum_select_fusion.1), channel_id=1, source_target_pairs={{0,4},{1,5},{2,6},{3,7},{4,0},{5,1},{6,2},{7,3},{8,12},{9,13},{10,... | collective-permute-start | bytes 2064392 | tf_op jit(solution)/shard_map/ppermute | solution.py:104
  68.3 33.7 %collective-permute-start.5 = (f32[4,192]{1,0:T(4,128)S(1)}, f32[4,192]{1,0:T(4,128)S(1)}, u32[]{:S(2)}, u32[]{:S(2)}) collective-permute-start(f32[4,192]{1,0:T(4,128)S(1)} %maximum_select_fusion.4), channel_id=1, source_target_pairs={{0,4},{1,5},{2,6},{3,7},{4,0},{5,1},{6,2},{7,3},{8,12},{9,13},{10,... | collective-permute-start | bytes 9224 | tf_op jit(solution)/shard_map/ppermute | solution.py:104
  105.5 2.7 copy-start.2
  110.8 1.4 slice-start
  110.8 2.9 slice-start.1
  114.9 48.5 %all-to-all-start.2 = ((bf16[8,192,192]{1,2,0:T(8,128)(2,1)}), bf16[8,192,192]{1,2,0:T(8,128)(2,1)}, u32[]{:S(2)}, u32[]{:S(2)}) async-start(bf16[8,192,192]{1,2,0:T(8,128)(2,1)} %copy.73), calls=%async_computation.2 | async-start | bytes 1572864 | tf_op jit(solution)/shard_map/all_to_all | solution.py:199
  120.9 146.8 %all-gather.6.cloned.1.call-start = ((), (), s32[]{:S(2)}) async-start(), calls=%async_computation.4 | async-start | bytes 3538944 | tf_op jit(solution)/shard_map/all_gather | solution.py:192
  124.8 75.7 %copy-start.3 = (f32[1024,384]{0,1:T(8,128)}, f32[1024,384]{0,1:T(8,128)S(1)}, u32[]{:S(2)}) copy-start(f32[1024,384]{0,1:T(8,128)S(1)} %fusion.88) | copy-start | bytes 4718596
  169.8 32.2 %copy-start.8 = (f32[1,192]{1,0:T(1,128)S(1)}, f32[1,192]{1,0:T(1,128)}, u32[]{:S(2)}) copy-start(f32[1,192]{1,0:T(1,128)} %get-tuple-element.119) | copy-start | bytes 2308
  169.8 32.2 %copy-start.9 = (f32[1,192]{1,0:T(1,128)S(1)}, f32[1,192]{1,0:T(1,128)}, u32[]{:S(2)}) copy-start(f32[1,192]{1,0:T(1,128)} %get-tuple-element.120) | copy-start | bytes 2308
  169.8 32.2 %copy-start.10 = (f32[1,192]{1,0:T(1,128)S(1)}, f32[1,192]{1,0:T(1,128)}, u32[]{:S(2)}) copy-start(f32[1,192]{1,0:T(1,128)} %get-tuple-element.121) | copy-start | bytes 2308
  169.8 32.2 %copy-start.11 = (f32[1,192]{1,0:T(1,128)S(1)}, f32[1,192]{1,0:T(1,128)}, u32[]{:S(2)}) copy-start(f32[1,192]{1,0:T(1,128)} %get-tuple-element.122) | copy-start | bytes 2308
  196.3 0.7 copy-start.12
  211.3 2.6 copy-start.5
  217.1 10.7 %collective-permute-start.6 = (f32[784,384]{1,0:T(8,128)}, f32[784,384]{1,0:T(8,128)S(1)}, u32[]{:S(2)}, u32[]{:S(2)}) collective-permute-start(f32[784,384]{1,0:T(8,128)} %pad_maximum_fusion), channel_id=1, source_target_pairs={{0,8},{8,0},{1,9},{9,1},{2,10},{10,2},{3,11},{11,3},{4,12},{12,4},... | collective-permute-start | bytes 3612680 | tf_op jit(solution)/shard_map/ppermute | solution.py:90
  228.2 17.0 %collective-permute-start.7 = (f32[400,384]{1,0:T(8,128)S(1)}, f32[400,384]{1,0:T(8,128)S(1)}, u32[]{:S(2)}, u32[]{:S(2)}) collective-permute-start(f32[400,384]{1,0:T(8,128)S(1)} %pad_maximum_fusion.1), channel_id=1, source_target_pairs={{0,16},{16,0},{32,48},{48,32},{64,80},{80,64},{96,112},{112,96},{1... | collective-permute-start | bytes 1843208 | tf_op jit(solution)/shard_map/ppermute | solution.py:90
  245.3 22.4 %copy-start.6 = (bf16[1024,192]{0,1:T(8,128)(2,1)S(1)}, bf16[1024,192]{0,1:T(8,128)(2,1)}, u32[]{:S(2)}) copy-start(bf16[1024,192]{0,1:T(8,128)(2,1)} %param.27) | copy-start | bytes 1179652
  245.5 9.9 %collective-permute-start.8 = (f32[208,384]{1,0:T(8,128)S(1)}, f32[208,384]{1,0:T(8,128)S(1)}, u32[]{:S(2)}, u32[]{:S(2)}) collective-permute-start(f32[208,384]{1,0:T(8,128)S(1)} %pad_maximum_fusion.2), channel_id=1, source_target_pairs={{0,128},{128,0},{256,384},{384,256},{1,129},{129,1},{257,385},{385... | collective-permute-start | bytes 958472 | tf_op jit(solution)/shard_map/ppermute | solution.py:90
  255.5 12.2 %collective-permute-start.9 = (f32[112,384]{1,0:T(8,128)S(1)}, f32[112,384]{1,0:T(8,128)S(1)}, u32[]{:S(2)}, u32[]{:S(2)}) collective-permute-start(f32[112,384]{1,0:T(8,128)S(1)} %pad_maximum_fusion.3), channel_id=1, source_target_pairs={{0,32},{16,48},{32,0},{48,16},{64,96},{80,112},{96,64},{112,80},{1... | collective-permute-start | bytes 516104 | tf_op jit(solution)/shard_map/ppermute | solution.py:90
  270.7 5.7 %collective-permute-start.12 = (f32[4,8,1,24,192]{4,3,1,0,2:T(8,128)S(1)}, f32[4,8,1,24,192]{4,3,1,0,2:T(8,128)S(1)}, u32[]{:S(2)}, u32[]{:S(2)}) collective-permute-start(f32[4,8,1,24,192]{4,3,1,0,2:T(8,128)S(1)} %dynamic-slice_bitcast_fusion), channel_id=1, source_target_pairs={{0,8},{8,0},{1,9},{9,1},{2,10},{10,2},{3,11},{11,3},{4,12},{12,4},... | collective-permute-start | bytes 1769480 | tf_op jit(solution)/shard_map/ppermute | solution.py:87
  273.6 43.0 %copy-start.4 = (bf16[1536,3,192]{2,0,1:T(8,128)(2,1)S(1)}, bf16[1536,3,192]{2,0,1:T(8,128)(2,1)}, u32[]{:S(2)}) copy-start(bf16[1536,3,192]{2,0,1:T(8,128)(2,1)} %all-gather.4.cloned.1.call-done) | copy-start | bytes 5308420
  273.6 7.9 %collective-permute-start.10 = (f32[64,384]{1,0:T(8,128)S(1)}, f32[64,384]{1,0:T(8,128)S(1)}, u32[]{:S(2)}, u32[]{:S(2)}) collective-permute-start(f32[64,384]{1,0:T(8,128)S(1)} %pad_maximum_fusion.4), channel_id=1, source_target_pairs={{0,256},{128,384},{256,0},{384,128},{1,257},{129,385},{257,1},{385... | collective-permute-start | bytes 294920 | tf_op jit(solution)/shard_map/ppermute | solution.py:90
  276.5 12.3 %collective-permute-start.13 = (f32[4,4,1,24,192]{4,3,1,0,2:T(8,128)S(1)}, f32[4,4,1,24,192]{4,3,1,0,2:T(8,128)S(1)}, u32[]{:S(2)}, u32[]{:S(2)}) collective-permute-start(f32[4,4,1,24,192]{4,3,1,0,2:T(8,128)S(1)} %dynamic-slice_bitcast_fusion.1), channel_id=1, source_target_pairs={{0,16},{16,0},{32,48},{48,32},{64,80},{80,64},{96,112},{112,96},{1... | collective-permute-start | bytes 884744 | tf_op jit(solution)/shard_map/ppermute | solution.py:87
  288.9 7.2 %collective-permute-start.14 = (f32[2,4,1,24,192]{4,3,1,0,2:T(8,128)S(1)}, f32[2,4,1,24,192]{4,3,1,0,2:T(8,128)S(1)}, u32[]{:S(2)}, u32[]{:S(2)}) collective-permute-start(f32[2,4,1,24,192]{4,3,1,0,2:T(8,128)S(1)} %dynamic-slice_bitcast_fusion.2), channel_id=1, source_target_pairs={{0,128},{128,0},{256,384},{384,256},{1,129},{129,1},{257,385},{385... | collective-permute-start | bytes 442376 | tf_op jit(solution)/shard_map/ppermute | solution.py:87
  290.9 8.9 %collective-permute-start.11 = (f32[40,384]{1,0:T(8,128)S(1)}, f32[40,384]{1,0:T(8,128)S(1)}, u32[]{:S(2)}, u32[]{:S(2)}) collective-permute-start(f32[40,384]{1,0:T(8,128)S(1)} %pad_maximum_fusion.5), channel_id=1, source_target_pairs={{0,64},{16,80},{32,96},{48,112},{64,0},{80,16},{96,32},{112,48},{1... | collective-permute-start | bytes 184328 | tf_op jit(solution)/shard_map/ppermute | solution.py:90
  296.1 7.6 %collective-permute-start.15 = (f32[2,2,1,24,192]{4,3,2,1,0:T(8,128)S(1)}, f32[2,2,1,24,192]{4,3,2,1,0:T(8,128)S(1)}, u32[]{:S(2)}, u32[]{:S(2)}) collective-permute-start(f32[2,2,1,24,192]{4,3,2,1,0:T(8,128)S(1)} %dynamic-slice_bitcast_fusion.3), channel_id=1, source_target_pairs={{0,32},{16,48},{32,0},{48,16},{64,96},{80,112},{96,64},{112,80},{1... | collective-permute-start | bytes 221192 | tf_op jit(solution)/shard_map/ppermute | solution.py:87
  303.8 8.9 %collective-permute-start.16 = (f32[1,2,1,24,192]{4,3,2,1,0:T(8,128)S(1)}, f32[1,2,1,24,192]{4,3,2,1,0:T(8,128)S(1)}, u32[]{:S(2)}, u32[]{:S(2)}) collective-permute-start(f32[1,2,1,24,192]{4,3,2,1,0:T(8,128)S(1)} %constant_dynamic-slice_fusion.1), channel_id=1, source_target_pairs={{0,256},{128,384},{256,0},{384,128},{1,257},{129,385},{257,1},{385... | collective-permute-start | bytes 110600 | tf_op jit(solution)/shard_map/ppermute | solution.py:87
  312.8 9.2 %copy-start.1 = (s32[128]{0:T(128)S(1)}, s32[128]{0:T(128)}, u32[]{:S(2)}) copy-start(s32[128]{0:T(128)} %param.17) | copy-start | bytes 1540
  312.8 8.5 %collective-permute-start.17 = (f32[1,1,1,24,192]{4,3,2,1,0:T(8,128)S(1)}, f32[1,1,1,24,192]{4,3,2,1,0:T(8,128)S(1)}, u32[]{:S(2)}, u32[]{:S(2)}) collective-permute-start(f32[1,1,1,24,192]{4,3,2,1,0:T(8,128)S(1)} %constant_dynamic-slice_fusion), channel_id=1, source_target_pairs={{0,64},{16,80},{32,96},{48,112},{64,0},{80,16},{96,32},{112,48},{1... | collective-permute-start | bytes 55304 | tf_op jit(solution)/shard_map/ppermute | solution.py:87
Sparse Core Ops, SparseCore 0:
  11.8 88.8 all-gather.3
  102.8 62.8 all-gather.7
  205.6 47.7 all-gather.5
